TPU v7x, 32 devices: a whole 2x2x4 slice. The times are simulated.
32 devices in a mesh: src: 4 (over x, core), ep: 8 (over z, y).
Axes of the slice: x: 2, y: 2, z: 4, core: 2. Of those that a mesh axis runs over, the one named last changes fastest.
Arguments:
- log_conductivity: float32 [8, 16, 32, 128], P('ep'), may hold values from -3 to 3
- forward_field: float32 [8, 4, 16, 32, 128], P('ep', 'src'), may hold values from -6 to 6
- adjoint_field: float32 [8, 4, 16, 32, 128], P('ep', 'src'), may hold values from -6 to 6
- source_cells: int32 [4, 2], P('src'), may hold values from 0 to 65535
- receiver_cells: int32 [128], replicated, may hold values from 0 to 65535
- observed: float32 [8, 4, 128], P('ep', 'src'), may hold values from -6 to 6
- split_term: float32 [6, 65536], P(None, ('src', 'ep')), may hold values from -1.2 to 1.2
- dual_term: float32 [6, 65536], P(None, ('src', 'ep')), may hold values from -1.2 to 1.2
Outputs:
- model_out: float32 [8, 16, 32, 128], P('ep')
- split_out: float32 [6, 65536], P(None, ('src', 'ep'))
- dual_out: float32 [6, 65536], P(None, ('src', 'ep'))
Inputs may be any that keep to these rules, and one draw needn't show every extreme that they name: `source_cells`: source and receiver cells may repeat; a source's two electrodes may coincide.
All inputs are finite; a program needn't handle non-finite values.
Results may differ from a plain program's by a relative error of at most 0.0003.
Values sent between devices are 32-bit elements; how exact they have to be, the bound alone decides.
No kernel may reach another device: no remote copies, remote signals or barrier semaphores. Data moves between devices by JAX's collectives and lax.ppermute only.
A program may use at most 128 MiB of HBM per device.

v0:
```python
import jax
import jax.numpy as jnp
from jax import lax
from jax.sharding import PartitionSpec as P

SWEEPS = 4


MASS_TERM = 0.5
RELAXATION = 0.8
CURRENT = 4.0
DATA_WEIGHT = 8.0
STEP_SIZE = 0.5
PENALTY = 64.0
THRESHOLD = 0.1


def pad_side(values, dim_index, at_low):
    widths = [(0, 0)] * values.ndim
    widths[dim_index] = (0, 1) if at_low else (1, 0)
    return jnp.pad(values, widths)


def conductances(conductivity):
    face_weights = []
    diagonal = MASS_TERM * conductivity
    ndims = conductivity.ndim
    for dim_index in range(ndims - 3, ndims):
        length = conductivity.shape[dim_index]
        lower_cells = lax.slice_in_dim(conductivity, 0, length - 1, axis=dim_index)
        upper_cells = lax.slice_in_dim(conductivity, 1, length, axis=dim_index)
        face_weight = 0.5 * (lower_cells + upper_cells)
        face_weights.append(face_weight)
        diagonal = (
            diagonal
            + pad_side(face_weight, dim_index, True)
            + pad_side(face_weight, dim_index, False)
        )
    return (face_weights, diagonal)


def operate(iterate, conductivity, face_weights):
    result = MASS_TERM * conductivity * iterate
    ndims = iterate.ndim
    for position, dim_index in enumerate(range(ndims - 3, ndims)):
        length = iterate.shape[dim_index]
        face_flux = face_weights[position] * (
            lax.slice_in_dim(iterate, 1, length, axis=dim_index)
            - lax.slice_in_dim(iterate, 0, length - 1, axis=dim_index)
        )
        result = (
            result - pad_side(face_flux, dim_index, True) + pad_side(face_flux, dim_index, False)
        )
    return result


def relax(iterate, right_side, conductivity, face_weights, diagonal):
    for sweep_index in range(SWEEPS):
        iterate = (
            iterate
            + RELAXATION * (right_side - operate(iterate, conductivity, face_weights)) / diagonal
        )
    return iterate


def source_field(source_cells, cell_count):
    source_count = source_cells.shape[0]
    row_index = jnp.arange(source_count, dtype=jnp.int32)[:, None] * jnp.ones((1, 2), jnp.int32)
    polarity = jnp.broadcast_to(jnp.array([CURRENT, -CURRENT], jnp.float32), (source_count, 2))
    return (
        jnp.zeros((source_count, cell_count), jnp.float32).at[row_index, source_cells].add(polarity)
    )


def sweep_epoch(model_log, forward, adjoint, sources, receiver_cells, observed):
    grid_shape = forward.shape
    conductivity = jnp.exp(model_log)[None]
    face_weights, diagonal = conductances(conductivity)
    forward = relax(forward, sources.reshape(grid_shape), conductivity, face_weights, diagonal)
    flat_field = forward.reshape(grid_shape[0], -1)
    misfit = flat_field[:, receiver_cells] - observed
    adjoint_source = (
        jnp.zeros_like(flat_field)
        .at[:, receiver_cells]
        .add(DATA_WEIGHT * misfit)
        .reshape(grid_shape)
    )
    adjoint = relax(adjoint, adjoint_source, conductivity, face_weights, diagonal)
    gradient = conductivity[0] * jnp.sum(forward * adjoint, axis=0)
    return (forward, adjoint, gradient)


def temporal_factor(epochs):
    second = (
        jnp.eye(epochs - 2, epochs, dtype=jnp.float32)
        - 2.0 * jnp.eye(epochs - 2, epochs, k=1, dtype=jnp.float32)
        + jnp.eye(epochs - 2, epochs, k=2, dtype=jnp.float32)
    )
    matrix = jnp.eye(epochs, dtype=jnp.float32) + PENALTY * jnp.dot(
        second.T, second, precision=lax.Precision.HIGHEST
    )
    return jnp.linalg.cholesky(matrix)


def difference(values):
    return values[:-2] - 2.0 * values[1:-1] + values[2:]


def difference_adjoint(values):
    widths_low = [(0, 2), (0, 0)]
    widths_mid = [(1, 1), (0, 0)]
    widths_high = [(2, 0), (0, 0)]
    return (
        jnp.pad(values, widths_low)
        - 2.0 * jnp.pad(values, widths_mid)
        + jnp.pad(values, widths_high)
    )


def splitting_update(local_rhs, split_term, dual_term, factor):
    right_side = local_rhs + PENALTY * difference_adjoint(split_term - dual_term)
    updated = jax.scipy.linalg.cho_solve((factor, True), right_side)
    shifted = difference(updated) + dual_term
    split_term = shifted - jnp.clip(shifted, -THRESHOLD, THRESHOLD)
    dual_term = shifted - split_term
    return (updated, split_term, dual_term)


def on_device(
    log_conductivity,
    forward_field,
    adjoint_field,
    source_cells,
    receiver_cells,
    observed,
    split_term,
    dual_term,
):
    slab_epochs, size_x, size_y, size_z = log_conductivity.shape
    cell_count = size_x * size_y * size_z
    share_cells = cell_count // lax.axis_size("src")
    offset = lax.axis_index("src") * share_cells
    total_epochs = slab_epochs * lax.axis_size("ep")
    sources = source_field(source_cells, cell_count)
    factor = temporal_factor(total_epochs)
    sweeper = jax.vmap(sweep_epoch, in_axes=(0, 0, 0, None, None, 0))
    model_log = log_conductivity
    forward = forward_field
    adjoint = adjoint_field
    forward, adjoint, partial_terms = sweeper(
        model_log, forward, adjoint, sources, receiver_cells, observed
    )
    partial_terms = partial_terms.reshape(slab_epochs, cell_count)
    summed = lax.psum(partial_terms, "src")
    gradient_share = lax.dynamic_slice_in_dim(summed, offset, share_cells, 1)
    model_share = lax.dynamic_slice_in_dim(
        model_log.reshape(slab_epochs, cell_count), offset, share_cells, 1
    )
    local_rhs = model_share - STEP_SIZE * gradient_share
    time_rhs = lax.all_to_all(local_rhs, "ep", split_axis=1, concat_axis=0, tiled=True)
    updated, split_term, dual_term = splitting_update(time_rhs, split_term, dual_term, factor)
    slab_share = lax.all_to_all(updated, "ep", split_axis=0, concat_axis=1, tiled=True)
    model_log = lax.all_gather(slab_share, "src", axis=1, tiled=True).reshape(
        slab_epochs, size_x, size_y, size_z
    )
    return (model_log, split_term, dual_term)


def solution(mesh):
    return jax.shard_map(
        on_device,
        mesh=mesh,
        in_specs=(
            P("ep", None, None, None),
            P("ep", "src", None, None, None),
            P("ep", "src", None, None, None),
            P("src", None),
            P(),
            P("ep", "src", None),
            P(None, ("src", "ep")),
            P(None, ("src", "ep")),
        ),
        out_specs=(P("ep", None, None, None), P(None, ("src", "ep")), P(None, ("src", "ep"))),
        check_vma=False,
    )
```

profile of v0, /device:TPU:0, one launch (start us, length us, event | category | flops | bytes accessed | tf_op | source)
XLA Modules:
  0.0 93.7 jit_solution(12895999680581403792)
XLA Ops:
  7.2 0.0 copy-start.1
  7.2 0.0 all-reduce.60.cloned.1.call-start
  7.2 1.0 %exponential_bitcast_fusion = f32[1,1,16,32,128]{4,3,2,1,0:T(8,128)S(1)} fusion(f32[1,16,32,128]{3,2,1,0:T(8,128)} %param.9), kind=kLoop, calls=%fused_computation.45 | loop fusion | bytes 524288 | tf_op jit(solution)/shard_map/vmap()/broadcast_in_dim | solution.py:77
  8.2 0.0 copy-done.1
  8.3 0.2 subtract_multiply_fusion
  8.5 0.1 subtract_multiply_fusion.1
  8.6 0.0 copy-start.2
  8.6 0.1 subtract_multiply_fusion.4
  8.6 0.9 copy-done.2
  9.5 0.1 subtract_multiply_fusion.2
  9.7 0.0 copy-start.5
  9.7 0.7 subtract_multiply_fusion.5
  10.4 0.0 copy-done.5
  10.4 0.0 copy-start
  10.4 0.1 copy.36
  10.5 0.1 pad_bitcast_fusion
  10.6 0.2 fusion.52
  10.8 0.8 scatter_custom_fusion
  11.6 0.0 copy-done
  11.6 1.4 %divide_add_fusion.6 = (f32[1,1,16,32,128]{4,3,2,1,0:T(8,128)S(1)}, f32[1,1,16,32,128]{4,3,2,1,0:T(8,128)S(1)}) fusion(f32[1,1,16,32,128]{4,3,2,1,0:T(8,128)S(1)} %copy-done.2, f32[1,1,16,32,128]{4,3,2,1,0:T(8,128)S(1)} %bitcast.67, f32[1,1,16,32,127]{4,3,2,1,0:T(8,128)S(1)} %subtract_multiply_fusion.2, ...), kind=kLoop, calls=%fused_computation.41 | loop fusion | flops 1179648 | bytes 2830336 | tf_op jit(solution)/shard_map/vmap()/add | solution.py:60
  13.1 0.1 fusion.11
  13.2 0.1 fusion.10
  13.3 0.3 divide_add_fusion.5
  13.7 0.1 fusion.8
  13.8 0.3 divide_add_fusion.4
  14.2 0.0 copy-start.6
  14.2 0.1 fusion.6
  14.3 0.5 copy-done.6
  14.8 0.2 divide_add_fusion.3
  15.1 0.0 copy-start.7
  15.1 1.1 %gather_fusion = f32[128]{0:T(128)S(1)} fusion(f32[65536]{0:T(1024)S(1)} %bitcast.71, s32[1024]{0:T(1024)S(1)} %pad_clamp_fusion), kind=kCustom, calls=%fused_computation | custom fusion | bytes 1536 | tf_op jit(solution)/shard_map/vmap()/gather | solution.py:81
  16.3 0.0 copy-done.7
  16.3 1.3 %scatter_custom_fusion.1 = f32[65536]{0:T(1024)S(1)} fusion(s32[128]{0:T(128)S(1)} %compare_select_fusion, f32[128]{0:T(128)S(1)} %fusion.55, f32[]{:T(128)} %constant.82.clone.1), kind=kCustom, calls=%fused_computation.62 | custom fusion | flops 128 | bytes 262148 | tf_op jit(solution)/shard_map/vmap()/scatter-add | solution.py:85
  17.6 0.3 divide_add_fusion.2
  18.0 0.1 fusion.4
  18.1 0.3 divide_add_fusion.1
  18.5 0.1 fusion.2
  18.6 0.3 divide_add_fusion
  19.0 0.1 fusion
  19.1 1.0 %bitcast_multiply_fusion = f32[1,16,32,128]{3,2,1,0:T(8,128)} fusion(f32[1,1,16,32,128]{4,3,2,1,0:T(8,128)S(1)} %divide_add_fusion.3, f32[1,1,16,32,128]{4,3,2,1,0:T(8,128)S(1)} %divide_add_fusion, f32[1,1,16,32,128]{4,3,2,1,0:T(8,128)S(1)} %get-tuple-element.12, f32[1,1,16,32,128]{4,3,2,1,0:T(8,128)S(1)} %bitcast.66, f32[1,1,16,32,127]{4,3,2,1,0:T(8,128)S(1)} %fusion, ...), kind=kLoop, calls=%fused_computation.32 | loop fusion | flops 917504 | bytes 2332672 | tf_op jit(solution)/shard_map/vmap()/mul | solution.py:89
  20.1 0.0 all-reduce.60.cloned.1.call-update
  20.1 0.3 convert_add_fusion
  20.4 0.1 copy.27
  20.5 0.7 cholesky.17
  21.2 0.1 copy.28
  21.2 0.2 select_reduce_fusion
  21.4 0.6 compare_reduce_fusion
  22.0 32.9 %all-reduce.60.cloned.1.call-done = f32[1,65536]{1,0:T(1,128)} async-done(((f32[1,65536]{1,0:T(1,128)}), f32[1,65536]{1,0:T(1,128)}) %all-reduce.60.cloned.1.call-update) | async-done | bytes 262160 | tf_op jit(solution)/shard_map/psum | solution.py:154
  54.9 1.6 %multiply_subtract_fusion = f32[1,16384]{1,0:T(1,128)} fusion(f32[1,65536]{1,0:T(1,128)} %all-reduce.60.cloned.1.call-done, s32[]{:T(128)S(6)} %select_n.16, f32[1,65536]{1,0:T(1,128)S(1)} %bitcast.62), kind=kLoop, calls=%fused_computation.81 | loop fusion | flops 32768 | bytes 196612 | tf_op jit(solution)/shard_map/sub | solution.py:159
  56.5 5.6 %all-to-all-start = ((f32[1,8,2048]{2,0,1:T(1,128)}), f32[1,8,2048]{2,0,1:T(1,128)S(1)}, u32[]{:S(2)}, u32[]{:S(2)}) async-start(f32[1,8,2048]{2,0,1:T(1,128)} %bitcast.14), calls=%async_computation | async-start | bytes 131072 | tf_op jit(solution)/shard_map/all_to_all | solution.py:160
  62.1 0.6 select_select_fusion
  62.8 0.1 copy.30
  62.9 0.6 custom-call.10
  63.5 0.0 copy-done.3
  63.5 0.0 copy-done.4
  63.5 5.5 %all-to-all-done = f32[1,8,2048]{2,0,1:T(1,128)S(1)} async-done(((f32[1,8,2048]{2,0,1:T(1,128)}), f32[1,8,2048]{2,0,1:T(1,128)S(1)}, u32[]{:S(2)}, u32[]{:S(2)}) %all-to-all-start) | async-done | bytes 65568 | tf_op jit(solution)/shard_map/all_to_all | solution.py:160
  69.0 0.3 fusion.27
  69.3 0.2 fusion.39
  69.5 0.7 copy.33
  70.2 3.4 %all-to-all-start.1 = ((f32[8,1,2048]{2,1,0:T(1,128)}), f32[8,1,2048]{2,1,0:T(1,128)S(1)}, u32[]{:S(2)}, u32[]{:S(2)}) async-start(f32[8,1,2048]{2,1,0:T(1,128)} %copy.33), calls=%async_computation.1 | async-start | bytes 131072 | tf_op jit(solution)/shard_map/all_to_all | solution.py:162
  73.6 0.7 fusion.61
  74.2 6.2 %all-to-all-done.1 = f32[8,1,2048]{2,1,0:T(1,128)S(1)} async-done(((f32[8,1,2048]{2,1,0:T(1,128)}), f32[8,1,2048]{2,1,0:T(1,128)S(1)}, u32[]{:S(2)}, u32[]{:S(2)}) %all-to-all-start.1) | async-done | bytes 65568 | tf_op jit(solution)/shard_map/all_to_all | solution.py:162
  80.4 5.8 %all_gather.3 = f32[1,65536]{1,0:T(1,128)S(1)} all-gather(f32[1,16384]{1,0:T(1,128)S(1)} %bitcast.75), channel_id=1, replica_groups=mesh['src'=4,'ep'=8] {'src'}, dimensions={1}, use_global_device_ids=true | all-gather | bytes 327680 | tf_op jit(solution)/shard_map/all_gather | solution.py:163
  86.2 0.7 copy.43
  (21 shorter events, 0.5 us)
Async XLA Ops:
  7.2 1.1 %copy-start.1 = (f32[1,1,16,32,128]{4,3,2,1,0:T(8,128)S(1)}, f32[1,1,16,32,128]{4,3,2,1,0:T(8,128)}, u32[]{:S(2)}) copy-start(f32[1,1,16,32,128]{4,3,2,1,0:T(8,128)} %param.11) | copy-start | bytes 786436
  7.2 47.8 %all-reduce.60.cloned.1.call-start = ((), (), s32[]{:S(2)}) async-start(), calls=%async_computation.2 | async-start | bytes 524288 | tf_op jit(solution)/shard_map/psum | solution.py:154
  8.6 1.0 %copy-start.2 = (f32[1,1,16,32,128]{4,3,2,1,0:T(8,128)S(1)}, f32[1,1,16,32,128]{4,3,2,1,0:T(8,128)}, u32[]{:S(2)}) copy-start(f32[1,1,16,32,128]{4,3,2,1,0:T(8,128)} %param.10) | copy-start | bytes 786436
  9.7 0.7 copy-start.5
  10.4 1.2 %copy-start = (f32[1,16,32,128]{3,2,1,0:T(8,128)S(1)}, f32[1,16,32,128]{3,2,1,0:T(8,128)}, u32[]{:S(2)}) copy-start(f32[1,16,32,128]{3,2,1,0:T(8,128)} %param.9) | copy-start | bytes 786436
  14.2 0.7 copy-start.6
  15.1 1.2 %copy-start.7 = (f32[1,1,128]{2,1,0:T(1,128)S(1)}, f32[1,1,128]{2,1,0:T(1,128)}, u32[]{:S(2)}) copy-start(f32[1,1,128]{2,1,0:T(1,128)} %param.14) | copy-start | bytes 1540
  56.5 7.0 %copy-start.3 = (f32[6,2048]{1,0:T(8,128)S(1)}, f32[6,2048]{1,0:T(8,128)}, u32[]{:S(2)}) copy-start(f32[6,2048]{1,0:T(8,128)} %param.16) | copy-start | bytes 147460
  56.5 7.0 %copy-start.4 = (f32[6,2048]{1,0:T(8,128)S(1)}, f32[6,2048]{1,0:T(8,128)}, u32[]{:S(2)}) copy-start(f32[6,2048]{1,0:T(8,128)} %param.15) | copy-start | bytes 147460
  56.5 12.6 %all-to-all-start = ((f32[1,8,2048]{2,0,1:T(1,128)}), f32[1,8,2048]{2,0,1:T(1,128)S(1)}, u32[]{:S(2)}, u32[]{:S(2)}) async-start(f32[1,8,2048]{2,0,1:T(1,128)} %bitcast.14), calls=%async_computation | async-start | bytes 131072 | tf_op jit(solution)/shard_map/all_to_all | solution.py:160
  70.2 10.2 %all-to-all-start.1 = ((f32[8,1,2048]{2,1,0:T(1,128)}), f32[8,1,2048]{2,1,0:T(1,128)S(1)}, u32[]{:S(2)}, u32[]{:S(2)}) async-start(f32[8,1,2048]{2,1,0:T(1,128)} %copy.33), calls=%async_computation.1 | async-start | bytes 131072 | tf_op jit(solution)/shard_map/all_to_all | solution.py:162
Sparse Core Ops, SparseCore 0:
  20.2 34.6 all-reduce.59
where the time goes:
time: 94.2 us; the launch traced here: 93.7 us
  waiting for transfers between devices  44.6 us (47%)
  between operations  14.4 us (15%)
  other arithmetic  13.8 us (15%)
  starting transfers between devices  9.04 us (10%)
  blocking collectives  5.77 us (6%)
  local copies, waits for them, and re-layouts  5.39 us (6%)
    psum x1, waiting for transfers between devices, on_device(): summed = lax.psum(partial_terms, 'src')  32.9 us
    all_to_all x1, waiting for transfers between devices, on_device(): lax.all_to_all(updated, 'ep', split_axis=0, concat_axis=1, tiled=True)  6.16 us
    all_gather x1, blocking collectives, on_device(): lax.all_gather(slab_share, 'src', axis=1, tiled=True)  5.77 us
    all_to_all x1, starting transfers between devices, on_device(): lax.all_to_all(local_rhs, 'ep', split_axis=1, concat_axis=0, tiled=True)  5.65 us
    all_to_all x1, waiting for transfers between devices, on_device(): lax.all_to_all(local_rhs, 'ep', split_axis=1, concat_axis=0, tiled=True)  5.53 us
    all_to_all x1, starting transfers between devices, on_device(): lax.all_to_all(updated, 'ep', split_axis=0, concat_axis=1, tiled=True)  3.35 us
    add x7, other arithmetic, relax(): iterate + RELAXATION * (right_side - operate(iterate, conductivity, face_...  2.93 us
    mul x24, other arithmetic, operate(): face_weights[position]  2.55 us
  transfers between devices with their start and end apart: 3, of which 3 were waited for; matrix products, arithmetic and copies ran while one was open for 4% of the time, Pallas kernels for 0%

commit v1 on v0

--- a/solution.py
+++ b/solution.py
@@ -138,31 +138,32 @@
 ):
     slab_epochs, size_x, size_y, size_z = log_conductivity.shape
     cell_count = size_x * size_y * size_z
-    share_cells = cell_count // lax.axis_size("src")
-    offset = lax.axis_index("src") * share_cells
-    total_epochs = slab_epochs * lax.axis_size("ep")
+    src_count = lax.axis_size("src")
+    ep_count = lax.axis_size("ep")
+    devices = src_count * ep_count
+    share_cells = cell_count // devices
+    total_epochs = slab_epochs * ep_count
     sources = source_field(source_cells, cell_count)
     factor = temporal_factor(total_epochs)
     sweeper = jax.vmap(sweep_epoch, in_axes=(0, 0, 0, None, None, 0))
     model_log = log_conductivity
-    forward = forward_field
-    adjoint = adjoint_field
     forward, adjoint, partial_terms = sweeper(
-        model_log, forward, adjoint, sources, receiver_cells, observed
+        model_log, forward_field, adjoint_field, sources, receiver_cells, observed
     )
-    partial_terms = partial_terms.reshape(slab_epochs, cell_count)
-    summed = lax.psum(partial_terms, "src")
-    gradient_share = lax.dynamic_slice_in_dim(summed, offset, share_cells, 1)
-    model_share = lax.dynamic_slice_in_dim(
-        model_log.reshape(slab_epochs, cell_count), offset, share_cells, 1
+    own_model = jnp.where(lax.axis_index("src") == 0, 1.0, 0.0) * model_log.reshape(
+        slab_epochs, cell_count
     )
-    local_rhs = model_share - STEP_SIZE * gradient_share
-    time_rhs = lax.all_to_all(local_rhs, "ep", split_axis=1, concat_axis=0, tiled=True)
+    partial_rhs = own_model - STEP_SIZE * partial_terms.reshape(slab_epochs, cell_count)
+    sent = partial_rhs.reshape(slab_epochs, devices, share_cells).transpose(1, 0, 2)
+    got = lax.all_to_all(sent, ("src", "ep"), split_axis=0, concat_axis=0, tiled=True)
+    time_rhs = got.reshape(src_count, total_epochs, share_cells).sum(axis=0)
     updated, split_term, dual_term = splitting_update(time_rhs, split_term, dual_term, factor)
-    slab_share = lax.all_to_all(updated, "ep", split_axis=0, concat_axis=1, tiled=True)
-    model_log = lax.all_gather(slab_share, "src", axis=1, tiled=True).reshape(
-        slab_epochs, size_x, size_y, size_z
-    )
+    back = jnp.broadcast_to(
+        updated.reshape(1, ep_count, slab_epochs, share_cells),
+        (src_count, ep_count, slab_epochs, share_cells),
+    ).reshape(devices, slab_epochs, share_cells)
+    model_rows = lax.all_to_all(back, ("src", "ep"), split_axis=0, concat_axis=0, tiled=True)
+    model_log = model_rows.transpose(1, 0, 2).reshape(slab_epochs, size_x, size_y, size_z)
     return (model_log, split_term, dual_term)
 
 

time: 94.2 us -> 47.4 us (0.50)
  waiting for transfers between devices: 44.6 us -> 17.3 us
  between operations: 14.4 us -> 1.03 us
  blocking collectives: 5.77 us -> 0 us
  other arithmetic: 13.8 us -> 12.4 us
    psum x1 -> x0, waiting for transfers between devices: 32.9 us -> none  [on_device(): summed = lax.psum(partial_terms, 'src')]
    all_gather x1 -> x0, blocking collectives: 5.77 us -> none  [on_device(): lax.all_gather(slab_share, 'src', axis=1, tiled=True)]
    all_to_all x2, waiting for transfers between devices: 11.7 us -> 17.3 us  [the longest x1 9.97 us: on_device(): lax.all_to_all(back, ('src', 'ep'), split_axis=0, concat_axis=0, tiled=True)]
    broadcast_in_dim x0 -> x2, local copies, waits for them, and re-layouts: none -> 1.03 us  [on_device(): jnp.broadcast_to(updated.reshape(1, ep_count, slab_epochs, share_cells),...]
    mul x1 -> x0, other arithmetic: 0.99 us -> none  [sweep_epoch(): gradient = conductivity[0] * jnp.sum(forward * adjoint, axis=0)]
  transfers between devices with their start and end apart: 3 -> 2, of which waited for: 3 -> 2; matrix products, arithmetic and copies ran while one was open for 4% -> 8% of each run, Pallas kernels for 0% -> 0%
where the time goes in v1:
time: 47.4 us; the launch traced here: 47 us
  waiting for transfers between devices  17.3 us (36%)
  other arithmetic  12.4 us (26%)
  starting transfers between devices  9.88 us (21%)
  local copies, waits for them, and re-layouts  5.74 us (12%)
  between operations  1.03 us (2%)
  matrix products  0.71 us (1%)
    all_to_all x1, waiting for transfers between devices, on_device(): lax.all_to_all(back, ('src', 'ep'), split_axis=0, concat_axis=0, tiled=True)  9.97 us
    all_to_all x1, waiting for transfers between devices, on_device(): lax.all_to_all(sent, ('src', 'ep'), split_axis=0, concat_axis=0, tiled=True)  7.31 us
    all_to_all x1, starting transfers between devices, on_device(): lax.all_to_all(sent, ('src', 'ep'), split_axis=0, concat_axis=0, tiled=True)  7.3 us
    add x7, other arithmetic, relax(): iterate + RELAXATION * (right_side - operate(iterate, conductivity, face_...  2.93 us
    all_to_all x1, starting transfers between devices, on_device(): lax.all_to_all(back, ('src', 'ep'), split_axis=0, concat_axis=0, tiled=True)  2.59 us
    mul x24, other arithmetic, operate(): face_weights[position]  2.55 us
    unnamed x18, local copies, waits for them, and re-layouts  2.23 us
    another operation x3, other arithmetic, temporal_factor(): return jnp.linalg.cholesky(matrix)  1.5 us
  transfers between devices with their start and end apart: 2, of which 2 were waited for; matrix products, arithmetic and copies ran while one was open for 8% of the time, Pallas kernels for 0%

profile of v1, /device:TPU:0, one launch (start us, length us, event | category | flops | bytes accessed | tf_op | source)
XLA Modules:
  0.0 47.0 jit_solution(17013736393892332482)
XLA Ops:
  0.6 0.0 copy-start.1
  0.6 1.0 %exponential_bitcast_fusion = f32[1,1,16,32,128]{4,3,2,1,0:T(8,128)S(1)} fusion(f32[1,16,32,128]{3,2,1,0:T(8,128)} %param.9), kind=kLoop, calls=%fused_computation.48 | loop fusion | bytes 524288 | tf_op jit(solution)/shard_map/vmap()/broadcast_in_dim | solution.py:77
  1.7 0.0 copy-done.1
  1.7 0.2 subtract_multiply_fusion
  1.9 0.1 subtract_multiply_fusion.1
  2.0 0.0 copy-start.2
  2.0 0.1 subtract_multiply_fusion.4
  2.1 0.9 %copy-done.2 = f32[1,1,16,32,128]{4,3,2,1,0:T(8,128)S(1)} copy-done((f32[1,1,16,32,128]{4,3,2,1,0:T(8,128)S(1)}, f32[1,1,16,32,128]{4,3,2,1,0:T(8,128)}, u32[]{:S(2)}) %copy-start.2) | copy-done | bytes 262168
  2.9 0.1 subtract_multiply_fusion.2
  3.1 0.0 copy-start.5
  3.1 0.7 %subtract_multiply_fusion.5 = f32[1,1,15,32,128]{4,3,2,1,0:T(8,128)} fusion(f32[1,1,15,32,128]{4,3,2,1,0:T(8,128)S(1)} %get-tuple-element.6, f32[1,1,16,32,128]{4,3,2,1,0:T(8,128)S(1)} %copy-done.2), kind=kLoop, calls=%fused_computation.64 | loop fusion | flops 122880 | bytes 983040 | tf_op jit(solution)/shard_map/vmap()/mul | solution.py:47
  3.9 0.0 copy-done.5
  3.9 0.0 copy-start
  3.9 0.1 copy.35
  4.0 0.1 pad_bitcast_fusion
  4.0 0.2 fusion.54
  4.2 0.8 %scatter_custom_fusion = f32[65536]{0:T(1024)S(1)} fusion(s32[2]{0:T(128)S(1)} %fusion.54, f32[2]{0:T(128)} %constant.220, f32[]{:T(128)} %constant.81.clone.1), kind=kCustom, calls=%fused_computation.67 | custom fusion | flops 2 | bytes 262656 | tf_op jit(solution)/shard_map/scatter-add | solution.py:71
  5.1 0.0 copy-done
  5.1 1.4 %divide_add_fusion.6 = (f32[1,1,16,32,128]{4,3,2,1,0:T(8,128)S(1)}, f32[1,1,16,32,128]{4,3,2,1,0:T(8,128)S(1)}) fusion(f32[1,1,16,32,128]{4,3,2,1,0:T(8,128)S(1)} %copy-done.2, f32[1,1,16,32,128]{4,3,2,1,0:T(8,128)S(1)} %bitcast.65, f32[1,1,16,32,127]{4,3,2,1,0:T(8,128)S(1)} %subtract_multiply_fusion.2, ...), kind=kLoop, calls=%fused_computation.44 | loop fusion | flops 1179648 | bytes 2830336 | tf_op jit(solution)/shard_map/vmap()/add | solution.py:60
  6.5 0.1 fusion.11
  6.6 0.1 fusion.10
  6.7 0.3 divide_add_fusion.5
  7.1 0.1 fusion.8
  7.2 0.3 divide_add_fusion.4
  7.6 0.0 copy-start.6
  7.6 0.1 fusion.6
  7.7 0.5 %copy-done.6 = s32[128]{0:T(128)S(1)} copy-done((s32[128]{0:T(128)S(1)}, s32[128]{0:T(128)}, u32[]{:S(2)}) %copy-start.6) | copy-done | bytes 536
  8.3 0.2 divide_add_fusion.3
  8.5 0.0 copy-start.7
  8.5 1.1 %gather_fusion = f32[128]{0:T(128)S(1)} fusion(f32[65536]{0:T(1024)S(1)} %bitcast.69, s32[1024]{0:T(1024)S(1)} %pad_clamp_fusion), kind=kCustom, calls=%fused_computation | custom fusion | bytes 1536 | tf_op jit(solution)/shard_map/vmap()/gather | solution.py:81
  9.7 0.0 copy-done.7
  9.7 1.3 %scatter_custom_fusion.1 = f32[65536]{0:T(1024)S(1)} fusion(s32[128]{0:T(128)S(1)} %compare_select_fusion, f32[128]{0:T(128)S(1)} %fusion.57, f32[]{:T(128)} %constant.81.clone.1), kind=kCustom, calls=%fused_computation.65 | custom fusion | flops 128 | bytes 262148 | tf_op jit(solution)/shard_map/vmap()/scatter-add | solution.py:85
  11.0 0.3 divide_add_fusion.2
  11.4 0.1 fusion.4
  11.5 0.3 divide_add_fusion.1
  11.9 0.1 fusion.2
  12.0 0.3 divide_add_fusion
  12.4 0.1 fusion
  12.5 1.0 %fusion.15 = f32[1,16,32,128]{3,2,1,0:T(8,128)} fusion(f32[1,1,16,32,128]{4,3,2,1,0:T(8,128)S(1)} %divide_add_fusion.3, f32[1,1,16,32,128]{4,3,2,1,0:T(8,128)S(1)} %divide_add_fusion, f32[1,1,16,32,128]{4,3,2,1,0:T(8,128)S(1)} %get-tuple-element.12, f32[1,1,16,32,128]{4,3,2,1,0:T(8,128)S(1)} %bitcast.64, f32[1,1,16,32,127]{4,3,2,1,0:T(8,128)S(1)} %fusion, ...), kind=kLoop, calls=%fused_computation.35 | loop fusion | flops 1114112 | bytes 2332676 | tf_op jit(solution)/shard_map/sub | solution.py:156
  13.5 7.3 %all-to-all-start = ((f32[32,1,2048]{2,1,0:T(1,128)}), f32[32,1,2048]{2,1,0:T(1,128)S(1)}, u32[]{:S(2)}, u32[]{:S(2)}) async-start(f32[32,1,2048]{2,1,0:T(1,128)} %bitcast.12), calls=%async_computation | async-start | bytes 524288 | tf_op jit(solution)/shard_map/all_to_all | solution.py:158
  20.9 0.0 copy-start.3
  20.9 0.0 copy-start.4
  20.9 0.3 convert_add_fusion
  21.1 0.1 copy.27
  21.2 0.7 %cholesky.17 = f32[8,8]{1,0:T(8,128)S(1)} custom-call(f32[8,8]{1,0:T(8,128)S(1)} %fusion.44), custom_call_target="Cholesky" | custom-call | tf_op jit(solution)/shard_map/jit(cholesky)/cholesky | solution.py:102
  21.9 0.1 copy.28
  22.0 0.2 select_reduce_fusion
  22.2 0.6 %compare_reduce_fusion = pred[]{:T(512)} fusion(f32[8]{0:T(128)S(1)} %select_reduce_fusion), kind=kLoop, calls=%fused_computation.113 | loop fusion | flops 15 | bytes 33 | tf_op jit(solution)/shard_map/jit(cholesky)/cholesky | solution.py:102
  22.8 0.6 %select_select_fusion = f32[8,8]{0,1:T(8,128)S(1)} fusion(f32[8,8]{0,1:T(8,128)S(1)} %copy.28, pred[]{:T(512)} %compare_reduce_fusion), kind=kLoop, calls=%fused_computation.88 | loop fusion | flops 256 | bytes 513 | tf_op jit(solution)/shard_map/jit(_cho_solve)/triangular_solve | solution.py:122
  23.5 0.1 copy.30
  23.5 0.6 %custom-call.10 = f32[1,8,8]{1,2,0:T(8,128)S(1)} custom-call(f32[1,8,8]{2,1,0:T(8,128)S(1)} %bitcast.71), custom_call_target="InvertDiagBlocksLowerTriangular" | custom-call | tf_op jit(solution)/shard_map/jit(_cho_solve)/triangular_solve | solution.py:122
  24.2 0.0 copy-done.3
  24.2 0.0 copy-done.4
  24.2 7.3 %all-to-all-done = f32[32,1,2048]{2,1,0:T(1,128)S(1)} async-done(((f32[32,1,2048]{2,1,0:T(1,128)}), f32[32,1,2048]{2,1,0:T(1,128)S(1)}, u32[]{:S(2)}, u32[]{:S(2)}) %all-to-all-start) | async-done | bytes 262176 | tf_op jit(solution)/shard_map/all_to_all | solution.py:158
  31.5 0.1 bitcast_reduce_fusion
  31.6 0.3 fusion.29
  31.8 0.2 fusion.41
  32.1 1.0 %broadcast_in_dim.35 = f32[32,1,2048]{2,1,0:T(1,128)} reshape(f32[4,8,2048]{2,1,0:T(8,128)S(1)} %broadcast_in_dim.34) | data formatting | bytes 524288 | tf_op jit(solution)/shard_map/broadcast_in_dim | solution.py:161
  33.1 2.6 %all-to-all-start.1 = ((f32[32,1,2048]{2,1,0:T(1,128)}), f32[32,1,2048]{2,1,0:T(1,128)S(1)}, u32[]{:S(2)}, u32[]{:S(2)}) async-start(f32[32,1,2048]{2,1,0:T(1,128)} %broadcast_in_dim.35), calls=%async_computation.1 | async-start | bytes 524288 | tf_op jit(solution)/shard_map/all_to_all | solution.py:165
  35.7 0.7 %fusion.63 = (f32[6,2048]{1,0:T(8,128)}, f32[6,2048]{1,0:T(8,128)}) fusion(f32[6,2048]{1,0:T(8,128)S(1)} %copy-done.3, f32[8,2048]{1,0:T(8,128)S(1)} %fusion.41), kind=kLoop, calls=%fused_computation.127 | loop fusion | flops 86016 | bytes 294912 | tf_op jit(solution)/shard_map/sub | solution.py:125
  36.3 10.0 %all-to-all-done.1 = f32[32,1,2048]{2,1,0:T(1,128)S(1)} async-done(((f32[32,1,2048]{2,1,0:T(1,128)}), f32[32,1,2048]{2,1,0:T(1,128)S(1)}, u32[]{:S(2)}, u32[]{:S(2)}) %all-to-all-start.1) | async-done | bytes 262176 | tf_op jit(solution)/shard_map/all_to_all | solution.py:165
  46.3 0.7 %copy.38 = f32[1,16,32,128]{3,2,1,0:T(8,128)} copy(f32[1,16,32,128]{3,2,1,0:T(8,128)S(1)} %bitcast.70) | data formatting | bytes 524288
  (20 shorter events, 0.6 us)
Async XLA Ops:
  0.6 1.1 %copy-start.1 = (f32[1,1,16,32,128]{4,3,2,1,0:T(8,128)S(1)}, f32[1,1,16,32,128]{4,3,2,1,0:T(8,128)}, u32[]{:S(2)}) copy-start(f32[1,1,16,32,128]{4,3,2,1,0:T(8,128)} %param.11) | copy-start | bytes 786436
  2.0 1.0 %copy-start.2 = (f32[1,1,16,32,128]{4,3,2,1,0:T(8,128)S(1)}, f32[1,1,16,32,128]{4,3,2,1,0:T(8,128)}, u32[]{:S(2)}) copy-start(f32[1,1,16,32,128]{4,3,2,1,0:T(8,128)} %param.10) | copy-start | bytes 786436
  3.1 0.7 %copy-start.5 = (s32[1,2]{1,0:T(1,128)S(1)}, s32[1,2]{1,0:T(1,128)}, u32[]{:S(2)}) copy-start(s32[1,2]{1,0:T(1,128)} %param.12) | copy-start | bytes 28
  3.9 1.2 %copy-start = (f32[1,16,32,128]{3,2,1,0:T(8,128)S(1)}, f32[1,16,32,128]{3,2,1,0:T(8,128)}, u32[]{:S(2)}) copy-start(f32[1,16,32,128]{3,2,1,0:T(8,128)} %param.9) | copy-start | bytes 786436
  7.6 0.7 %copy-start.6 = (s32[128]{0:T(128)S(1)}, s32[128]{0:T(128)}, u32[]{:S(2)}) copy-start(s32[128]{0:T(128)} %param.13) | copy-start | bytes 1540
  8.5 1.2 %copy-start.7 = (f32[1,1,128]{2,1,0:T(1,128)S(1)}, f32[1,1,128]{2,1,0:T(1,128)}, u32[]{:S(2)}) copy-start(f32[1,1,128]{2,1,0:T(1,128)} %param.14) | copy-start | bytes 1540
  13.5 18.0 %all-to-all-start = ((f32[32,1,2048]{2,1,0:T(1,128)}), f32[32,1,2048]{2,1,0:T(1,128)S(1)}, u32[]{:S(2)}, u32[]{:S(2)}) async-start(f32[32,1,2048]{2,1,0:T(1,128)} %bitcast.12), calls=%async_computation | async-start | bytes 524288 | tf_op jit(solution)/shard_map/all_to_all | solution.py:158
  20.9 3.3 %copy-start.3 = (f32[6,2048]{1,0:T(8,128)S(1)}, f32[6,2048]{1,0:T(8,128)}, u32[]{:S(2)}) copy-start(f32[6,2048]{1,0:T(8,128)} %param.16) | copy-start | bytes 147460
  20.9 3.3 %copy-start.4 = (f32[6,2048]{1,0:T(8,128)S(1)}, f32[6,2048]{1,0:T(8,128)}, u32[]{:S(2)}) copy-start(f32[6,2048]{1,0:T(8,128)} %param.15) | copy-start | bytes 147460
  33.1 13.2 %all-to-all-start.1 = ((f32[32,1,2048]{2,1,0:T(1,128)}), f32[32,1,2048]{2,1,0:T(1,128)S(1)}, u32[]{:S(2)}, u32[]{:S(2)}) async-start(f32[32,1,2048]{2,1,0:T(1,128)} %broadcast_in_dim.35), calls=%async_computation.1 | async-start | bytes 524288 | tf_op jit(solution)/shard_map/all_to_all | solution.py:165

commit v2 on v1

--- a/solution.py
+++ b/solution.py
@@ -1,7 +1,11 @@
+import functools
+
 import jax
 import jax.numpy as jnp
 from jax import lax
 from jax.sharding import PartitionSpec as P
+from jax.experimental import pallas as pl
+from jax.experimental.pallas import tpu as pltpu
 
 SWEEPS = 4
 
@@ -124,6 +128,97 @@
     split_term = shifted - jnp.clip(shifted, -THRESHOLD, THRESHOLD)
     dual_term = shifted - split_term
     return (updated, split_term, dual_term)
+
+
+def stencil_kernel(
+    size_y,
+    model_ref, forward_ref, adjoint_ref, keep_ref, source_ref, receiver_ref, observed_ref,
+    out_ref, field_ref, drive_ref,
+):
+    rows, lanes = model_ref.shape
+    conductivity = jnp.exp(model_ref[...])
+    row_id = lax.broadcasted_iota(jnp.int32, (rows, lanes), 0)
+    lane_id = lax.broadcasted_iota(jnp.int32, (rows, lanes), 1)
+    def next_z(v):
+        return pltpu.roll(v, lanes - 1, 1)
+
+    def prev_z(v):
+        return pltpu.roll(v, 1, 1)
+
+    def next_y(v):
+        return pltpu.roll(v, rows - 1, 0)
+
+    def prev_y(v):
+        return pltpu.roll(v, 1, 0)
+
+    def next_x(v):
+        return jnp.concatenate([v[size_y:], v[:size_y]], axis=0)
+
+    def prev_x(v):
+        return jnp.concatenate([v[rows - size_y:], v[: rows - size_y]], axis=0)
+
+    zero = jnp.zeros_like(conductivity)
+    weight_x = jnp.where(row_id < rows - size_y, 0.5 * (conductivity + next_x(conductivity)), zero)
+    weight_y = jnp.where(row_id % size_y < size_y - 1, 0.5 * (conductivity + next_y(conductivity)), zero)
+    weight_z = jnp.where(lane_id < lanes - 1, 0.5 * (conductivity + next_z(conductivity)), zero)
+    mass = MASS_TERM * conductivity
+    diagonal = mass + weight_x + prev_x(weight_x)
+    diagonal = diagonal + weight_y + prev_y(weight_y)
+    diagonal = diagonal + weight_z + prev_z(weight_z)
+
+    def operate(v):
+        result = mass * v
+        flux = weight_x * (next_x(v) - v)
+        result = result - flux + prev_x(flux)
+        flux = weight_y * (next_y(v) - v)
+        result = result - flux + prev_y(flux)
+        flux = weight_z * (next_z(v) - v)
+        result = result - flux + prev_z(flux)
+        return result
+
+    def relax(v, right_side):
+        for sweep_index in range(SWEEPS):
+            v = v + RELAXATION * (right_side - operate(v)) / diagonal
+        return v
+
+    one_row = lax.broadcasted_iota(jnp.int32, (1, lanes), 1)
+
+    def add_at(cell, amount):
+        row = cell // lanes
+        drive_ref[pl.ds(row, 1), :] += jnp.where(one_row == cell % lanes, amount, 0.0)
+
+    drive_ref[...] = zero
+    add_at(source_ref[0], CURRENT)
+    add_at(source_ref[1], -CURRENT)
+    forward = relax(forward_ref[...], drive_ref[...])
+    field_ref[...] = forward
+    drive_ref[...] = zero
+
+    def gather_scatter(index, carry):
+        cell = receiver_ref[index]
+        row = cell // lanes
+        hit = one_row == cell % lanes
+        value = jnp.sum(jnp.where(hit, field_ref[pl.ds(row, 1), :], 0.0), axis=1, keepdims=True)
+        misfit = value - observed_ref[index]
+        drive_ref[pl.ds(row, 1), :] += jnp.where(hit, DATA_WEIGHT * misfit, 0.0)
+        return carry
+
+    lax.fori_loop(0, receiver_ref.shape[0], gather_scatter, 0)
+    adjoint = relax(adjoint_ref[...], drive_ref[...])
+    out_ref[...] = keep_ref[0] * model_ref[...] - STEP_SIZE * (conductivity * (forward * adjoint))
+
+
+def stencil_terms(size_y, model, forward, adjoint, keep, source_cells, receiver_cells, observed):
+    rows, lanes = model.shape
+    vmem = pl.BlockSpec(memory_space=pltpu.VMEM)
+    smem = pl.BlockSpec(memory_space=pltpu.SMEM)
+    return pl.pallas_call(
+        functools.partial(stencil_kernel, size_y),
+        out_shape=jax.ShapeDtypeStruct((rows, lanes), jnp.float32),
+        in_specs=[vmem, vmem, vmem, smem, smem, smem, smem],
+        out_specs=vmem,
+        scratch_shapes=[pltpu.VMEM((rows, lanes), jnp.float32), pltpu.VMEM((rows, lanes), jnp.float32)],
+    )(model, forward, adjoint, keep, source_cells, receiver_cells, observed)
 
 
 def on_device(
@@ -142,28 +237,32 @@
     ep_count = lax.axis_size("ep")
     devices = src_count * ep_count
     share_cells = cell_count // devices
+    share_rows = share_cells // size_z
     total_epochs = slab_epochs * ep_count
-    sources = source_field(source_cells, cell_count)
     factor = temporal_factor(total_epochs)
-    sweeper = jax.vmap(sweep_epoch, in_axes=(0, 0, 0, None, None, 0))
-    model_log = log_conductivity
-    forward, adjoint, partial_terms = sweeper(
-        model_log, forward_field, adjoint_field, sources, receiver_cells, observed
-    )
-    own_model = jnp.where(lax.axis_index("src") == 0, 1.0, 0.0) * model_log.reshape(
-        slab_epochs, cell_count
-    )
-    partial_rhs = own_model - STEP_SIZE * partial_terms.reshape(slab_epochs, cell_count)
-    sent = partial_rhs.reshape(slab_epochs, devices, share_cells).transpose(1, 0, 2)
+    keep = jnp.where(lax.axis_index("src") == 0, 1.0, 0.0).astype(jnp.float32).reshape(1)
+    partial_rhs = stencil_terms(
+        size_y,
+        log_conductivity.reshape(size_x * size_y, size_z),
+        forward_field.reshape(size_x * size_y, size_z),
+        adjoint_field.reshape(size_x * size_y, size_z),
+        keep,
+        source_cells.reshape(2),
+        receiver_cells,
+        observed.reshape(-1),
+    )
+    sent = partial_rhs.reshape(devices, share_rows, size_z)
     got = lax.all_to_all(sent, ("src", "ep"), split_axis=0, concat_axis=0, tiled=True)
-    time_rhs = got.reshape(src_count, total_epochs, share_cells).sum(axis=0)
-    updated, split_term, dual_term = splitting_update(time_rhs, split_term, dual_term, factor)
+    time_rhs = got.reshape(src_count, total_epochs, share_rows, size_z).sum(axis=0)
+    updated, split_term, dual_term = splitting_update(
+        time_rhs.reshape(total_epochs, share_cells), split_term, dual_term, factor
+    )
     back = jnp.broadcast_to(
-        updated.reshape(1, ep_count, slab_epochs, share_cells),
-        (src_count, ep_count, slab_epochs, share_cells),
-    ).reshape(devices, slab_epochs, share_cells)
+        updated.reshape(1, total_epochs, share_rows, size_z),
+        (src_count, total_epochs, share_rows, size_z),
+    ).reshape(devices, share_rows, size_z)
     model_rows = lax.all_to_all(back, ("src", "ep"), split_axis=0, concat_axis=0, tiled=True)
-    model_log = model_rows.transpose(1, 0, 2).reshape(slab_epochs, size_x, size_y, size_z)
+    model_log = model_rows.reshape(slab_epochs, size_x, size_y, size_z)
     return (model_log, split_term, dual_term)
 
 

time: 47.4 us -> 48.5 us (1.023)
  Pallas kernels: 0 us -> 14.4 us
  other arithmetic: 12.4 us -> 3.49 us
  local copies, waits for them, and re-layouts: 5.74 us -> 1.67 us
    pallas_call x0 -> x1, Pallas kernels: none -> 14.4 us  [stencil_terms(): pl.pallas_call(functools.partial(stencil_kernel, size_y), out_shape=jax.S...]
    add x7 -> x0, other arithmetic: 2.93 us -> none  [relax(): iterate + RELAXATION * (right_side - operate(iterate, conductivity, face_...]
    mul x25 -> x0, other arithmetic: 2.56 us -> none  [the longest x24 2.55 us: operate(): face_weights[position]]
    scatter-add x2 -> x0, other arithmetic: 2.13 us -> none  [the longest x1 1.32 us: sweep_epoch(): adjoint_source = jnp.zeros_like(flat_field).at[:, receiver_cells].add(DAT...]
    unnamed x18 -> x5, local copies, waits for them, and re-layouts: 2.23 us -> 0.72 us
    broadcast_in_dim x3 -> x2, local copies, waits for them, and re-layouts: 2.07 us -> 0.74 us  [on_device(): jnp.broadcast_to(updated.reshape(1, total_epochs, share_rows, size_z), (s...]
    gather x1 -> x0, local copies, waits for them, and re-layouts: 1.15 us -> none  [sweep_epoch(): misfit = flat_field[:, receiver_cells] - observed]
    sub x1 -> x0, other arithmetic: 1 us -> none  [on_device(): own_model - STEP_SIZE * partial_terms.reshape(slab_epochs, cell_count)]
where the time goes in v2:
time: 48.5 us; the launch traced here: 48.1 us
  waiting for transfers between devices  17.3 us (36%)
  Pallas kernels  14.4 us (30%)
  starting transfers between devices  9.88 us (20%)
  other arithmetic  3.49 us (7%)
  local copies, waits for them, and re-layouts  1.67 us (3%)
  between operations  0.73 us (2%)
  matrix products  0.71 us (1%)
    pallas_call x1, Pallas kernels, stencil_terms(): pl.pallas_call(functools.partial(stencil_kernel, size_y), out_shape=jax.S...  14.4 us
    all_to_all x1, waiting for transfers between devices, on_device(): lax.all_to_all(back, ('src', 'ep'), split_axis=0, concat_axis=0, tiled=True)  9.97 us
    all_to_all x1, waiting for transfers between devices, on_device(): lax.all_to_all(sent, ('src', 'ep'), split_axis=0, concat_axis=0, tiled=True)  7.31 us
    all_to_all x1, starting transfers between devices, on_device(): lax.all_to_all(sent, ('src', 'ep'), split_axis=0, concat_axis=0, tiled=True)  7.3 us
    all_to_all x1, starting transfers between devices, on_device(): lax.all_to_all(back, ('src', 'ep'), split_axis=0, concat_axis=0, tiled=True)  2.59 us
    another operation x3, other arithmetic, temporal_factor(): return jnp.linalg.cholesky(matrix)  1.5 us
    another operation x2, other arithmetic, splitting_update(): updated = jax.scipy.linalg.cho_solve((factor, True), right_side)  1.28 us
  transfers between devices with their start and end apart: 2, of which 2 were waited for; matrix products, arithmetic and copies ran while one was open for 8% of the time, Pallas kernels for 0%

profile of v2, /device:TPU:0, one launch (start us, length us, event | category | flops | bytes accessed | tf_op | source)
XLA Modules:
  0.0 48.1 jit_solution(9740817765758740226)
XLA Ops:
  0.6 14.4 %shard_map.103 = f32[512,128]{1,0:T(8,128)} custom-call(f32[512,128]{1,0:T(8,128)} %bitcast.35, f32[512,128]{1,0:T(8,128)} %bitcast.36, f32[512,128]{1,0:T(8,128)} %bitcast.37, f32[1]{0:T(128)} %bitcast.6.keep_ref, s32[2]{0:T(128)} %bitcast.39, s32[128]{0:T(128)} %receiver_ref.1, f32[128]{0:T(128)} %bitcast.40), custom_call_target="tpu_custom_call" | custom-call | tf_op jit(solution)/shard_map/pallas_call | solution.py:215
  15.0 7.3 %all-to-all-start = ((f32[32,16,128]{2,1,0:T(8,128)}), f32[32,16,128]{2,1,0:T(8,128)S(1)}, u32[]{:S(2)}, u32[]{:S(2)}) async-start(f32[32,16,128]{2,1,0:T(8,128)} %bitcast.33), calls=%async_computation | async-start | bytes 524288 | tf_op jit(solution)/shard_map/all_to_all | solution.py:255
  22.3 0.0 copy-start
  22.4 0.0 copy-start.1
  22.4 0.3 convert_add_fusion
  22.6 0.1 copy.19
  22.7 0.7 %cholesky.17 = f32[8,8]{1,0:T(8,128)S(1)} custom-call(f32[8,8]{1,0:T(8,128)S(1)} %fusion.17), custom_call_target="Cholesky" | custom-call | tf_op jit(solution)/shard_map/jit(cholesky)/cholesky | solution.py:106
  23.4 0.1 copy.20
  23.5 0.2 select_reduce_fusion
  23.6 0.6 %compare_reduce_fusion = pred[]{:T(512)} fusion(f32[8]{0:T(128)S(1)} %select_reduce_fusion), kind=kLoop, calls=%fused_computation.42 | loop fusion | flops 15 | bytes 33 | tf_op jit(solution)/shard_map/jit(cholesky)/cholesky | solution.py:106
  24.3 0.6 %select_select_fusion = f32[8,8]{0,1:T(8,128)S(1)} fusion(f32[8,8]{0,1:T(8,128)S(1)} %copy.20, pred[]{:T(512)} %compare_reduce_fusion), kind=kLoop, calls=%fused_computation.21 | loop fusion | flops 256 | bytes 513 | tf_op jit(solution)/shard_map/jit(_cho_solve)/triangular_solve | solution.py:126
  24.9 0.1 copy.22
  25.0 0.6 %custom-call.10 = f32[1,8,8]{1,2,0:T(8,128)S(1)} custom-call(f32[1,8,8]{2,1,0:T(8,128)S(1)} %bitcast.38), custom_call_target="InvertDiagBlocksLowerTriangular" | custom-call | tf_op jit(solution)/shard_map/jit(_cho_solve)/triangular_solve | solution.py:126
  25.6 0.0 copy-done
  25.6 0.0 copy-done.1
  25.7 7.3 %all-to-all-done = f32[32,16,128]{2,1,0:T(8,128)S(1)} async-done(((f32[32,16,128]{2,1,0:T(8,128)}), f32[32,16,128]{2,1,0:T(8,128)S(1)}, u32[]{:S(2)}, u32[]{:S(2)}) %all-to-all-start) | async-done | bytes 262176 | tf_op jit(solution)/shard_map/all_to_all | solution.py:255
  33.0 0.3 fusion
  33.3 0.2 fusion.14
  33.5 0.7 %broadcast_in_dim.10 = f32[4,8,16,128]{3,2,1,0:T(8,128)} broadcast(f32[8,16,128]{2,1,0:T(8,128)S(1)} %copy.24), dimensions={1,2,3} | broadcast | bytes 327680 | tf_op jit(solution)/shard_map/broadcast_in_dim | solution.py:260
  34.2 2.6 %all-to-all-start.1 = ((f32[32,16,128]{2,1,0:T(8,128)}), f32[32,16,128]{2,1,0:T(8,128)S(1)}, u32[]{:S(2)}, u32[]{:S(2)}) async-start(f32[32,16,128]{2,1,0:T(8,128)} %bitcast.12), calls=%async_computation.1 | async-start | bytes 524288 | tf_op jit(solution)/shard_map/all_to_all | solution.py:264
  36.8 0.7 %fusion.32 = (f32[6,2048]{1,0:T(8,128)}, f32[6,2048]{1,0:T(8,128)}) fusion(f32[6,2048]{1,0:T(8,128)S(1)} %copy-done, f32[8,2048]{1,0:T(8,128)S(1)} %fusion.14), kind=kLoop, calls=%fused_computation.50 | loop fusion | flops 86016 | bytes 294912 | tf_op jit(solution)/shard_map/sub | solution.py:129
  37.5 10.0 %all-to-all-done.1 = f32[32,16,128]{2,1,0:T(8,128)S(1)} async-done(((f32[32,16,128]{2,1,0:T(8,128)}), f32[32,16,128]{2,1,0:T(8,128)S(1)}, u32[]{:S(2)}, u32[]{:S(2)}) %all-to-all-start.1) | async-done | bytes 262176 | tf_op jit(solution)/shard_map/all_to_all | solution.py:264
  47.4 0.7 %copy.32 = f32[1,16,32,128]{3,2,1,0:T(8,128)} copy(f32[1,16,32,128]{3,2,1,0:T(8,128)S(1)} %bitcast.32) | data formatting | bytes 524288
  (5 shorter events, 0.1 us)
Async XLA Ops:
  15.0 18.0 %all-to-all-start = ((f32[32,16,128]{2,1,0:T(8,128)}), f32[32,16,128]{2,1,0:T(8,128)S(1)}, u32[]{:S(2)}, u32[]{:S(2)}) async-start(f32[32,16,128]{2,1,0:T(8,128)} %bitcast.33), calls=%async_computation | async-start | bytes 524288 | tf_op jit(solution)/shard_map/all_to_all | solution.py:255
  22.3 3.3 %copy-start = (f32[6,2048]{1,0:T(8,128)S(1)}, f32[6,2048]{1,0:T(8,128)}, u32[]{:S(2)}) copy-start(f32[6,2048]{1,0:T(8,128)} %param.15) | copy-start | bytes 147460
  22.4 3.3 %copy-start.1 = (f32[6,2048]{1,0:T(8,128)S(1)}, f32[6,2048]{1,0:T(8,128)}, u32[]{:S(2)}) copy-start(f32[6,2048]{1,0:T(8,128)} %param.14) | copy-start | bytes 147460
  34.2 13.2 %all-to-all-start.1 = ((f32[32,16,128]{2,1,0:T(8,128)}), f32[32,16,128]{2,1,0:T(8,128)S(1)}, u32[]{:S(2)}, u32[]{:S(2)}) async-start(f32[32,16,128]{2,1,0:T(8,128)} %bitcast.12), calls=%async_computation.1 | async-start | bytes 524288 | tf_op jit(solution)/shard_map/all_to_all | solution.py:264

commit v3 on v2

--- a/solution.py
+++ b/solution.py
@@ -132,8 +132,9 @@
 
 def stencil_kernel(
     size_y,
-    model_ref, forward_ref, adjoint_ref, keep_ref, source_ref, receiver_ref, observed_ref,
-    out_ref, field_ref, drive_ref,
+    model_ref, forward_ref, adjoint_ref, receiver_vec_ref, observed_vec_ref,
+    keep_ref, source_ref, receiver_ref,
+    out_ref, field_ref, drive_ref, picked_ref,
 ):
     rows, lanes = model_ref.shape
     conductivity = jnp.exp(model_ref[...])
@@ -192,33 +193,48 @@
     add_at(source_ref[1], -CURRENT)
     forward = relax(forward_ref[...], drive_ref[...])
     field_ref[...] = forward
-    drive_ref[...] = zero
-
-    def gather_scatter(index, carry):
+    receivers = receiver_ref.shape[0]
+
+    def pick_row(index, carry):
         cell = receiver_ref[index]
-        row = cell // lanes
-        hit = one_row == cell % lanes
-        value = jnp.sum(jnp.where(hit, field_ref[pl.ds(row, 1), :], 0.0), axis=1, keepdims=True)
-        misfit = value - observed_ref[index]
-        drive_ref[pl.ds(row, 1), :] += jnp.where(hit, DATA_WEIGHT * misfit, 0.0)
+        picked_ref[pl.ds(index, 1), :] = field_ref[pl.ds(cell // lanes, 1), :]
         return carry
 
-    lax.fori_loop(0, receiver_ref.shape[0], gather_scatter, 0)
-    adjoint = relax(adjoint_ref[...], drive_ref[...])
+    lax.fori_loop(0, receivers, pick_row, 0, unroll=8)
+    cells = receiver_vec_ref[...]
+    picked = picked_ref[...].T
+    hit = lax.broadcasted_iota(jnp.int32, (lanes, receivers), 0) == cells % lanes
+    value = jnp.sum(jnp.where(hit, picked, 0.0), axis=0, keepdims=True)
+    misfit = value - observed_vec_ref[...]
+    weighted = jnp.where(hit, DATA_WEIGHT * misfit, 0.0)
+    placed = (lax.broadcasted_iota(jnp.int32, (rows, receivers), 0) == cells // lanes).astype(jnp.float32)
+    drive = lax.dot_general(
+        placed, weighted, (((1,), (1,)), ((), ())),
+        precision=lax.Precision.HIGHEST, preferred_element_type=jnp.float32,
+    )
+    adjoint = relax(adjoint_ref[...], drive)
     out_ref[...] = keep_ref[0] * model_ref[...] - STEP_SIZE * (conductivity * (forward * adjoint))
 
 
 def stencil_terms(size_y, model, forward, adjoint, keep, source_cells, receiver_cells, observed):
     rows, lanes = model.shape
+    receivers = receiver_cells.shape[0]
     vmem = pl.BlockSpec(memory_space=pltpu.VMEM)
     smem = pl.BlockSpec(memory_space=pltpu.SMEM)
     return pl.pallas_call(
         functools.partial(stencil_kernel, size_y),
         out_shape=jax.ShapeDtypeStruct((rows, lanes), jnp.float32),
-        in_specs=[vmem, vmem, vmem, smem, smem, smem, smem],
+        in_specs=[vmem, vmem, vmem, vmem, vmem, smem, smem, smem],
         out_specs=vmem,
-        scratch_shapes=[pltpu.VMEM((rows, lanes), jnp.float32), pltpu.VMEM((rows, lanes), jnp.float32)],
-    )(model, forward, adjoint, keep, source_cells, receiver_cells, observed)
+        scratch_shapes=[
+            pltpu.VMEM((rows, lanes), jnp.float32),
+            pltpu.VMEM((rows, lanes), jnp.float32),
+            pltpu.VMEM((receivers, lanes), jnp.float32),
+        ],
+    )(
+        model, forward, adjoint, receiver_cells.reshape(1, receivers),
+        observed.reshape(1, receivers), keep, source_cells, receiver_cells,
+    )
 
 
 def on_device(

time: 48.5 us -> 38.9 us (0.80)
  Pallas kernels: 14.4 us -> 4.83 us
    pallas_call x1, Pallas kernels: 14.4 us -> 4.83 us  [stencil_terms(): pl.pallas_call(functools.partial(stencil_kernel, size_y), out_shape=jax.S...]
  transfers between devices with their start and end apart: 2 -> 2, of which waited for: 2 -> 2; matrix products, arithmetic and copies ran while one was open for 8% -> 10% of each run, Pallas kernels for 0% -> 0%
where the time goes in v3:
time: 38.9 us; the launch traced here: 38.6 us
  waiting for transfers between devices  17.3 us (44%)
  starting transfers between devices  9.88 us (25%)
  Pallas kernels  4.83 us (12%)
  other arithmetic  3.49 us (9%)
  local copies, waits for them, and re-layouts  1.67 us (4%)
  between operations  0.73 us (2%)
  matrix products  0.71 us (2%)
    all_to_all x1, waiting for transfers between devices, on_device(): lax.all_to_all(back, ('src', 'ep'), split_axis=0, concat_axis=0, tiled=True)  9.97 us
    all_to_all x1, waiting for transfers between devices, on_device(): lax.all_to_all(sent, ('src', 'ep'), split_axis=0, concat_axis=0, tiled=True)  7.31 us
    all_to_all x1, starting transfers between devices, on_device(): lax.all_to_all(sent, ('src', 'ep'), split_axis=0, concat_axis=0, tiled=True)  7.3 us
    pallas_call x1, Pallas kernels, stencil_terms(): pl.pallas_call(functools.partial(stencil_kernel, size_y), out_shape=jax.S...  4.83 us
    all_to_all x1, starting transfers between devices, on_device(): lax.all_to_all(back, ('src', 'ep'), split_axis=0, concat_axis=0, tiled=True)  2.59 us
    another operation x3, other arithmetic, temporal_factor(): return jnp.linalg.cholesky(matrix)  1.5 us
    another operation x2, other arithmetic, splitting_update(): updated = jax.scipy.linalg.cho_solve((factor, True), right_side)  1.28 us
  transfers between devices with their start and end apart: 2, of which 2 were waited for; matrix products, arithmetic and copies ran while one was open for 10% of the time, Pallas kernels for 0%

profile of v3, /device:TPU:0, one launch (start us, length us, event | category | flops | bytes accessed | tf_op | source)
XLA Modules:
  0.0 38.6 jit_solution(2723697269845605546)
XLA Ops:
  0.6 4.8 %shard_map.103 = f32[512,128]{1,0:T(8,128)} custom-call(f32[512,128]{1,0:T(8,128)} %bitcast.36, f32[512,128]{1,0:T(8,128)} %bitcast.37, f32[512,128]{1,0:T(8,128)} %bitcast.38, s32[1,128]{1,0:T(1,128)} %bitcast.40, f32[1,128]{1,0:T(1,128)} %bitcast.41, f32[1]{0:T(128)} %bitcast.8.keep_ref, s32[2]{0:T(128)} %bitcast.42, s32[128]{0:T(128)} %receiver_ref.1), custom_call_target="tpu_custom_call" | custom-call | tf_op jit(solution)/shard_map/pallas_call | solution.py:224
  5.5 7.3 %all-to-all-start = ((f32[32,16,128]{2,1,0:T(8,128)}), f32[32,16,128]{2,1,0:T(8,128)S(1)}, u32[]{:S(2)}, u32[]{:S(2)}) async-start(f32[32,16,128]{2,1,0:T(8,128)} %bitcast.34), calls=%async_computation | async-start | bytes 524288 | tf_op jit(solution)/shard_map/all_to_all | solution.py:271
  12.8 0.0 copy-start
  12.8 0.0 copy-start.1
  12.8 0.3 convert_add_fusion
  13.1 0.1 copy.19
  13.2 0.7 %cholesky.17 = f32[8,8]{1,0:T(8,128)S(1)} custom-call(f32[8,8]{1,0:T(8,128)S(1)} %fusion.17), custom_call_target="Cholesky" | custom-call | tf_op jit(solution)/shard_map/jit(cholesky)/cholesky | solution.py:106
  13.9 0.1 copy.20
  13.9 0.2 select_reduce_fusion
  14.1 0.6 %compare_reduce_fusion = pred[]{:T(512)} fusion(f32[8]{0:T(128)S(1)} %select_reduce_fusion), kind=kLoop, calls=%fused_computation.42 | loop fusion | flops 15 | bytes 33 | tf_op jit(solution)/shard_map/jit(cholesky)/cholesky | solution.py:106
  14.7 0.6 %select_select_fusion = f32[8,8]{0,1:T(8,128)S(1)} fusion(f32[8,8]{0,1:T(8,128)S(1)} %copy.20, pred[]{:T(512)} %compare_reduce_fusion), kind=kLoop, calls=%fused_computation.21 | loop fusion | flops 256 | bytes 513 | tf_op jit(solution)/shard_map/jit(_cho_solve)/triangular_solve | solution.py:126
  15.4 0.1 copy.22
  15.5 0.6 %custom-call.10 = f32[1,8,8]{1,2,0:T(8,128)S(1)} custom-call(f32[1,8,8]{2,1,0:T(8,128)S(1)} %bitcast.39), custom_call_target="InvertDiagBlocksLowerTriangular" | custom-call | tf_op jit(solution)/shard_map/jit(_cho_solve)/triangular_solve | solution.py:126
  16.1 0.0 copy-done
  16.1 0.0 copy-done.1
  16.1 7.3 %all-to-all-done = f32[32,16,128]{2,1,0:T(8,128)S(1)} async-done(((f32[32,16,128]{2,1,0:T(8,128)}), f32[32,16,128]{2,1,0:T(8,128)S(1)}, u32[]{:S(2)}, u32[]{:S(2)}) %all-to-all-start) | async-done | bytes 262176 | tf_op jit(solution)/shard_map/all_to_all | solution.py:271
  23.4 0.3 fusion
  23.7 0.2 fusion.14
  23.9 0.7 %broadcast_in_dim.10 = f32[4,8,16,128]{3,2,1,0:T(8,128)} broadcast(f32[8,16,128]{2,1,0:T(8,128)S(1)} %copy.24), dimensions={1,2,3} | broadcast | bytes 327680 | tf_op jit(solution)/shard_map/broadcast_in_dim | solution.py:276
  24.7 2.6 %all-to-all-start.1 = ((f32[32,16,128]{2,1,0:T(8,128)}), f32[32,16,128]{2,1,0:T(8,128)S(1)}, u32[]{:S(2)}, u32[]{:S(2)}) async-start(f32[32,16,128]{2,1,0:T(8,128)} %bitcast.13), calls=%async_computation.1 | async-start | bytes 524288 | tf_op jit(solution)/shard_map/all_to_all | solution.py:280
  27.2 0.7 %fusion.32 = (f32[6,2048]{1,0:T(8,128)}, f32[6,2048]{1,0:T(8,128)}) fusion(f32[6,2048]{1,0:T(8,128)S(1)} %copy-done, f32[8,2048]{1,0:T(8,128)S(1)} %fusion.14), kind=kLoop, calls=%fused_computation.50 | loop fusion | flops 86016 | bytes 294912 | tf_op jit(solution)/shard_map/sub | solution.py:129
  27.9 10.0 %all-to-all-done.1 = f32[32,16,128]{2,1,0:T(8,128)S(1)} async-done(((f32[32,16,128]{2,1,0:T(8,128)}), f32[32,16,128]{2,1,0:T(8,128)S(1)}, u32[]{:S(2)}, u32[]{:S(2)}) %all-to-all-start.1) | async-done | bytes 262176 | tf_op jit(solution)/shard_map/all_to_all | solution.py:280
  37.9 0.7 %copy.32 = f32[1,16,32,128]{3,2,1,0:T(8,128)} copy(f32[1,16,32,128]{3,2,1,0:T(8,128)S(1)} %bitcast.33) | data formatting | bytes 524288
  (5 shorter events, 0.1 us)
Async XLA Ops:
  5.5 18.0 %all-to-all-start = ((f32[32,16,128]{2,1,0:T(8,128)}), f32[32,16,128]{2,1,0:T(8,128)S(1)}, u32[]{:S(2)}, u32[]{:S(2)}) async-start(f32[32,16,128]{2,1,0:T(8,128)} %bitcast.34), calls=%async_computation | async-start | bytes 524288 | tf_op jit(solution)/shard_map/all_to_all | solution.py:271
  12.8 3.3 %copy-start = (f32[6,2048]{1,0:T(8,128)S(1)}, f32[6,2048]{1,0:T(8,128)}, u32[]{:S(2)}) copy-start(f32[6,2048]{1,0:T(8,128)} %param.15) | copy-start | bytes 147460
  12.8 3.3 %copy-start.1 = (f32[6,2048]{1,0:T(8,128)S(1)}, f32[6,2048]{1,0:T(8,128)}, u32[]{:S(2)}) copy-start(f32[6,2048]{1,0:T(8,128)} %param.14) | copy-start | bytes 147460
  24.7 13.2 %all-to-all-start.1 = ((f32[32,16,128]{2,1,0:T(8,128)}), f32[32,16,128]{2,1,0:T(8,128)S(1)}, u32[]{:S(2)}, u32[]{:S(2)}) async-start(f32[32,16,128]{2,1,0:T(8,128)} %bitcast.13), calls=%async_computation.1 | async-start | bytes 524288 | tf_op jit(solution)/shard_map/all_to_all | solution.py:280

commit v4 on v3

--- a/solution.py
+++ b/solution.py
@@ -235,6 +235,59 @@
         model, forward, adjoint, receiver_cells.reshape(1, receivers),
         observed.reshape(1, receivers), keep, source_cells, receiver_cells,
     )
+
+
+def solve_kernel(src_count, got_ref, split_ref, dual_ref, factor_ref, back_ref, split_out_ref, dual_out_ref):
+    epochs = factor_ref.shape[0]
+    rhs = []
+    for t in range(epochs):
+        total = got_ref[t]
+        for s in range(1, src_count):
+            total = total + got_ref[s * epochs + t]
+        rhs.append(total)
+    gap = [split_ref[k] - dual_ref[k] for k in range(epochs - 2)]
+    for t in range(epochs):
+        adjoint_term = gap[t] if t < epochs - 2 else jnp.zeros_like(rhs[t])
+        if 1 <= t <= epochs - 2:
+            adjoint_term = adjoint_term - 2.0 * gap[t - 1]
+        if t >= 2:
+            adjoint_term = adjoint_term + gap[t - 2]
+        rhs[t] = rhs[t] + PENALTY * adjoint_term
+    lower = []
+    for t in range(epochs):
+        total = rhs[t]
+        for j in range(t):
+            total = total - factor_ref[t, j] * lower[j]
+        lower.append(total / factor_ref[t, t])
+    solved = [None] * epochs
+    for t in reversed(range(epochs)):
+        total = lower[t]
+        for j in range(t + 1, epochs):
+            total = total - factor_ref[j, t] * solved[j]
+        solved[t] = total / factor_ref[t, t]
+    for k in range(epochs - 2):
+        shifted = solved[k] - 2.0 * solved[k + 1] + solved[k + 2] + dual_ref[k]
+        split = shifted - jnp.clip(shifted, -THRESHOLD, THRESHOLD)
+        split_out_ref[k] = split
+        dual_out_ref[k] = shifted - split
+    for s in range(src_count):
+        for t in range(epochs):
+            back_ref[s * epochs + t] = solved[t]
+
+
+def solve_epochs(src_count, got, split_term, dual_term, factor):
+    vmem = pl.BlockSpec(memory_space=pltpu.VMEM)
+    smem = pl.BlockSpec(memory_space=pltpu.SMEM)
+    return pl.pallas_call(
+        functools.partial(solve_kernel, src_count),
+        out_shape=(
+            jax.ShapeDtypeStruct(got.shape, jnp.float32),
+            jax.ShapeDtypeStruct(split_term.shape, jnp.float32),
+            jax.ShapeDtypeStruct(dual_term.shape, jnp.float32),
+        ),
+        in_specs=[vmem, vmem, vmem, smem],
+        out_specs=(vmem, vmem, vmem),
+    )(got, split_term, dual_term, factor)
 
 
 def on_device(
@@ -269,14 +322,16 @@
     )
     sent = partial_rhs.reshape(devices, share_rows, size_z)
     got = lax.all_to_all(sent, ("src", "ep"), split_axis=0, concat_axis=0, tiled=True)
-    time_rhs = got.reshape(src_count, total_epochs, share_rows, size_z).sum(axis=0)
-    updated, split_term, dual_term = splitting_update(
-        time_rhs.reshape(total_epochs, share_cells), split_term, dual_term, factor
-    )
-    back = jnp.broadcast_to(
-        updated.reshape(1, total_epochs, share_rows, size_z),
-        (src_count, total_epochs, share_rows, size_z),
-    ).reshape(devices, share_rows, size_z)
+    gaps = split_term.shape[0]
+    back, split_rows, dual_rows = solve_epochs(
+        src_count,
+        got,
+        split_term.reshape(gaps, share_rows, size_z),
+        dual_term.reshape(gaps, share_rows, size_z),
+        factor,
+    )
+    split_term = split_rows.reshape(gaps, share_cells)
+    dual_term = dual_rows.reshape(gaps, share_cells)
     model_rows = lax.all_to_all(back, ("src", "ep"), split_axis=0, concat_axis=0, tiled=True)
     model_log = model_rows.reshape(slab_epochs, size_x, size_y, size_z)
     return (model_log, split_term, dual_term)

time: 38.9 us -> 40.4 us (1.039)
  local copies, waits for them, and re-layouts: 1.67 us -> 3.58 us
  Pallas kernels: 4.83 us -> 6.67 us
  waiting for transfers between devices: 17.3 us -> 16.2 us
  other arithmetic: 3.49 us -> 2.65 us
  matrix products: 0.71 us -> 0.26 us
    unnamed x5 -> x13, local copies, waits for them, and re-layouts: 0.72 us -> 2.86 us
    pallas_call x0 -> x1, Pallas kernels: none -> 1.83 us  [solve_epochs(): pl.pallas_call(functools.partial(solve_kernel, src_count), out_shape=(jax...]
    another operation x2 -> x0, other arithmetic: 1.28 us -> none  [splitting_update(): updated = jax.scipy.linalg.cho_solve((factor, True), right_side)]
    select_n x0 -> x1, other arithmetic: none -> 1.24 us  [temporal_factor(): return jnp.linalg.cholesky(matrix)]
    all_to_all x1, waiting for transfers between devices: 9.97 us -> 9.19 us  [on_device(): lax.all_to_all(back, ('src', 'ep'), split_axis=0, concat_axis=0, tiled=True)]
    broadcast_in_dim x2 -> x0, local copies, waits for them, and re-layouts: 0.74 us -> none  [on_device(): jnp.broadcast_to(updated.reshape(1, total_epochs, share_rows, size_z), (s...]
    sub x2 -> x0, other arithmetic: 0.69 us -> none  [the longest x1 0.68 us: splitting_update(): dual_term = shifted - split_term]
    reshape x0 -> x1, local copies, waits for them, and re-layouts: none -> 0.65 us  [on_device(): dual_term.reshape(gaps, share_rows, size_z)]
  transfers between devices with their start and end apart: 2 -> 2, of which waited for: 2 -> 2; matrix products, arithmetic and copies ran while one was open for 10% -> 12% of each run, Pallas kernels for 0% -> 0%
where the time goes in v4:
time: 40.4 us; the launch traced here: 40 us
  waiting for transfers between devices  16.2 us (40%)
  starting transfers between devices  10 us (25%)
  Pallas kernels  6.67 us (17%)
  local copies, waits for them, and re-layouts  3.58 us (9%)
  other arithmetic  2.65 us (7%)
  between operations  0.71 us (2%)
    all_to_all x1, waiting for transfers between devices, on_device(): lax.all_to_all(back, ('src', 'ep'), split_axis=0, concat_axis=0, tiled=True)  9.19 us
    all_to_all x1, starting transfers between devices, on_device(): lax.all_to_all(sent, ('src', 'ep'), split_axis=0, concat_axis=0, tiled=True)  7.3 us
    all_to_all x1, waiting for transfers between devices, on_device(): lax.all_to_all(sent, ('src', 'ep'), split_axis=0, concat_axis=0, tiled=True)  6.97 us
    pallas_call x1, Pallas kernels, stencil_terms(): pl.pallas_call(functools.partial(stencil_kernel, size_y), out_shape=jax.S...  4.83 us
    unnamed x13, local copies, waits for them, and re-layouts  2.86 us
    all_to_all x1, starting transfers between devices, on_device(): lax.all_to_all(back, ('src', 'ep'), split_axis=0, concat_axis=0, tiled=True)  2.71 us
    pallas_call x1, Pallas kernels, solve_epochs(): pl.pallas_call(functools.partial(solve_kernel, src_count), out_shape=(jax...  1.83 us
    another operation x3, other arithmetic, temporal_factor(): return jnp.linalg.cholesky(matrix)  1.4 us
  transfers between devices with their start and end apart: 2, of which 2 were waited for; matrix products, arithmetic and copies ran while one was open for 12% of the time, Pallas kernels for 0%

profile of v4, /device:TPU:0, one launch (start us, length us, event | category | flops | bytes accessed | tf_op | source)
XLA Modules:
  0.0 40.0 jit_solution(5983938072986531965)
XLA Ops:
  0.6 4.8 %shard_map.103 = f32[512,128]{1,0:T(8,128)} custom-call(f32[512,128]{1,0:T(8,128)} %bitcast.31, f32[512,128]{1,0:T(8,128)} %bitcast.32, f32[512,128]{1,0:T(8,128)} %bitcast.33, s32[1,128]{1,0:T(1,128)} %bitcast.40, f32[1,128]{1,0:T(1,128)} %bitcast.41, f32[1]{0:T(128)} %bitcast.5.keep_ref, s32[2]{0:T(128)} %bitcast.42, s32[128]{0:T(128)} %receiver_ref.1), custom_call_target="tpu_custom_call" | custom-call | tf_op jit(solution)/shard_map/pallas_call | solution.py:224
  5.5 7.3 %all-to-all-start = ((f32[32,16,128]{2,1,0:T(8,128)}), f32[32,16,128]{2,1,0:T(8,128)S(1)}, u32[]{:S(2)}, u32[]{:S(2)}) async-start(f32[32,16,128]{2,1,0:T(8,128)} %bitcast.30), calls=%async_computation | async-start | bytes 524288 | tf_op jit(solution)/shard_map/all_to_all | solution.py:324
  12.8 0.0 copy-start.1
  12.8 0.0 copy-start.2
  12.8 0.3 convolution_multiply_fusion
  13.1 0.1 copy.12
  13.2 0.7 %cholesky.20 = f32[8,8]{1,0:T(8,128)S(1)} custom-call(f32[8,8]{1,0:T(8,128)S(1)} %fusion.1), custom_call_target="Cholesky" | custom-call | tf_op jit(solution)/shard_map/jit(cholesky)/cholesky | solution.py:106
  13.9 0.1 select_reduce_fusion
  13.9 0.6 %compare_reduce_fusion = pred[]{:T(512)} fusion(f32[8]{0:T(128)S(1)} %select_reduce_fusion), kind=kLoop, calls=%fused_computation.25 | loop fusion | flops 15 | bytes 33 | tf_op jit(solution)/shard_map/jit(cholesky)/cholesky | solution.py:106
  14.6 1.2 %select_select_fusion.factor_ref = f32[8,8]{1,0:T(8,128)} fusion(f32[8,8]{1,0:T(8,128)S(1)} %cholesky.20, pred[]{:T(512)} %compare_reduce_fusion), kind=kLoop, calls=%fused_computation.11 | loop fusion | flops 192 | bytes 513 | tf_op jit(solution)/shard_map/jit(cholesky)/select_n | solution.py:106
  15.8 0.0 copy-done.1
  15.8 0.0 copy-done.2
  15.8 0.6 %copy_bitcast_fusion.2 = (f32[6,16,128]{2,1,0:T(8,128)}, f32[6,16,128]{2,1,0:T(8,128)}) fusion(f32[1,6,16,128]{3,1,2,0:T(8,128)S(1)} %bitcast.34, f32[1,6,16,128]{3,1,2,0:T(8,128)S(1)} %bitcast.35), kind=kLoop, calls=%fused_computation.3 | loop fusion | bytes 196608 | tf_op jit(solution)/shard_map/reshape | solution.py:330
  16.5 7.0 %all-to-all-done.got_ref = f32[32,16,128]{2,1,0:T(8,128)S(1)} async-done(((f32[32,16,128]{2,1,0:T(8,128)}), f32[32,16,128]{2,1,0:T(8,128)S(1)}, u32[]{:S(2)}, u32[]{:S(2)}) %all-to-all-start) | async-done | bytes 262176 | tf_op jit(solution)/shard_map/all_to_all | solution.py:324
  23.4 0.0 copy-start
  23.4 0.7 %copy-done = f32[32,16,128]{2,1,0:T(8,128)} copy-done((f32[32,16,128]{2,1,0:T(8,128)}, f32[32,16,128]{2,1,0:T(8,128)S(1)}, u32[]{:S(2)}) %copy-start) | copy-done | bytes 262168
  24.1 1.8 %shard_map.104 = (f32[32,16,128]{2,1,0:T(8,128)}, f32[6,16,128]{2,1,0:T(8,128)}, f32[6,16,128]{2,1,0:T(8,128)}) custom-call(f32[32,16,128]{2,1,0:T(8,128)} %copy-done, f32[6,16,128]{2,1,0:T(8,128)} %get-tuple-element.12.split_ref, f32[6,16,128]{2,1,0:T(8,128)} %get-tuple-element.11.dual_ref, f32[8,8]{1,0:T(8,128)} %select_select_fusion.factor_ref), custom_call_target="tpu_custom_call" | custom-call | tf_op jit(solution)/shard_map/pallas_call | solution.py:281
  26.0 0.0 copy-start.4
  26.0 2.7 %all-to-all-start.1 = ((f32[32,16,128]{2,1,0:T(8,128)}), f32[32,16,128]{2,1,0:T(8,128)S(1)}, u32[]{:S(2)}, u32[]{:S(2)}) async-start(f32[32,16,128]{2,1,0:T(8,128)} %get-tuple-element.6), calls=%async_computation.1 | async-start | bytes 524288 | tf_op jit(solution)/shard_map/all_to_all | solution.py:335
  28.7 0.0 copy-done.4
  28.7 0.0 copy-start.3
  28.7 0.6 %copy.23 = f32[1,6,16,128]{3,1,2,0:T(8,128)} copy(f32[1,6,16,128]{3,2,1,0:T(8,128)S(1)} %bitcast.39) | data formatting | bytes 98304
  29.4 0.1 copy-done.3
  29.5 0.6 %copy.22 = f32[1,6,16,128]{3,1,2,0:T(8,128)} copy(f32[1,6,16,128]{3,2,1,0:T(8,128)S(1)} %bitcast.38) | data formatting | bytes 98304
  30.1 9.2 %all-to-all-done.1 = f32[32,16,128]{2,1,0:T(8,128)S(1)} async-done(((f32[32,16,128]{2,1,0:T(8,128)}), f32[32,16,128]{2,1,0:T(8,128)S(1)}, u32[]{:S(2)}, u32[]{:S(2)}) %all-to-all-start.1) | async-done | bytes 262176 | tf_op jit(solution)/shard_map/all_to_all | solution.py:335
  39.3 0.7 %copy.25 = f32[1,16,32,128]{3,2,1,0:T(8,128)} copy(f32[1,16,32,128]{3,2,1,0:T(8,128)S(1)} %bitcast.29) | data formatting | bytes 524288
  (2 shorter events, 0.0 us)
Async XLA Ops:
  5.5 18.0 %all-to-all-start = ((f32[32,16,128]{2,1,0:T(8,128)}), f32[32,16,128]{2,1,0:T(8,128)S(1)}, u32[]{:S(2)}, u32[]{:S(2)}) async-start(f32[32,16,128]{2,1,0:T(8,128)} %bitcast.30), calls=%async_computation | async-start | bytes 524288 | tf_op jit(solution)/shard_map/all_to_all | solution.py:324
  12.8 3.0 %copy-start.1 = (f32[6,2048]{1,0:T(8,128)S(1)}, f32[6,2048]{1,0:T(8,128)}, u32[]{:S(2)}) copy-start(f32[6,2048]{1,0:T(8,128)} %param.15) | copy-start | bytes 147460
  12.8 3.0 %copy-start.2 = (f32[6,2048]{1,0:T(8,128)S(1)}, f32[6,2048]{1,0:T(8,128)}, u32[]{:S(2)}) copy-start(f32[6,2048]{1,0:T(8,128)} %param.14) | copy-start | bytes 147460
  23.4 0.7 %copy-start = (f32[32,16,128]{2,1,0:T(8,128)}, f32[32,16,128]{2,1,0:T(8,128)S(1)}, u32[]{:S(2)}) copy-start(f32[32,16,128]{2,1,0:T(8,128)S(1)} %all-to-all-done.got_ref) | copy-start | bytes 786436
  26.0 2.7 %copy-start.4 = (f32[6,16,128]{2,1,0:T(8,128)S(1)}, f32[6,16,128]{2,1,0:T(8,128)}, u32[]{:S(2)}) copy-start(f32[6,16,128]{2,1,0:T(8,128)} %get-tuple-element.7) | copy-start | bytes 147460
  26.0 13.4 %all-to-all-start.1 = ((f32[32,16,128]{2,1,0:T(8,128)}), f32[32,16,128]{2,1,0:T(8,128)S(1)}, u32[]{:S(2)}, u32[]{:S(2)}) async-start(f32[32,16,128]{2,1,0:T(8,128)} %get-tuple-element.6), calls=%async_computation.1 | async-start | bytes 524288 | tf_op jit(solution)/shard_map/all_to_all | solution.py:335
  28.7 0.8 %copy-start.3 = (f32[6,16,128]{2,1,0:T(8,128)S(1)}, f32[6,16,128]{2,1,0:T(8,128)}, u32[]{:S(2)}) copy-start(f32[6,16,128]{2,1,0:T(8,128)} %get-tuple-element.8) | copy-start | bytes 147460

commit v5 on v3

--- a/solution.py
+++ b/solution.py
@@ -134,7 +134,7 @@
     size_y,
     model_ref, forward_ref, adjoint_ref, receiver_vec_ref, observed_vec_ref,
     keep_ref, source_ref, receiver_ref,
-    out_ref, field_ref, drive_ref, picked_ref,
+    out_ref, drive_ref,
 ):
     rows, lanes = model_ref.shape
     conductivity = jnp.exp(model_ref[...])
@@ -192,22 +192,18 @@
     add_at(source_ref[0], CURRENT)
     add_at(source_ref[1], -CURRENT)
     forward = relax(forward_ref[...], drive_ref[...])
-    field_ref[...] = forward
     receivers = receiver_ref.shape[0]
 
-    def pick_row(index, carry):
-        cell = receiver_ref[index]
-        picked_ref[pl.ds(index, 1), :] = field_ref[pl.ds(cell // lanes, 1), :]
-        return carry
-
-    lax.fori_loop(0, receivers, pick_row, 0, unroll=8)
     cells = receiver_vec_ref[...]
-    picked = picked_ref[...].T
+    placed = (lax.broadcasted_iota(jnp.int32, (rows, receivers), 0) == cells // lanes).astype(jnp.float32)
+    picked = lax.dot_general(
+        forward, placed, (((0,), (0,)), ((), ())),
+        precision=lax.Precision.HIGHEST, preferred_element_type=jnp.float32,
+    )
     hit = lax.broadcasted_iota(jnp.int32, (lanes, receivers), 0) == cells % lanes
     value = jnp.sum(jnp.where(hit, picked, 0.0), axis=0, keepdims=True)
     misfit = value - observed_vec_ref[...]
     weighted = jnp.where(hit, DATA_WEIGHT * misfit, 0.0)
-    placed = (lax.broadcasted_iota(jnp.int32, (rows, receivers), 0) == cells // lanes).astype(jnp.float32)
     drive = lax.dot_general(
         placed, weighted, (((1,), (1,)), ((), ())),
         precision=lax.Precision.HIGHEST, preferred_element_type=jnp.float32,
@@ -226,11 +222,7 @@
         out_shape=jax.ShapeDtypeStruct((rows, lanes), jnp.float32),
         in_specs=[vmem, vmem, vmem, vmem, vmem, smem, smem, smem],
         out_specs=vmem,
-        scratch_shapes=[
-            pltpu.VMEM((rows, lanes), jnp.float32),
-            pltpu.VMEM((rows, lanes), jnp.float32),
-            pltpu.VMEM((receivers, lanes), jnp.float32),
-        ],
+        scratch_shapes=[pltpu.VMEM((rows, lanes), jnp.float32)],
     )(
         model, forward, adjoint, receiver_cells.reshape(1, receivers),
         observed.reshape(1, receivers), keep, source_cells, receiver_cells,

time: 38.9 us -> 38.6 us (level)
  no operation moved by 1% of the time
where the time goes in v5:
time: 38.6 us; the launch traced here: 38.3 us
  waiting for transfers between devices  17.3 us (45%)
  starting transfers between devices  9.88 us (26%)
  Pallas kernels  4.53 us (12%)
  other arithmetic  3.49 us (9%)
  local copies, waits for them, and re-layouts  1.67 us (4%)
  between operations  0.73 us (2%)
  matrix products  0.71 us (2%)
    all_to_all x1, waiting for transfers between devices, on_device(): lax.all_to_all(back, ('src', 'ep'), split_axis=0, concat_axis=0, tiled=True)  9.97 us
    all_to_all x1, waiting for transfers between devices, on_device(): lax.all_to_all(sent, ('src', 'ep'), split_axis=0, concat_axis=0, tiled=True)  7.31 us
    all_to_all x1, starting transfers between devices, on_device(): lax.all_to_all(sent, ('src', 'ep'), split_axis=0, concat_axis=0, tiled=True)  7.3 us
    pallas_call x1, Pallas kernels, stencil_terms(): pl.pallas_call(functools.partial(stencil_kernel, size_y), out_shape=jax.S...  4.53 us
    all_to_all x1, starting transfers between devices, on_device(): lax.all_to_all(back, ('src', 'ep'), split_axis=0, concat_axis=0, tiled=True)  2.59 us
    another operation x3, other arithmetic, temporal_factor(): return jnp.linalg.cholesky(matrix)  1.5 us
    another operation x2, other arithmetic, splitting_update(): updated = jax.scipy.linalg.cho_solve((factor, True), right_side)  1.28 us
  transfers between devices with their start and end apart: 2, of which 2 were waited for; matrix products, arithmetic and copies ran while one was open for 10% of the time, Pallas kernels for 0%

profile of v5, /device:TPU:0, one launch (start us, length us, event | category | flops | bytes accessed | tf_op | source)
XLA Modules:
  0.0 38.3 jit_solution(8860408725367110177)
XLA Ops:
  0.6 4.5 %shard_map.103 = f32[512,128]{1,0:T(8,128)} custom-call(f32[512,128]{1,0:T(8,128)} %bitcast.36, f32[512,128]{1,0:T(8,128)} %bitcast.37, f32[512,128]{1,0:T(8,128)} %bitcast.38, s32[1,128]{1,0:T(1,128)} %bitcast.40, f32[1,128]{1,0:T(1,128)} %bitcast.41, f32[1]{0:T(128)} %bitcast.8.keep_ref, s32[2]{0:T(128)} %bitcast.42, s32[128]{0:T(128)} %receiver_ref.1), custom_call_target="tpu_custom_call" | custom-call | tf_op jit(solution)/shard_map/pallas_call | solution.py:220
  5.2 7.3 %all-to-all-start = ((f32[32,16,128]{2,1,0:T(8,128)}), f32[32,16,128]{2,1,0:T(8,128)S(1)}, u32[]{:S(2)}, u32[]{:S(2)}) async-start(f32[32,16,128]{2,1,0:T(8,128)} %bitcast.34), calls=%async_computation | async-start | bytes 524288 | tf_op jit(solution)/shard_map/all_to_all | solution.py:263
  12.5 0.0 copy-start
  12.5 0.0 copy-start.1
  12.5 0.3 convert_add_fusion
  12.8 0.1 copy.19
  12.9 0.7 %cholesky.17 = f32[8,8]{1,0:T(8,128)S(1)} custom-call(f32[8,8]{1,0:T(8,128)S(1)} %fusion.17), custom_call_target="Cholesky" | custom-call | tf_op jit(solution)/shard_map/jit(cholesky)/cholesky | solution.py:106
  13.6 0.1 copy.20
  13.6 0.2 select_reduce_fusion
  13.8 0.6 %compare_reduce_fusion = pred[]{:T(512)} fusion(f32[8]{0:T(128)S(1)} %select_reduce_fusion), kind=kLoop, calls=%fused_computation.42 | loop fusion | flops 15 | bytes 33 | tf_op jit(solution)/shard_map/jit(cholesky)/cholesky | solution.py:106
  14.4 0.6 %select_select_fusion = f32[8,8]{0,1:T(8,128)S(1)} fusion(f32[8,8]{0,1:T(8,128)S(1)} %copy.20, pred[]{:T(512)} %compare_reduce_fusion), kind=kLoop, calls=%fused_computation.21 | loop fusion | flops 256 | bytes 513 | tf_op jit(solution)/shard_map/jit(_cho_solve)/triangular_solve | solution.py:126
  15.1 0.1 copy.22
  15.2 0.6 %custom-call.10 = f32[1,8,8]{1,2,0:T(8,128)S(1)} custom-call(f32[1,8,8]{2,1,0:T(8,128)S(1)} %bitcast.39), custom_call_target="InvertDiagBlocksLowerTriangular" | custom-call | tf_op jit(solution)/shard_map/jit(_cho_solve)/triangular_solve | solution.py:126
  15.8 0.0 copy-done
  15.8 0.0 copy-done.1
  15.8 7.3 %all-to-all-done = f32[32,16,128]{2,1,0:T(8,128)S(1)} async-done(((f32[32,16,128]{2,1,0:T(8,128)}), f32[32,16,128]{2,1,0:T(8,128)S(1)}, u32[]{:S(2)}, u32[]{:S(2)}) %all-to-all-start) | async-done | bytes 262176 | tf_op jit(solution)/shard_map/all_to_all | solution.py:263
  23.1 0.3 fusion
  23.4 0.2 fusion.14
  23.6 0.7 %broadcast_in_dim.10 = f32[4,8,16,128]{3,2,1,0:T(8,128)} broadcast(f32[8,16,128]{2,1,0:T(8,128)S(1)} %copy.24), dimensions={1,2,3} | broadcast | bytes 327680 | tf_op jit(solution)/shard_map/broadcast_in_dim | solution.py:268
  24.4 2.6 %all-to-all-start.1 = ((f32[32,16,128]{2,1,0:T(8,128)}), f32[32,16,128]{2,1,0:T(8,128)S(1)}, u32[]{:S(2)}, u32[]{:S(2)}) async-start(f32[32,16,128]{2,1,0:T(8,128)} %bitcast.13), calls=%async_computation.1 | async-start | bytes 524288 | tf_op jit(solution)/shard_map/all_to_all | solution.py:272
  26.9 0.7 %fusion.32 = (f32[6,2048]{1,0:T(8,128)}, f32[6,2048]{1,0:T(8,128)}) fusion(f32[6,2048]{1,0:T(8,128)S(1)} %copy-done, f32[8,2048]{1,0:T(8,128)S(1)} %fusion.14), kind=kLoop, calls=%fused_computation.50 | loop fusion | flops 86016 | bytes 294912 | tf_op jit(solution)/shard_map/sub | solution.py:129
  27.6 10.0 %all-to-all-done.1 = f32[32,16,128]{2,1,0:T(8,128)S(1)} async-done(((f32[32,16,128]{2,1,0:T(8,128)}), f32[32,16,128]{2,1,0:T(8,128)S(1)}, u32[]{:S(2)}, u32[]{:S(2)}) %all-to-all-start.1) | async-done | bytes 262176 | tf_op jit(solution)/shard_map/all_to_all | solution.py:272
  37.6 0.7 %copy.32 = f32[1,16,32,128]{3,2,1,0:T(8,128)} copy(f32[1,16,32,128]{3,2,1,0:T(8,128)S(1)} %bitcast.33) | data formatting | bytes 524288
  (5 shorter events, 0.1 us)
Async XLA Ops:
  5.2 18.0 %all-to-all-start = ((f32[32,16,128]{2,1,0:T(8,128)}), f32[32,16,128]{2,1,0:T(8,128)S(1)}, u32[]{:S(2)}, u32[]{:S(2)}) async-start(f32[32,16,128]{2,1,0:T(8,128)} %bitcast.34), calls=%async_computation | async-start | bytes 524288 | tf_op jit(solution)/shard_map/all_to_all | solution.py:263
  12.5 3.3 %copy-start = (f32[6,2048]{1,0:T(8,128)S(1)}, f32[6,2048]{1,0:T(8,128)}, u32[]{:S(2)}) copy-start(f32[6,2048]{1,0:T(8,128)} %param.15) | copy-start | bytes 147460
  12.5 3.3 %copy-start.1 = (f32[6,2048]{1,0:T(8,128)S(1)}, f32[6,2048]{1,0:T(8,128)}, u32[]{:S(2)}) copy-start(f32[6,2048]{1,0:T(8,128)} %param.14) | copy-start | bytes 147460
  24.4 13.2 %all-to-all-start.1 = ((f32[32,16,128]{2,1,0:T(8,128)}), f32[32,16,128]{2,1,0:T(8,128)S(1)}, u32[]{:S(2)}, u32[]{:S(2)}) async-start(f32[32,16,128]{2,1,0:T(8,128)} %bitcast.13), calls=%async_computation.1 | async-start | bytes 524288 | tf_op jit(solution)/shard_map/all_to_all | solution.py:272

commit v6 on v5

--- a/solution.py
+++ b/solution.py
@@ -2,6 +2,7 @@
 
 import jax
 import jax.numpy as jnp
+import numpy as np
 from jax import lax
 from jax.sharding import PartitionSpec as P
 from jax.experimental import pallas as pl
@@ -137,31 +138,48 @@
     out_ref, drive_ref,
 ):
     rows, lanes = model_ref.shape
-    conductivity = jnp.exp(model_ref[...])
-    row_id = lax.broadcasted_iota(jnp.int32, (rows, lanes), 0)
-    lane_id = lax.broadcasted_iota(jnp.int32, (rows, lanes), 1)
+    size_x = rows // size_y
+    inner = 8
+    parts = size_y // inner
+    slab_rows = rows // parts
+    shape = (parts, size_x, inner, lanes)
+
+    def load(ref):
+        slabs = [ref[pl.ds(part, slab_rows, stride=parts), :] for part in range(parts)]
+        return jnp.stack(slabs).reshape(shape)
+
+    def store(ref, v):
+        for part in range(parts):
+            ref[pl.ds(part, slab_rows, stride=parts), :] = v[part].reshape(slab_rows, lanes)
+
     def next_z(v):
-        return pltpu.roll(v, lanes - 1, 1)
+        return pltpu.roll(v, lanes - 1, 3)
 
     def prev_z(v):
-        return pltpu.roll(v, 1, 1)
+        return pltpu.roll(v, 1, 3)
 
     def next_y(v):
-        return pltpu.roll(v, rows - 1, 0)
+        return jnp.concatenate([v[1:], pltpu.roll(v[:1], inner - 1, 2)], axis=0)
 
     def prev_y(v):
-        return pltpu.roll(v, 1, 0)
+        return jnp.concatenate([pltpu.roll(v[parts - 1:], 1, 2), v[:-1]], axis=0)
 
     def next_x(v):
-        return jnp.concatenate([v[size_y:], v[:size_y]], axis=0)
+        return jnp.concatenate([v[:, 1:], v[:, :1]], axis=1)
 
     def prev_x(v):
-        return jnp.concatenate([v[rows - size_y:], v[: rows - size_y]], axis=0)
-
+        return jnp.concatenate([v[:, size_x - 1:], v[:, : size_x - 1]], axis=1)
+
+    model = load(model_ref)
+    conductivity = jnp.exp(model)
+    part_id = lax.broadcasted_iota(jnp.int32, shape, 0)
+    x_id = lax.broadcasted_iota(jnp.int32, shape, 1)
+    y_id = lax.broadcasted_iota(jnp.int32, shape, 2) * parts + part_id
+    z_id = lax.broadcasted_iota(jnp.int32, shape, 3)
     zero = jnp.zeros_like(conductivity)
-    weight_x = jnp.where(row_id < rows - size_y, 0.5 * (conductivity + next_x(conductivity)), zero)
-    weight_y = jnp.where(row_id % size_y < size_y - 1, 0.5 * (conductivity + next_y(conductivity)), zero)
-    weight_z = jnp.where(lane_id < lanes - 1, 0.5 * (conductivity + next_z(conductivity)), zero)
+    weight_x = jnp.where(x_id < size_x - 1, 0.5 * (conductivity + next_x(conductivity)), zero)
+    weight_y = jnp.where(y_id < size_y - 1, 0.5 * (conductivity + next_y(conductivity)), zero)
+    weight_z = jnp.where(z_id < lanes - 1, 0.5 * (conductivity + next_z(conductivity)), zero)
     mass = MASS_TERM * conductivity
     diagonal = mass + weight_x + prev_x(weight_x)
     diagonal = diagonal + weight_y + prev_y(weight_y)
@@ -186,18 +204,22 @@
 
     def add_at(cell, amount):
         row = cell // lanes
-        drive_ref[pl.ds(row, 1), :] += jnp.where(one_row == cell % lanes, amount, 0.0)
-
-    drive_ref[...] = zero
+        y = row % size_y
+        slot = ((y % parts) * size_x + row // size_y) * inner + y // parts
+        drive_ref[pl.ds(slot, 1), :] += jnp.where(one_row == cell % lanes, amount, 0.0)
+
+    drive_ref[...] = jnp.zeros((rows, lanes), jnp.float32)
     add_at(source_ref[0], CURRENT)
     add_at(source_ref[1], -CURRENT)
-    forward = relax(forward_ref[...], drive_ref[...])
+    forward = relax(load(forward_ref), drive_ref[...].reshape(shape))
     receivers = receiver_ref.shape[0]
 
     cells = receiver_vec_ref[...]
-    placed = (lax.broadcasted_iota(jnp.int32, (rows, receivers), 0) == cells // lanes).astype(jnp.float32)
+    slot_id = lax.broadcasted_iota(jnp.int32, (rows, receivers), 0)
+    slot_row = ((slot_id // inner) % size_x) * size_y + (slot_id % inner) * parts + slot_id // (size_x * inner)
+    placed = (slot_row == cells // lanes).astype(jnp.float32)
     picked = lax.dot_general(
-        forward, placed, (((0,), (0,)), ((), ())),
+        forward.reshape(rows, lanes), placed, (((0,), (0,)), ((), ())),
         precision=lax.Precision.HIGHEST, preferred_element_type=jnp.float32,
     )
     hit = lax.broadcasted_iota(jnp.int32, (lanes, receivers), 0) == cells % lanes
@@ -208,8 +230,8 @@
         placed, weighted, (((1,), (1,)), ((), ())),
         precision=lax.Precision.HIGHEST, preferred_element_type=jnp.float32,
     )
-    adjoint = relax(adjoint_ref[...], drive)
-    out_ref[...] = keep_ref[0] * model_ref[...] - STEP_SIZE * (conductivity * (forward * adjoint))
+    adjoint = relax(load(adjoint_ref), drive.reshape(shape))
+    store(out_ref, keep_ref[0] * model - STEP_SIZE * (conductivity * (forward * adjoint)))
 
 
 def stencil_terms(size_y, model, forward, adjoint, keep, source_cells, receiver_cells, observed):
@@ -227,6 +249,14 @@
         model, forward, adjoint, receiver_cells.reshape(1, receivers),
         observed.reshape(1, receivers), keep, source_cells, receiver_cells,
     )
+
+
+def temporal_operators(epochs, src_count):
+    second = np.eye(epochs - 2, epochs) - 2.0 * np.eye(epochs - 2, epochs, k=1) + np.eye(epochs - 2, epochs, k=2)
+    inverse = np.linalg.inv(np.eye(epochs) + PENALTY * second.T @ second)
+    solve = np.tile(inverse, (src_count, src_count))
+    coupling = np.tile(PENALTY * inverse @ second.T, (src_count, 1))
+    return jnp.asarray(solve, jnp.float32), jnp.asarray(coupling, jnp.float32)
 
 
 def on_device(
@@ -247,7 +277,6 @@
     share_cells = cell_count // devices
     share_rows = share_cells // size_z
     total_epochs = slab_epochs * ep_count
-    factor = temporal_factor(total_epochs)
     keep = jnp.where(lax.axis_index("src") == 0, 1.0, 0.0).astype(jnp.float32).reshape(1)
     partial_rhs = stencil_terms(
         size_y,
@@ -261,14 +290,15 @@
     )
     sent = partial_rhs.reshape(devices, share_rows, size_z)
     got = lax.all_to_all(sent, ("src", "ep"), split_axis=0, concat_axis=0, tiled=True)
-    time_rhs = got.reshape(src_count, total_epochs, share_rows, size_z).sum(axis=0)
-    updated, split_term, dual_term = splitting_update(
-        time_rhs.reshape(total_epochs, share_cells), split_term, dual_term, factor
-    )
-    back = jnp.broadcast_to(
-        updated.reshape(1, total_epochs, share_rows, size_z),
-        (src_count, total_epochs, share_rows, size_z),
-    ).reshape(devices, share_rows, size_z)
+    solve, coupling = temporal_operators(total_epochs, src_count)
+    gaps = split_term.shape[0]
+    gap = (split_term - dual_term).reshape(gaps, share_rows, size_z)
+    fixed_part = jnp.einsum("pk,krz->prz", coupling, gap, precision=lax.Precision.HIGHEST)
+    back = jnp.einsum("pq,qrz->prz", solve, got, precision=lax.Precision.HIGHEST) + fixed_part
+    updated = back[:total_epochs].reshape(total_epochs, share_cells)
+    shifted = difference(updated) + dual_term
+    split_term = shifted - jnp.clip(shifted, -THRESHOLD, THRESHOLD)
+    dual_term = shifted - split_term
     model_rows = lax.all_to_all(back, ("src", "ep"), split_axis=0, concat_axis=0, tiled=True)
     model_log = model_rows.reshape(slab_epochs, size_x, size_y, size_z)
     return (model_log, split_term, dual_term)

time: 38.6 us -> 38.5 us (level)
  waiting for transfers between devices: 17.3 us -> 20.2 us
  other arithmetic: 3.49 us -> 0.68 us
    all_to_all x1, waiting for transfers between devices: 7.31 us -> 10.2 us  [on_device(): lax.all_to_all(sent, ('src', 'ep'), split_axis=0, concat_axis=0, tiled=True)]
    another operation x5 -> x0, other arithmetic: 2.77 us -> none  [the longest x3 1.5 us: temporal_factor(): return jnp.linalg.cholesky(matrix)]
    add x1, local copies, waits for them, and re-layouts: 0.07 us -> 0.86 us  [on_device(): jnp.einsum('pq,qrz->prz', solve, got, precision=lax.Precision.HIGHEST)]
    broadcast_in_dim x2 -> x0, local copies, waits for them, and re-layouts: 0.74 us -> none  [on_device(): jnp.broadcast_to(updated.reshape(1, total_epochs, share_rows, size_z), (s...]
    dot_general x1 -> x2, matrix products: 0.26 us -> 0.85 us  [the longest x1 0.45 us: on_device(): jnp.einsum('pq,qrz->prz', solve, got, precision=lax.Precision.HIGHEST)]
    another operation x2 -> x0, matrix products: 0.44 us -> none  [splitting_update(): updated = jax.scipy.linalg.cho_solve((factor, True), right_side)]
  transfers between devices with their start and end apart: 2 -> 2, of which waited for: 2 -> 2; matrix products, arithmetic and copies ran while one was open for 10% -> 3% of each run, Pallas kernels for 0% -> 0%
where the time goes in v6:
time: 38.5 us; the launch traced here: 38.2 us
  waiting for transfers between devices  20.2 us (52%)
  starting transfers between devices  9.89 us (26%)
  Pallas kernels  4.3 us (11%)
  local copies, waits for them, and re-layouts  1.58 us (4%)
  matrix products  0.85 us (2%)
  between operations  0.71 us (2%)
  other arithmetic  0.68 us (2%)
    all_to_all x1, waiting for transfers between devices, on_device(): lax.all_to_all(sent, ('src', 'ep'), split_axis=0, concat_axis=0, tiled=True)  10.2 us
    all_to_all x1, waiting for transfers between devices, on_device(): lax.all_to_all(back, ('src', 'ep'), split_axis=0, concat_axis=0, tiled=True)  9.97 us
    all_to_all x1, starting transfers between devices, on_device(): lax.all_to_all(sent, ('src', 'ep'), split_axis=0, concat_axis=0, tiled=True)  7.3 us
    pallas_call x1, Pallas kernels, stencil_terms(): pl.pallas_call(functools.partial(stencil_kernel, size_y), out_shape=jax.S...  4.3 us
    all_to_all x1, starting transfers between devices, on_device(): lax.all_to_all(back, ('src', 'ep'), split_axis=0, concat_axis=0, tiled=True)  2.59 us
    add x1, local copies, waits for them, and re-layouts, on_device(): jnp.einsum('pq,qrz->prz', solve, got, precision=lax.Precision.HIGHEST)  0.86 us
  transfers between devices with their start and end apart: 2, of which 2 were waited for; matrix products, arithmetic and copies ran while one was open for 3% of the time, Pallas kernels for 0%

profile of v6, /device:TPU:0, one launch (start us, length us, event | category | flops | bytes accessed | tf_op | source)
XLA Modules:
  0.0 38.2 jit_solution(2285123472012441206)
XLA Ops:
  0.6 4.3 %shard_map.121 = f32[512,128]{1,0:T(8,128)} custom-call(f32[512,128]{1,0:T(8,128)} %bitcast.24, f32[512,128]{1,0:T(8,128)} %bitcast.25, f32[512,128]{1,0:T(8,128)} %bitcast.26, s32[1,128]{1,0:T(1,128)} %bitcast.27, f32[1,128]{1,0:T(1,128)} %bitcast.28, f32[1]{0:T(128)} %bitcast.5.keep_ref, s32[2]{0:T(128)} %bitcast.29, s32[128]{0:T(128)} %receiver_ref.1), custom_call_target="tpu_custom_call" | custom-call | tf_op jit(solution)/shard_map/pallas_call | solution.py:242
  4.9 0.0 copy-start
  4.9 0.0 copy-start.1
  4.9 0.0 copy-start.3
  4.9 7.3 %all-to-all-start = ((f32[32,16,128]{2,1,0:T(8,128)}), f32[32,16,128]{2,1,0:T(8,128)S(1)}, u32[]{:S(2)}, u32[]{:S(2)}) async-start(f32[32,16,128]{2,1,0:T(8,128)} %bitcast.23), calls=%async_computation | async-start | bytes 524288 | tf_op jit(solution)/shard_map/all_to_all | solution.py:292
  12.3 0.0 copy-done
  12.3 0.0 copy-done.1
  12.3 0.0 copy-done.3
  12.3 0.0 copy-start.2
  12.3 0.4 %fusion.5 = f32[16,128,32]{1,2,0:T(8,128)S(1)} fusion(f32[32,6,1]{0,1,2:T(8,128)S(1)} %copy-done.3, f32[6,2048]{1,0:T(8,128)S(1)} %copy-done.1, f32[6,2048]{1,0:T(8,128)S(1)} %copy-done), kind=kOutput, calls=%fused_computation.9 | convolution fusion | flops 4730880 | bytes 361216 | tf_op jit(solution)/shard_map/pk,krz->prz/dot_general | solution.py:296
  12.7 10.2 %all-to-all-done = f32[32,16,128]{2,1,0:T(8,128)S(1)} async-done(((f32[32,16,128]{2,1,0:T(8,128)}), f32[32,16,128]{2,1,0:T(8,128)S(1)}, u32[]{:S(2)}, u32[]{:S(2)}) %all-to-all-start) | async-done | bytes 262176 | tf_op jit(solution)/shard_map/all_to_all | solution.py:292
  22.9 0.0 copy-done.2
  22.9 0.5 %fusion = f32[32,16,128]{2,0,1:T(8,128)S(1)} fusion(f32[16,128,32]{1,2,0:T(8,128)S(1)} %fusion.5, f32[32,32,1]{1,0,2:T(8,128)S(1)} %copy-done.2, f32[32,16,128]{2,1,0:T(8,128)S(1)} %all-to-all-done), kind=kOutput, calls=%fused_computation.1 | convolution fusion | flops 25231360 | bytes 790528 | tf_op jit(solution)/shard_map/pq,qrz->prz/dot_general | solution.py:297
  23.4 0.9 %copy.20 = f32[32,16,128]{2,1,0:T(8,128)} copy(f32[32,16,128]{2,0,1:T(8,128)S(1)} %fusion) | data formatting | bytes 524288 | tf_op jit(solution)/shard_map/add | solution.py:297
  24.2 2.6 %all-to-all-start.1 = ((f32[32,16,128]{2,1,0:T(8,128)}), f32[32,16,128]{2,1,0:T(8,128)S(1)}, u32[]{:S(2)}, u32[]{:S(2)}) async-start(f32[32,16,128]{2,1,0:T(8,128)} %copy.20), calls=%async_computation.1 | async-start | bytes 524288 | tf_op jit(solution)/shard_map/all_to_all | solution.py:302
  26.8 0.7 %fusion.8 = (f32[6,2048]{1,0:T(8,128)}, f32[6,2048]{1,0:T(8,128)}) fusion(f32[6,2048]{1,0:T(8,128)S(1)} %copy-done, f32[32,16,128]{2,0,1:T(8,128)S(1)} %fusion), kind=kLoop, calls=%fused_computation.12 | loop fusion | flops 86016 | bytes 294912 | tf_op jit(solution)/shard_map/sub | solution.py:301
  27.5 10.0 %all-to-all-done.1 = f32[32,16,128]{2,1,0:T(8,128)S(1)} async-done(((f32[32,16,128]{2,1,0:T(8,128)}), f32[32,16,128]{2,1,0:T(8,128)S(1)}, u32[]{:S(2)}, u32[]{:S(2)}) %all-to-all-start.1) | async-done | bytes 262176 | tf_op jit(solution)/shard_map/all_to_all | solution.py:302
  37.5 0.7 %copy.24 = f32[1,16,32,128]{3,2,1,0:T(8,128)} copy(f32[1,16,32,128]{3,2,1,0:T(8,128)S(1)} %bitcast.22) | data formatting | bytes 524288
Async XLA Ops:
  4.9 7.3 %copy-start = (f32[6,2048]{1,0:T(8,128)S(1)}, f32[6,2048]{1,0:T(8,128)}, u32[]{:S(2)}) copy-start(f32[6,2048]{1,0:T(8,128)} %param.17) | copy-start | bytes 147460
  4.9 7.3 %copy-start.1 = (f32[6,2048]{1,0:T(8,128)S(1)}, f32[6,2048]{1,0:T(8,128)}, u32[]{:S(2)}) copy-start(f32[6,2048]{1,0:T(8,128)} %param.16) | copy-start | bytes 147460
  4.9 7.3 %copy-start.3 = (f32[32,6,1]{0,1,2:T(8,128)S(1)}, f32[32,6,1]{0,1,2:T(8,128)}, u32[]{:S(2)}) copy-start(f32[32,6,1]{0,1,2:T(8,128)} %constant.29) | copy-start | bytes 2308
  4.9 18.0 %all-to-all-start = ((f32[32,16,128]{2,1,0:T(8,128)}), f32[32,16,128]{2,1,0:T(8,128)S(1)}, u32[]{:S(2)}, u32[]{:S(2)}) async-start(f32[32,16,128]{2,1,0:T(8,128)} %bitcast.23), calls=%async_computation | async-start | bytes 524288 | tf_op jit(solution)/shard_map/all_to_all | solution.py:292
  12.3 10.6 %copy-start.2 = (f32[32,32,1]{1,0,2:T(8,128)S(1)}, f32[32,32,1]{1,0,2:T(8,128)}, u32[]{:S(2)}) copy-start(f32[32,32,1]{1,0,2:T(8,128)} %constant.28) | copy-start | bytes 12292
  24.2 13.2 %all-to-all-start.1 = ((f32[32,16,128]{2,1,0:T(8,128)}), f32[32,16,128]{2,1,0:T(8,128)S(1)}, u32[]{:S(2)}, u32[]{:S(2)}) async-start(f32[32,16,128]{2,1,0:T(8,128)} %copy.20), calls=%async_computation.1 | async-start | bytes 524288 | tf_op jit(solution)/shard_map/all_to_all | solution.py:302

commit v7 on v6

--- a/solution.py
+++ b/solution.py
@@ -251,12 +251,11 @@
     )
 
 
-def temporal_operators(epochs, src_count):
+def temporal_operators(epochs):
     second = np.eye(epochs - 2, epochs) - 2.0 * np.eye(epochs - 2, epochs, k=1) + np.eye(epochs - 2, epochs, k=2)
     inverse = np.linalg.inv(np.eye(epochs) + PENALTY * second.T @ second)
-    solve = np.tile(inverse, (src_count, src_count))
-    coupling = np.tile(PENALTY * inverse @ second.T, (src_count, 1))
-    return jnp.asarray(solve, jnp.float32), jnp.asarray(coupling, jnp.float32)
+    coupling = PENALTY * inverse @ second.T
+    return inverse, jnp.asarray(coupling, jnp.float32)
 
 
 def on_device(
@@ -290,11 +289,17 @@
     )
     sent = partial_rhs.reshape(devices, share_rows, size_z)
     got = lax.all_to_all(sent, ("src", "ep"), split_axis=0, concat_axis=0, tiled=True)
-    solve, coupling = temporal_operators(total_epochs, src_count)
+    inverse, coupling = temporal_operators(total_epochs)
     gaps = split_term.shape[0]
     gap = (split_term - dual_term).reshape(gaps, share_rows, size_z)
     fixed_part = jnp.einsum("pk,krz->prz", coupling, gap, precision=lax.Precision.HIGHEST)
-    back = jnp.einsum("pq,qrz->prz", solve, got, precision=lax.Precision.HIGHEST) + fixed_part
+    summed = got[:total_epochs]
+    for s in range(1, src_count):
+        summed = summed + got[s * total_epochs : (s + 1) * total_epochs]
+    weights = jnp.asarray(np.tile(inverse, (src_count, 1)), jnp.float32)
+    back = jnp.tile(fixed_part, (src_count, 1, 1))
+    for k in range(total_epochs):
+        back = back + weights[:, k, None, None] * summed[k][None]
     updated = back[:total_epochs].reshape(total_epochs, share_cells)
     shifted = difference(updated) + dual_term
     split_term = shifted - jnp.clip(shifted, -THRESHOLD, THRESHOLD)

time: 38.5 us -> 39 us (1.013)
  other arithmetic: 0.68 us -> 2.66 us
  waiting for transfers between devices: 20.2 us -> 19.4 us
  matrix products: 0.85 us -> 0.19 us
    add x0 -> x2, other arithmetic: none -> 1.06 us  [the longest x1 1.04 us: on_device(): back = back + weights[:, k, None, None] * summed[k][None]]
    all_to_all x1, waiting for transfers between devices: 9.97 us -> 9.04 us  [on_device(): lax.all_to_all(back, ('src', 'ep'), split_axis=0, concat_axis=0, tiled=True)]
    unnamed x0 -> x1, other arithmetic: none -> 0.93 us
    add x1 -> x0, local copies, waits for them, and re-layouts: 0.86 us -> none  [on_device(): jnp.einsum('pq,qrz->prz', solve, got, precision=lax.Precision.HIGHEST)]
    unnamed x9 -> x23, local copies, waits for them, and re-layouts: 0.72 us -> 1.4 us
    dot_general x1 -> x0, matrix products: 0.45 us -> none  [on_device(): jnp.einsum('pq,qrz->prz', solve, got, precision=lax.Precision.HIGHEST)]
  transfers between devices with their start and end apart: 2 -> 2, of which waited for: 2 -> 2; matrix products, arithmetic and copies ran while one was open for 3% -> 5% of each run, Pallas kernels for 0% -> 0%
where the time goes in v7:
time: 39 us; the launch traced here: 38.7 us
  waiting for transfers between devices  19.4 us (50%)
  starting transfers between devices  9.89 us (25%)
  Pallas kernels  4.3 us (11%)
  other arithmetic  2.66 us (7%)
  local copies, waits for them, and re-layouts  1.42 us (4%)
  between operations  0.78 us (2%)
    all_to_all x1, waiting for transfers between devices, on_device(): lax.all_to_all(sent, ('src', 'ep'), split_axis=0, concat_axis=0, tiled=True)  10.4 us
    all_to_all x1, waiting for transfers between devices, on_device(): lax.all_to_all(back, ('src', 'ep'), split_axis=0, concat_axis=0, tiled=True)  9.04 us
    all_to_all x1, starting transfers between devices, on_device(): lax.all_to_all(sent, ('src', 'ep'), split_axis=0, concat_axis=0, tiled=True)  7.3 us
    pallas_call x1, Pallas kernels, stencil_terms(): pl.pallas_call(functools.partial(stencil_kernel, size_y), out_shape=jax.S...  4.3 us
    all_to_all x1, starting transfers between devices, on_device(): lax.all_to_all(back, ('src', 'ep'), split_axis=0, concat_axis=0, tiled=True)  2.59 us
    unnamed x23, local copies, waits for them, and re-layouts  1.4 us
    add x1, other arithmetic, on_device(): back = back + weights[:, k, None, None] * summed[k][None]  1.04 us
    unnamed x1, other arithmetic  0.93 us
  transfers between devices with their start and end apart: 2, of which 2 were waited for; matrix products, arithmetic and copies ran while one was open for 5% of the time, Pallas kernels for 0%

profile of v7, /device:TPU:0, one launch (start us, length us, event | category | flops | bytes accessed | tf_op | source)
XLA Modules:
  0.0 38.7 jit_solution(12000554424349482503)
XLA Ops:
  0.6 4.3 %shard_map.121 = f32[512,128]{1,0:T(8,128)} custom-call(f32[512,128]{1,0:T(8,128)} %bitcast.57, f32[512,128]{1,0:T(8,128)} %bitcast.58, f32[512,128]{1,0:T(8,128)} %bitcast.59, s32[1,128]{1,0:T(1,128)} %bitcast.60, f32[1,128]{1,0:T(1,128)} %bitcast.61, f32[1]{0:T(128)} %bitcast.8.keep_ref, s32[2]{0:T(128)} %bitcast.62, s32[128]{0:T(128)} %receiver_ref.1), custom_call_target="tpu_custom_call" | custom-call | tf_op jit(solution)/shard_map/pallas_call | solution.py:242
  4.9 0.0 copy-start
  4.9 0.0 copy-start.1
  4.9 0.0 copy-start.2
  4.9 7.3 %all-to-all-start = ((f32[32,16,128]{2,1,0:T(8,128)}), f32[32,16,128]{2,1,0:T(8,128)S(1)}, u32[]{:S(2)}, u32[]{:S(2)}) async-start(f32[32,16,128]{2,1,0:T(8,128)} %bitcast.56), calls=%async_computation | async-start | bytes 524288 | tf_op jit(solution)/shard_map/all_to_all | solution.py:291
  12.3 0.0 copy-done
  12.3 0.0 copy-done.1
  12.3 0.0 copy-done.2
  12.3 0.2 fusion.7
  12.5 10.4 %all-to-all-done = f32[32,16,128]{2,1,0:T(8,128)S(1)} async-done(((f32[32,16,128]{2,1,0:T(8,128)}), f32[32,16,128]{2,1,0:T(8,128)S(1)}, u32[]{:S(2)}, u32[]{:S(2)}) %all-to-all-start) | async-done | bytes 262176 | tf_op jit(solution)/shard_map/all_to_all | solution.py:291
  22.9 0.0 copy-start.6
  22.9 0.0 copy-start.7
  23.0 0.0 copy-start.8
  23.0 0.0 copy-start.9
  23.0 0.0 copy-start.10
  23.0 0.0 copy-start.3
  23.0 0.0 copy-start.4
  23.0 0.0 copy-start.5
  23.0 0.5 %copy-done.6 = f32[32]{0:T(128)S(1)} copy-done((f32[32]{0:T(128)S(1)}, f32[32]{0:T(128)}, u32[]{:S(2)}) %copy-start.6) | copy-done | bytes 152
  23.6 0.0 copy-done.7
  23.6 0.0 copy-done.8
  23.6 0.0 copy-done.9
  23.6 0.0 copy-done.10
  23.6 0.0 copy-done.3
  23.7 0.0 copy-done.4
  23.7 0.0 copy-done.5
  23.7 1.0 %fusion.6 = f32[32,16,128]{2,1,0:T(8,128)} fusion(f32[16,128]{1,0:T(8,128)S(1)} %get-tuple-element.6, f32[32]{0:T(128)S(1)} %copy-done.10, f32[16,128]{1,0:T(8,128)S(1)} %get-tuple-element.7, f32[32]{0:T(128)S(1)} %copy-done.9, f32[16,128]{1,0:T(8,128)S(1)} %get-tuple-element.8, f32[32]{0:T(128)S(1)} %copy-done.8, f32[16,128]{1,0:T(8,128)S(1)} %get-tuple-element.9, ...), kind=kLoop, calls=%fused_computation.7 | loop fusion | flops 1048576 | bytes 394240 | tf_op jit(solution)/shard_map/add | solution.py:302
  24.7 2.6 %all-to-all-start.1 = ((f32[32,16,128]{2,1,0:T(8,128)}), f32[32,16,128]{2,1,0:T(8,128)S(1)}, u32[]{:S(2)}, u32[]{:S(2)}) async-start(f32[32,16,128]{2,1,0:T(8,128)} %fusion.6), calls=%async_computation.1 | async-start | bytes 524288 | tf_op jit(solution)/shard_map/all_to_all | solution.py:307
  27.3 0.9 %fusion.10 = f32[1,6,16,128]{3,2,1,0:T(8,128)S(1)} fusion(f32[32,16,128]{2,1,0:T(8,128)} %fusion.6), kind=kLoop, calls=%fused_computation.17 | loop fusion | flops 36864 | bytes 196608
  28.3 0.7 %fusion.12 = (f32[6,2048]{1,0:T(8,128)}, f32[6,2048]{1,0:T(8,128)}) fusion(f32[6,2048]{1,0:T(8,128)S(1)} %copy-done, f32[1,6,16,128]{3,2,1,0:T(8,128)S(1)} %fusion.10), kind=kLoop, calls=%fused_computation.20 | loop fusion | flops 49152 | bytes 196608 | tf_op jit(solution)/shard_map/sub | solution.py:306
  28.9 9.0 %all-to-all-done.1 = f32[32,16,128]{2,1,0:T(8,128)S(1)} async-done(((f32[32,16,128]{2,1,0:T(8,128)}), f32[32,16,128]{2,1,0:T(8,128)S(1)}, u32[]{:S(2)}, u32[]{:S(2)}) %all-to-all-start.1) | async-done | bytes 262176 | tf_op jit(solution)/shard_map/all_to_all | solution.py:307
  38.0 0.7 %copy.23 = f32[1,16,32,128]{3,2,1,0:T(8,128)} copy(f32[1,16,32,128]{3,2,1,0:T(8,128)S(1)} %bitcast.55) | data formatting | bytes 524288
  (3 shorter events, 0.0 us)
Async XLA Ops:
  4.9 7.3 %copy-start = (f32[6,2048]{1,0:T(8,128)S(1)}, f32[6,2048]{1,0:T(8,128)}, u32[]{:S(2)}) copy-start(f32[6,2048]{1,0:T(8,128)} %param.17) | copy-start | bytes 147460
  4.9 7.3 %copy-start.1 = (f32[6,2048]{1,0:T(8,128)S(1)}, f32[6,2048]{1,0:T(8,128)}, u32[]{:S(2)}) copy-start(f32[6,2048]{1,0:T(8,128)} %param.16) | copy-start | bytes 147460
  4.9 7.3 %copy-start.2 = (f32[8,6,1]{1,0,2:T(8,128)S(1)}, f32[8,6,1]{1,0,2:T(8,128)}, u32[]{:S(2)}) copy-start(f32[8,6,1]{1,0,2:T(8,128)} %constant.44) | copy-start | bytes 580
  4.9 18.0 %all-to-all-start = ((f32[32,16,128]{2,1,0:T(8,128)}), f32[32,16,128]{2,1,0:T(8,128)S(1)}, u32[]{:S(2)}, u32[]{:S(2)}) async-start(f32[32,16,128]{2,1,0:T(8,128)} %bitcast.56), calls=%async_computation | async-start | bytes 524288 | tf_op jit(solution)/shard_map/all_to_all | solution.py:291
  22.9 0.7 %copy-start.6 = (f32[32]{0:T(128)S(1)}, f32[32]{0:T(128)}, u32[]{:S(2)}) copy-start(f32[32]{0:T(128)} %constant.35) | copy-start | bytes 388
  22.9 0.7 %copy-start.7 = (f32[32]{0:T(128)S(1)}, f32[32]{0:T(128)}, u32[]{:S(2)}) copy-start(f32[32]{0:T(128)} %constant.37) | copy-start | bytes 388
  23.0 0.7 %copy-start.8 = (f32[32]{0:T(128)S(1)}, f32[32]{0:T(128)}, u32[]{:S(2)}) copy-start(f32[32]{0:T(128)} %constant.39) | copy-start | bytes 388
  23.0 0.7 %copy-start.9 = (f32[32]{0:T(128)S(1)}, f32[32]{0:T(128)}, u32[]{:S(2)}) copy-start(f32[32]{0:T(128)} %constant.41) | copy-start | bytes 388
  23.0 0.7 %copy-start.10 = (f32[32]{0:T(128)S(1)}, f32[32]{0:T(128)}, u32[]{:S(2)}) copy-start(f32[32]{0:T(128)} %constant.43) | copy-start | bytes 388
  23.0 0.7 %copy-start.3 = (f32[32]{0:T(128)S(1)}, f32[32]{0:T(128)}, u32[]{:S(2)}) copy-start(f32[32]{0:T(128)} %constant.29) | copy-start | bytes 388
  23.0 0.7 %copy-start.4 = (f32[32]{0:T(128)S(1)}, f32[32]{0:T(128)}, u32[]{:S(2)}) copy-start(f32[32]{0:T(128)} %constant.31) | copy-start | bytes 388
  23.0 0.7 %copy-start.5 = (f32[32]{0:T(128)S(1)}, f32[32]{0:T(128)}, u32[]{:S(2)}) copy-start(f32[32]{0:T(128)} %constant.33) | copy-start | bytes 388
  24.7 13.2 %all-to-all-start.1 = ((f32[32,16,128]{2,1,0:T(8,128)}), f32[32,16,128]{2,1,0:T(8,128)S(1)}, u32[]{:S(2)}, u32[]{:S(2)}) async-start(f32[32,16,128]{2,1,0:T(8,128)} %fusion.6), calls=%async_computation.1 | async-start | bytes 524288 | tf_op jit(solution)/shard_map/all_to_all | solution.py:307

commit v8 on v6

--- a/solution.py
+++ b/solution.py
@@ -299,7 +299,18 @@
     shifted = difference(updated) + dual_term
     split_term = shifted - jnp.clip(shifted, -THRESHOLD, THRESHOLD)
     dual_term = shifted - split_term
-    model_rows = lax.all_to_all(back, ("src", "ep"), split_axis=0, concat_axis=0, tiled=True)
+    half = share_rows // 2
+    if share_rows % 2 == 0 and src_count % 2 == 0:
+        core = lax.axis_index("src") % 2
+        own_rows = back[:total_epochs].reshape(total_epochs, 2, half, size_z).transpose(1, 0, 2, 3)
+        halves = jnp.broadcast_to(own_rows[None], (src_count // 2,) + own_rows.shape).reshape(devices, half, size_z)
+        mine = lax.all_to_all(halves, ("src", "ep"), split_axis=0, concat_axis=0, tiled=True)
+        theirs = lax.ppermute(mine, "src", [(i, i ^ 1) for i in range(src_count)])
+        model_rows = jnp.where(
+            core == 0, jnp.concatenate([mine, theirs], axis=1), jnp.concatenate([theirs, mine], axis=1)
+        )
+    else:
+        model_rows = lax.all_to_all(back, ("src", "ep"), split_axis=0, concat_axis=0, tiled=True)
     model_log = model_rows.reshape(slab_epochs, size_x, size_y, size_z)
     return (model_log, split_term, dual_term)
 

time: 38.5 us -> 36.7 us (0.953)
  waiting for transfers between devices: 20.2 us -> 18.5 us
  local copies, waits for them, and re-layouts: 1.58 us -> 0.71 us
  other arithmetic: 0.68 us -> 1.4 us
    all_to_all x1, waiting for transfers between devices: 9.97 us -> 7.73 us  [on_device(): lax.all_to_all(halves, ('src', 'ep'), split_axis=0, concat_axis=0, tiled=...]
    add x1 -> x0, local copies, waits for them, and re-layouts: 0.86 us -> none  [on_device(): jnp.einsum('pq,qrz->prz', solve, got, precision=lax.Precision.HIGHEST)]
    select_n x0 -> x1, other arithmetic: none -> 0.72 us  [on_device(): jnp.where(core == 0, jnp.concatenate([mine, theirs], axis=1), jnp.concate...]
    unnamed x9 -> x8, local copies, waits for them, and re-layouts: 0.72 us -> 0.02 us
    broadcast_in_dim x0 -> x1, local copies, waits for them, and re-layouts: none -> 0.66 us  [on_device(): jnp.broadcast_to(own_rows[None], (src_count // 2,) + own_rows.shape)]
    ppermute x0 -> x1, waiting for transfers between devices: none -> 0.56 us  [on_device(): theirs = lax.ppermute(mine, 'src', [(i, i ^ 1) for i in range(src_count)])]
  transfers between devices with their start and end apart: 2 -> 3, of which waited for: 2 -> 3; matrix products, arithmetic and copies ran while one was open for 3% -> 3% of each run, Pallas kernels for 0% -> 0%
where the time goes in v8:
time: 36.7 us; the launch traced here: 36.5 us
  waiting for transfers between devices  18.5 us (50%)
  starting transfers between devices  9.99 us (27%)
  Pallas kernels  4.3 us (12%)
  other arithmetic  1.4 us (4%)
  matrix products  0.85 us (2%)
  between operations  0.74 us (2%)
  local copies, waits for them, and re-layouts  0.71 us (2%)
    all_to_all x1, waiting for transfers between devices, on_device(): lax.all_to_all(sent, ('src', 'ep'), split_axis=0, concat_axis=0, tiled=True)  10.2 us
    all_to_all x1, waiting for transfers between devices, on_device(): lax.all_to_all(halves, ('src', 'ep'), split_axis=0, concat_axis=0, tiled=...  7.73 us
    all_to_all x1, starting transfers between devices, on_device(): lax.all_to_all(sent, ('src', 'ep'), split_axis=0, concat_axis=0, tiled=True)  7.3 us
    pallas_call x1, Pallas kernels, stencil_terms(): pl.pallas_call(functools.partial(stencil_kernel, size_y), out_shape=jax.S...  4.3 us
    all_to_all x1, starting transfers between devices, on_device(): lax.all_to_all(halves, ('src', 'ep'), split_axis=0, concat_axis=0, tiled=...  2.58 us
  transfers between devices with their start and end apart: 3, of which 3 were waited for; matrix products, arithmetic and copies ran while one was open for 3% of the time, Pallas kernels for 0%

profile of v8, /device:TPU:0, one launch (start us, length us, event | category | flops | bytes accessed | tf_op | source)
XLA Modules:
  0.0 36.5 jit_solution(15683980068480491370)
XLA Ops:
  0.6 4.3 %shard_map.121 = f32[512,128]{1,0:T(8,128)} custom-call(f32[512,128]{1,0:T(8,128)} %bitcast.29, f32[512,128]{1,0:T(8,128)} %bitcast.30, f32[512,128]{1,0:T(8,128)} %bitcast.31, s32[1,128]{1,0:T(1,128)} %bitcast.32, f32[1,128]{1,0:T(1,128)} %bitcast.33, f32[1]{0:T(128)} %bitcast.5.keep_ref, s32[2]{0:T(128)} %bitcast.34, s32[128]{0:T(128)} %receiver_ref.1), custom_call_target="tpu_custom_call" | custom-call | tf_op jit(solution)/shard_map/pallas_call | solution.py:242
  4.9 0.0 copy-start
  4.9 0.0 copy-start.1
  4.9 0.0 copy-start.3
  5.0 7.3 %all-to-all-start = ((f32[32,16,128]{2,1,0:T(8,128)}), f32[32,16,128]{2,1,0:T(8,128)S(1)}, u32[]{:S(2)}, u32[]{:S(2)}) async-start(f32[32,16,128]{2,1,0:T(8,128)} %bitcast.26), calls=%async_computation | async-start | bytes 524288 | tf_op jit(solution)/shard_map/all_to_all | solution.py:292
  12.3 0.0 copy-done
  12.3 0.0 copy-done.1
  12.3 0.0 copy-done.3
  12.3 0.0 copy-start.2
  12.3 0.4 %fusion.5 = f32[16,128,32]{1,2,0:T(8,128)S(1)} fusion(f32[32,6,1]{0,1,2:T(8,128)S(1)} %copy-done.3, f32[6,2048]{1,0:T(8,128)S(1)} %copy-done.1, f32[6,2048]{1,0:T(8,128)S(1)} %copy-done), kind=kOutput, calls=%fused_computation.10 | convolution fusion | flops 4730880 | bytes 361216 | tf_op jit(solution)/shard_map/pk,krz->prz/dot_general | solution.py:296
  12.7 10.2 %all-to-all-done = f32[32,16,128]{2,1,0:T(8,128)S(1)} async-done(((f32[32,16,128]{2,1,0:T(8,128)}), f32[32,16,128]{2,1,0:T(8,128)S(1)}, u32[]{:S(2)}, u32[]{:S(2)}) %all-to-all-start) | async-done | bytes 262176 | tf_op jit(solution)/shard_map/all_to_all | solution.py:292
  22.9 0.0 copy-done.2
  22.9 0.5 %fusion = f32[32,16,128]{2,0,1:T(8,128)S(1)} fusion(f32[16,128,32]{1,2,0:T(8,128)S(1)} %fusion.5, f32[32,32,1]{1,0,2:T(8,128)S(1)} %copy-done.2, f32[32,16,128]{2,1,0:T(8,128)S(1)} %all-to-all-done), kind=kOutput, calls=%fused_computation.1 | convolution fusion | flops 25231360 | bytes 790528 | tf_op jit(solution)/shard_map/pq,qrz->prz/dot_general | solution.py:297
  23.4 0.7 %broadcast_in_dim.2 = f32[2,2,8,8,128]{4,3,2,1,0:T(8,128)} broadcast(f32[2,8,8,128]{3,2,1,0:T(8,128)S(1)} %copy.18), dimensions={1,2,3,4} | broadcast | bytes 196608 | tf_op jit(solution)/shard_map/broadcast_in_dim | solution.py:306
  24.1 2.6 %all-to-all-start.1 = ((f32[32,8,128]{2,1,0:T(8,128)}), f32[32,8,128]{2,1,0:T(8,128)S(1)}, u32[]{:S(2)}, u32[]{:S(2)}) async-start(f32[32,8,128]{2,1,0:T(8,128)} %bitcast.14), calls=%async_computation.1 | async-start | bytes 262144 | tf_op jit(solution)/shard_map/all_to_all | solution.py:307
  26.7 7.7 %all-to-all-done.1 = f32[32,8,128]{2,1,0:T(8,128)S(1)} async-done(((f32[32,8,128]{2,1,0:T(8,128)}), f32[32,8,128]{2,1,0:T(8,128)S(1)}, u32[]{:S(2)}, u32[]{:S(2)}) %all-to-all-start.1) | async-done | bytes 131104 | tf_op jit(solution)/shard_map/all_to_all | solution.py:307
  34.4 0.1 collective-permute-start
  34.5 0.7 %fusion.8 = (f32[6,2048]{1,0:T(8,128)}, f32[6,2048]{1,0:T(8,128)}) fusion(f32[6,2048]{1,0:T(8,128)S(1)} %copy-done, f32[32,16,128]{2,0,1:T(8,128)S(1)} %fusion), kind=kLoop, calls=%fused_computation.13 | loop fusion | flops 86016 | bytes 294912 | tf_op jit(solution)/shard_map/sub | solution.py:301
  35.2 0.6 %collective-permute-done = f32[32,8,128]{2,1,0:T(8,128)S(1)} collective-permute-done((f32[32,8,128]{2,1,0:T(8,128)S(1)}, f32[32,8,128]{2,1,0:T(8,128)S(1)}, u32[]{:S(2)}, u32[]{:S(2)}) %collective-permute-start) | collective-permute-done | bytes 131104 | tf_op jit(solution)/shard_map/ppermute | solution.py:308
  35.7 0.7 %maximum_select_fusion = f32[32,16,128]{2,1,0:T(8,128)} fusion(f32[32,8,128]{2,1,0:T(8,128)S(1)} %collective-permute-done, f32[32,8,128]{2,1,0:T(8,128)S(1)} %all-to-all-done.1, pred[]{:T(512)S(6)} %eq.8), kind=kLoop, calls=%fused_computation.2 | loop fusion | flops 196608 | bytes 524289 | tf_op jit(solution)/shard_map/jit(_where)/select_n | solution.py:309
  (2 shorter events, 0.0 us)
Async XLA Ops:
  4.9 7.3 %copy-start = (f32[6,2048]{1,0:T(8,128)S(1)}, f32[6,2048]{1,0:T(8,128)}, u32[]{:S(2)}) copy-start(f32[6,2048]{1,0:T(8,128)} %param.17) | copy-start | bytes 147460
  4.9 7.3 %copy-start.1 = (f32[6,2048]{1,0:T(8,128)S(1)}, f32[6,2048]{1,0:T(8,128)}, u32[]{:S(2)}) copy-start(f32[6,2048]{1,0:T(8,128)} %param.16) | copy-start | bytes 147460
  4.9 7.3 %copy-start.3 = (f32[32,6,1]{0,1,2:T(8,128)S(1)}, f32[32,6,1]{0,1,2:T(8,128)}, u32[]{:S(2)}) copy-start(f32[32,6,1]{0,1,2:T(8,128)} %constant.41) | copy-start | bytes 2308
  5.0 18.0 %all-to-all-start = ((f32[32,16,128]{2,1,0:T(8,128)}), f32[32,16,128]{2,1,0:T(8,128)S(1)}, u32[]{:S(2)}, u32[]{:S(2)}) async-start(f32[32,16,128]{2,1,0:T(8,128)} %bitcast.26), calls=%async_computation | async-start | bytes 524288 | tf_op jit(solution)/shard_map/all_to_all | solution.py:292
  12.3 10.6 %copy-start.2 = (f32[32,32,1]{1,0,2:T(8,128)S(1)}, f32[32,32,1]{1,0,2:T(8,128)}, u32[]{:S(2)}) copy-start(f32[32,32,1]{1,0,2:T(8,128)} %constant.40) | copy-start | bytes 12292
  24.1 10.3 %all-to-all-start.1 = ((f32[32,8,128]{2,1,0:T(8,128)}), f32[32,8,128]{2,1,0:T(8,128)S(1)}, u32[]{:S(2)}, u32[]{:S(2)}) async-start(f32[32,8,128]{2,1,0:T(8,128)} %bitcast.14), calls=%async_computation.1 | async-start | bytes 262144 | tf_op jit(solution)/shard_map/all_to_all | solution.py:307
  34.4 1.3 %collective-permute-start = (f32[32,8,128]{2,1,0:T(8,128)S(1)}, f32[32,8,128]{2,1,0:T(8,128)S(1)}, u32[]{:S(2)}, u32[]{:S(2)}) collective-permute-start(f32[32,8,128]{2,1,0:T(8,128)S(1)} %all-to-all-done.1), channel_id=1, source_target_pairs={{0,8},{8,0},{16,24},{24,16},{1,9},{9,1},{17,25},{25,17},{2,10},{10... | collective-permute-start | bytes 393224 | tf_op jit(solution)/shard_map/ppermute | solution.py:308

commit v9 on v6

--- a/solution.py
+++ b/solution.py
@@ -133,10 +133,12 @@
 
 def stencil_kernel(
     size_y,
+    half,
     model_ref, forward_ref, adjoint_ref, receiver_vec_ref, observed_vec_ref,
-    keep_ref, source_ref, receiver_ref,
-    out_ref, drive_ref,
+    keep_ref, core_ref, source_ref, receiver_ref,
+    *outputs,
 ):
+    drive_ref = outputs[-1]
     rows, lanes = model_ref.shape
     size_x = rows // size_y
     inner = 8
@@ -231,32 +233,48 @@
         precision=lax.Precision.HIGHEST, preferred_element_type=jnp.float32,
     )
     adjoint = relax(load(adjoint_ref), drive.reshape(shape))
-    store(out_ref, keep_ref[0] * model - STEP_SIZE * (conductivity * (forward * adjoint)))
-
-
-def stencil_terms(size_y, model, forward, adjoint, keep, source_cells, receiver_cells, observed):
+    terms = keep_ref[0] * model - STEP_SIZE * (conductivity * (forward * adjoint))
+    if not half:
+        store(outputs[0], terms)
+        return
+    keep_out, send_out = outputs[0], outputs[1]
+    store(drive_ref, terms)
+    core = core_ref[0]
+    for chunk in range(keep_out.shape[0]):
+        start = chunk * 2 * half
+        keep_out[chunk] = drive_ref[pl.ds(pl.multiple_of(start + core * half, half), half), :]
+        send_out[chunk] = drive_ref[pl.ds(pl.multiple_of(start + (1 - core) * half, half), half), :]
+
+
+def stencil_terms(size_y, half, model, forward, adjoint, keep, core, source_cells, receiver_cells, observed):
     rows, lanes = model.shape
     receivers = receiver_cells.shape[0]
     vmem = pl.BlockSpec(memory_space=pltpu.VMEM)
     smem = pl.BlockSpec(memory_space=pltpu.SMEM)
+    if half:
+        chunks = rows // (2 * half)
+        out_shape = (jax.ShapeDtypeStruct((chunks, half, lanes), jnp.float32),) * 2
+        out_specs = (vmem, vmem)
+    else:
+        out_shape = jax.ShapeDtypeStruct((rows, lanes), jnp.float32)
+        out_specs = vmem
     return pl.pallas_call(
-        functools.partial(stencil_kernel, size_y),
-        out_shape=jax.ShapeDtypeStruct((rows, lanes), jnp.float32),
-        in_specs=[vmem, vmem, vmem, vmem, vmem, smem, smem, smem],
-        out_specs=vmem,
+        functools.partial(stencil_kernel, size_y, half),
+        out_shape=out_shape,
+        in_specs=[vmem, vmem, vmem, vmem, vmem, smem, smem, smem, smem],
+        out_specs=out_specs,
         scratch_shapes=[pltpu.VMEM((rows, lanes), jnp.float32)],
     )(
         model, forward, adjoint, receiver_cells.reshape(1, receivers),
-        observed.reshape(1, receivers), keep, source_cells, receiver_cells,
-    )
-
-
-def temporal_operators(epochs, src_count):
+        observed.reshape(1, receivers), keep, core, source_cells, receiver_cells,
+    )
+
+
+def temporal_operators(epochs):
     second = np.eye(epochs - 2, epochs) - 2.0 * np.eye(epochs - 2, epochs, k=1) + np.eye(epochs - 2, epochs, k=2)
     inverse = np.linalg.inv(np.eye(epochs) + PENALTY * second.T @ second)
-    solve = np.tile(inverse, (src_count, src_count))
-    coupling = np.tile(PENALTY * inverse @ second.T, (src_count, 1))
-    return jnp.asarray(solve, jnp.float32), jnp.asarray(coupling, jnp.float32)
+    coupling = PENALTY * inverse @ second.T
+    return inverse.astype(np.float32), coupling.astype(np.float32)
 
 
 def on_device(
@@ -277,29 +295,55 @@
     share_cells = cell_count // devices
     share_rows = share_cells // size_z
     total_epochs = slab_epochs * ep_count
-    keep = jnp.where(lax.axis_index("src") == 0, 1.0, 0.0).astype(jnp.float32).reshape(1)
-    partial_rhs = stencil_terms(
+    gaps = split_term.shape[0]
+    inverse, coupling = temporal_operators(total_epochs)
+    gap = (split_term - dual_term).reshape(gaps, share_rows, size_z)
+    fixed_part = jnp.einsum("pk,krz->prz", coupling, gap, precision=lax.Precision.HIGHEST)
+    src_index = lax.axis_index("src")
+    keep = jnp.where(src_index == 0, 1.0, 0.0).astype(jnp.float32).reshape(1)
+    core = (src_index % 2).astype(jnp.int32)
+    pairs = [(i, i ^ 1) for i in range(src_count)]
+    half = share_rows // 2 if share_rows % 2 == 0 and src_count % 2 == 0 else 0
+    terms = stencil_terms(
         size_y,
+        half,
         log_conductivity.reshape(size_x * size_y, size_z),
         forward_field.reshape(size_x * size_y, size_z),
         adjoint_field.reshape(size_x * size_y, size_z),
         keep,
+        core.reshape(1),
         source_cells.reshape(2),
         receiver_cells,
         observed.reshape(-1),
     )
-    sent = partial_rhs.reshape(devices, share_rows, size_z)
-    got = lax.all_to_all(sent, ("src", "ep"), split_axis=0, concat_axis=0, tiled=True)
-    solve, coupling = temporal_operators(total_epochs, src_count)
-    gaps = split_term.shape[0]
-    gap = (split_term - dual_term).reshape(gaps, share_rows, size_z)
-    fixed_part = jnp.einsum("pk,krz->prz", coupling, gap, precision=lax.Precision.HIGHEST)
-    back = jnp.einsum("pq,qrz->prz", solve, got, precision=lax.Precision.HIGHEST) + fixed_part
-    updated = back[:total_epochs].reshape(total_epochs, share_cells)
+    if half:
+        kept, sent = terms
+        summed = kept + lax.ppermute(sent, "src", pairs)
+        got = lax.all_to_all(summed, ("src", "ep"), split_axis=0, concat_axis=0, tiled=True)
+        rows_by_half = got.reshape(src_count // 2, 2, total_epochs, half, size_z).sum(axis=0)
+        fixed_by_half = fixed_part.reshape(total_epochs, 2, half, size_z).transpose(1, 0, 2, 3)
+        solved = (
+            jnp.einsum("tk,ckrz->ctrz", inverse, rows_by_half, precision=lax.Precision.HIGHEST)
+            + fixed_by_half
+        )
+        updated = solved.transpose(1, 0, 2, 3).reshape(total_epochs, share_cells)
+        halves = jnp.broadcast_to(solved[None], (src_count // 2,) + solved.shape).reshape(devices, half, size_z)
+        mine = lax.all_to_all(halves, ("src", "ep"), split_axis=0, concat_axis=0, tiled=True)
+        theirs = lax.ppermute(mine, "src", pairs)
+        model_rows = jnp.where(
+            core == 0, jnp.concatenate([mine, theirs], axis=1), jnp.concatenate([theirs, mine], axis=1)
+        )
+    else:
+        sent = terms.reshape(devices, share_rows, size_z)
+        got = lax.all_to_all(sent, ("src", "ep"), split_axis=0, concat_axis=0, tiled=True)
+        solve = np.tile(inverse, (src_count, src_count))
+        back = jnp.einsum("pq,qrz->prz", solve, got, precision=lax.Precision.HIGHEST)
+        back = back + jnp.tile(fixed_part, (src_count, 1, 1))
+        updated = back[:total_epochs].reshape(total_epochs, share_cells)
+        model_rows = lax.all_to_all(back, ("src", "ep"), split_axis=0, concat_axis=0, tiled=True)
     shifted = difference(updated) + dual_term
     split_term = shifted - jnp.clip(shifted, -THRESHOLD, THRESHOLD)
     dual_term = shifted - split_term
-    model_rows = lax.all_to_all(back, ("src", "ep"), split_axis=0, concat_axis=0, tiled=True)
     model_log = model_rows.reshape(slab_epochs, size_x, size_y, size_z)
     return (model_log, split_term, dual_term)
 

time: 38.5 us -> 37.4 us (0.971)
  waiting for transfers between devices: 20.2 us -> 17 us
  other arithmetic: 0.68 us -> 3.01 us
  matrix products: 0.85 us -> 0.38 us
  starting transfers between devices: 9.89 us -> 10.3 us
    all_to_all x2, waiting for transfers between devices: 20.2 us -> 15.2 us  [the longest x1 7.69 us: on_device(): lax.all_to_all(halves, ('src', 'ep'), split_axis=0, concat_axis=0, tiled=...]
    ppermute x0 -> x2, waiting for transfers between devices: none -> 1.77 us  [the longest x1 1.2 us: on_device(): summed = kept + lax.ppermute(sent, 'src', pairs)]
    add x0 -> x3, other arithmetic: none -> 1.61 us  [the longest x1 1.58 us: on_device(): summed = kept + lax.ppermute(sent, 'src', pairs)]
    add x1, local copies, waits for them, and re-layouts: 0.86 us -> 0.01 us  [on_device(): jnp.einsum('tk,ckrz->ctrz', inverse, rows_by_half, precision=lax.Precisio...]
    select_n x0 -> x1, other arithmetic: none -> 0.72 us  [on_device(): jnp.where(core == 0, jnp.concatenate([mine, theirs], axis=1), jnp.concate...]
    broadcast_in_dim x0 -> x1, local copies, waits for them, and re-layouts: none -> 0.66 us  [on_device(): jnp.broadcast_to(solved[None], (src_count // 2,) + solved.shape)]
    ppermute x0 -> x2, starting transfers between devices: none -> 0.56 us  [the longest x1 0.45 us: on_device(): summed = kept + lax.ppermute(sent, 'src', pairs)]
  transfers between devices with their start and end apart: 2 -> 4, of which waited for: 2 -> 4; matrix products, arithmetic and copies ran while one was open for 3% -> 2% of each run, Pallas kernels for 0% -> 0%
where the time goes in v9:
time: 37.4 us; the launch traced here: 37.1 us
  waiting for transfers between devices  17 us (45%)
  starting transfers between devices  10.3 us (28%)
  Pallas kernels  4.28 us (11%)
  other arithmetic  3.01 us (8%)
  local copies, waits for them, and re-layouts  1.36 us (4%)
  between operations  0.74 us (2%)
  matrix products  0.38 us (1%)
    all_to_all x1, waiting for transfers between devices, on_device(): lax.all_to_all(halves, ('src', 'ep'), split_axis=0, concat_axis=0, tiled=...  7.69 us
    all_to_all x1, waiting for transfers between devices, on_device(): lax.all_to_all(summed, ('src', 'ep'), split_axis=0, concat_axis=0, tiled=...  7.51 us
    all_to_all x1, starting transfers between devices, on_device(): lax.all_to_all(summed, ('src', 'ep'), split_axis=0, concat_axis=0, tiled=...  7.2 us
    pallas_call x1, Pallas kernels, stencil_terms(): pl.pallas_call(functools.partial(stencil_kernel, size_y, half), out_shape...  4.28 us
    all_to_all x1, starting transfers between devices, on_device(): lax.all_to_all(halves, ('src', 'ep'), split_axis=0, concat_axis=0, tiled=...  2.58 us
    add x1, other arithmetic, on_device(): summed = kept + lax.ppermute(sent, 'src', pairs)  1.58 us
    ppermute x1, waiting for transfers between devices, on_device(): summed = kept + lax.ppermute(sent, 'src', pairs)  1.2 us
  transfers between devices with their start and end apart: 4, of which 4 were waited for; matrix products, arithmetic and copies ran while one was open for 2% of the time, Pallas kernels for 0%

profile of v9, /device:TPU:0, one launch (start us, length us, event | category | flops | bytes accessed | tf_op | source)
XLA Modules:
  0.0 37.1 jit_solution(4701805091723406874)
XLA Ops:
  0.6 4.3 %shard_map.121 = (f32[32,8,128]{2,1,0:T(8,128)}, f32[32,8,128]{2,1,0:T(8,128)}) custom-call(f32[512,128]{1,0:T(8,128)} %bitcast.32, f32[512,128]{1,0:T(8,128)} %bitcast.33, f32[512,128]{1,0:T(8,128)} %bitcast.34, s32[1,128]{1,0:T(1,128)} %bitcast.36, f32[1,128]{1,0:T(1,128)} %bitcast.37, f32[1]{0:T(128)} %bitcast.5.keep_ref, s32[1]{0:T(128)} %bitcast.6.core_ref, ...), custom_call_target="tpu_custom_call" | custom-call | tf_op jit(solution)/shard_map/pallas_call | solution.py:261
  4.9 0.5 %collective-permute-start = (f32[32,8,128]{2,1,0:T(8,128)}, f32[32,8,128]{2,1,0:T(8,128)S(1)}, u32[]{:S(2)}, u32[]{:S(2)}) collective-permute-start(f32[32,8,128]{2,1,0:T(8,128)} %get-tuple-element.6), channel_id=1, source_target_pairs={{0,8},{8,0},{16,24},{24,16},{1,9},{9,1},{17,25},{25,17},{2,10},{10... | collective-permute-start | bytes 393224 | tf_op jit(solution)/shard_map/ppermute | solution.py:321
  5.4 1.2 %collective-permute-done = f32[32,8,128]{2,1,0:T(8,128)S(1)} collective-permute-done((f32[32,8,128]{2,1,0:T(8,128)}, f32[32,8,128]{2,1,0:T(8,128)S(1)}, u32[]{:S(2)}, u32[]{:S(2)}) %collective-permute-start) | collective-permute-done | bytes 131104 | tf_op jit(solution)/shard_map/ppermute | solution.py:321
  6.6 1.6 %add.23 = f32[32,8,128]{2,1,0:T(8,128)} add(f32[32,8,128]{2,1,0:T(8,128)} %get-tuple-element.5, f32[32,8,128]{2,1,0:T(8,128)S(1)} %collective-permute-done) | non-fusion elementwise | flops 32768 | bytes 393216 | tf_op jit(solution)/shard_map/add | solution.py:321
  8.2 0.0 copy-start
  8.2 0.0 copy-start.1
  8.2 0.0 copy-start.3
  8.2 7.2 %all-to-all-start = ((f32[32,8,128]{2,1,0:T(8,128)}), f32[32,8,128]{2,1,0:T(8,128)S(1)}, u32[]{:S(2)}, u32[]{:S(2)}) async-start(f32[32,8,128]{2,1,0:T(8,128)} %add.23), calls=%async_computation | async-start | bytes 262144 | tf_op jit(solution)/shard_map/all_to_all | solution.py:322
  15.4 0.0 copy-done
  15.4 0.0 copy-done.1
  15.4 0.0 copy-done.3
  15.4 0.2 fusion.1
  15.6 7.5 %all-to-all-done = f32[32,8,128]{2,1,0:T(8,128)S(1)} async-done(((f32[32,8,128]{2,1,0:T(8,128)}), f32[32,8,128]{2,1,0:T(8,128)S(1)}, u32[]{:S(2)}, u32[]{:S(2)}) %all-to-all-start) | async-done | bytes 131104 | tf_op jit(solution)/shard_map/all_to_all | solution.py:322
  23.1 0.0 copy-start.2
  23.1 0.7 %copy-done.2 = f32[8,8,1,1]{1,0,3,2:T(8,128)S(1)} copy-done((f32[8,8,1,1]{1,0,3,2:T(8,128)S(1)}, f32[8,8,1,1]{1,0,3,2:T(8,128)}, u32[]{:S(2)}) %copy-start.2) | copy-done | bytes 280
  23.8 0.2 bitcast_add_fusion.1
  24.0 0.7 %broadcast_in_dim.2 = f32[2,2,8,8,128]{4,3,2,1,0:T(8,128)} broadcast(f32[2,8,8,128]{3,2,1,0:T(8,128)S(1)} %copy.17), dimensions={1,2,3,4} | broadcast | bytes 196608 | tf_op jit(solution)/shard_map/broadcast_in_dim | solution.py:330
  24.7 2.6 %all-to-all-start.1 = ((f32[32,8,128]{2,1,0:T(8,128)}), f32[32,8,128]{2,1,0:T(8,128)S(1)}, u32[]{:S(2)}, u32[]{:S(2)}) async-start(f32[32,8,128]{2,1,0:T(8,128)} %bitcast.16), calls=%async_computation.1 | async-start | bytes 262144 | tf_op jit(solution)/shard_map/all_to_all | solution.py:331
  27.3 7.7 %all-to-all-done.1 = f32[32,8,128]{2,1,0:T(8,128)S(1)} async-done(((f32[32,8,128]{2,1,0:T(8,128)}), f32[32,8,128]{2,1,0:T(8,128)S(1)}, u32[]{:S(2)}, u32[]{:S(2)}) %all-to-all-start.1) | async-done | bytes 131104 | tf_op jit(solution)/shard_map/all_to_all | solution.py:331
  35.0 0.1 collective-permute-start.1
  35.1 0.7 %fusion.6 = (f32[6,2048]{1,0:T(8,128)}, f32[6,2048]{1,0:T(8,128)}) fusion(f32[6,2048]{1,0:T(8,128)S(1)} %bitcast.35, f32[6,2048]{1,0:T(8,128)S(1)} %copy-done), kind=kLoop, calls=%fused_computation.12 | loop fusion | flops 49152 | bytes 196608 | tf_op jit(solution)/shard_map/sub | solution.py:346
  35.8 0.6 %collective-permute-done.1 = f32[32,8,128]{2,1,0:T(8,128)S(1)} collective-permute-done((f32[32,8,128]{2,1,0:T(8,128)S(1)}, f32[32,8,128]{2,1,0:T(8,128)S(1)}, u32[]{:S(2)}, u32[]{:S(2)}) %collective-permute-start.1) | collective-permute-done | bytes 131104 | tf_op jit(solution)/shard_map/ppermute | solution.py:332
  36.4 0.7 %maximum_select_fusion = f32[32,16,128]{2,1,0:T(8,128)} fusion(f32[32,8,128]{2,1,0:T(8,128)S(1)} %collective-permute-done.1, f32[32,8,128]{2,1,0:T(8,128)S(1)} %all-to-all-done.1, pred[]{:T(512)S(6)} %eq.8), kind=kLoop, calls=%fused_computation | loop fusion | flops 196608 | bytes 524289 | tf_op jit(solution)/shard_map/jit(_where)/select_n | solution.py:333
  (4 shorter events, 0.1 us)
Async XLA Ops:
  4.9 1.6 %collective-permute-start = (f32[32,8,128]{2,1,0:T(8,128)}, f32[32,8,128]{2,1,0:T(8,128)S(1)}, u32[]{:S(2)}, u32[]{:S(2)}) collective-permute-start(f32[32,8,128]{2,1,0:T(8,128)} %get-tuple-element.6), channel_id=1, source_target_pairs={{0,8},{8,0},{16,24},{24,16},{1,9},{9,1},{17,25},{25,17},{2,10},{10... | collective-permute-start | bytes 393224 | tf_op jit(solution)/shard_map/ppermute | solution.py:321
  8.2 7.2 %copy-start = (f32[6,2048]{1,0:T(8,128)S(1)}, f32[6,2048]{1,0:T(8,128)}, u32[]{:S(2)}) copy-start(f32[6,2048]{1,0:T(8,128)} %param.17) | copy-start | bytes 147460
  8.2 7.2 %copy-start.1 = (f32[6,2048]{1,0:T(8,128)S(1)}, f32[6,2048]{1,0:T(8,128)}, u32[]{:S(2)}) copy-start(f32[6,2048]{1,0:T(8,128)} %param.16) | copy-start | bytes 147460
  8.2 7.2 %copy-start.3 = (f32[8,6,1]{1,0,2:T(8,128)S(1)}, f32[8,6,1]{1,0,2:T(8,128)}, u32[]{:S(2)}) copy-start(f32[8,6,1]{1,0,2:T(8,128)} %constant.41) | copy-start | bytes 580
  8.2 15.0 %all-to-all-start = ((f32[32,8,128]{2,1,0:T(8,128)}), f32[32,8,128]{2,1,0:T(8,128)S(1)}, u32[]{:S(2)}, u32[]{:S(2)}) async-start(f32[32,8,128]{2,1,0:T(8,128)} %add.23), calls=%async_computation | async-start | bytes 262144 | tf_op jit(solution)/shard_map/all_to_all | solution.py:322
  23.1 0.7 %copy-start.2 = (f32[8,8,1,1]{1,0,3,2:T(8,128)S(1)}, f32[8,8,1,1]{1,0,3,2:T(8,128)}, u32[]{:S(2)}) copy-start(f32[8,8,1,1]{1,0,3,2:T(8,128)} %constant.40) | copy-start | bytes 772
  24.7 10.3 %all-to-all-start.1 = ((f32[32,8,128]{2,1,0:T(8,128)}), f32[32,8,128]{2,1,0:T(8,128)S(1)}, u32[]{:S(2)}, u32[]{:S(2)}) async-start(f32[32,8,128]{2,1,0:T(8,128)} %bitcast.16), calls=%async_computation.1 | async-start | bytes 262144 | tf_op jit(solution)/shard_map/all_to_all | solution.py:331
  35.0 1.3 %collective-permute-start.1 = (f32[32,8,128]{2,1,0:T(8,128)S(1)}, f32[32,8,128]{2,1,0:T(8,128)S(1)}, u32[]{:S(2)}, u32[]{:S(2)}) collective-permute-start(f32[32,8,128]{2,1,0:T(8,128)S(1)} %all-to-all-done.1), channel_id=1, source_target_pairs={{0,8},{8,0},{16,24},{24,16},{1,9},{9,1},{17,25},{25,17},{2,10},{10... | collective-permute-start | bytes 393224 | tf_op jit(solution)/shard_map/ppermute | solution.py:332

commit v10 on v9

--- a/solution.py
+++ b/solution.py
@@ -300,10 +300,10 @@
     gap = (split_term - dual_term).reshape(gaps, share_rows, size_z)
     fixed_part = jnp.einsum("pk,krz->prz", coupling, gap, precision=lax.Precision.HIGHEST)
     src_index = lax.axis_index("src")
-    keep = jnp.where(src_index == 0, 1.0, 0.0).astype(jnp.float32).reshape(1)
     core = (src_index % 2).astype(jnp.int32)
     pairs = [(i, i ^ 1) for i in range(src_count)]
     half = share_rows // 2 if share_rows % 2 == 0 and src_count % 2 == 0 else 0
+    keep = jnp.where((src_index == 0) & (half == 0), 1.0, 0.0).astype(jnp.float32).reshape(1)
     terms = stencil_terms(
         size_y,
         half,
@@ -318,14 +318,17 @@
     )
     if half:
         kept, sent = terms
-        summed = kept + lax.ppermute(sent, "src", pairs)
+        first_chip = jnp.where(src_index < 2, 1.0, 0.0).astype(jnp.float32)
+        model_half = lax.dynamic_index_in_dim(
+            log_conductivity.reshape(devices, 2, half, size_z), core, axis=1, keepdims=False
+        )
+        summed = kept + lax.ppermute(sent, "src", pairs) + first_chip * model_half
         got = lax.all_to_all(summed, ("src", "ep"), split_axis=0, concat_axis=0, tiled=True)
-        rows_by_half = got.reshape(src_count // 2, 2, total_epochs, half, size_z).sum(axis=0)
+        picks = np.kron(np.ones((1, src_count // 2)), np.kron(np.eye(2), inverse)).astype(np.float32)
         fixed_by_half = fixed_part.reshape(total_epochs, 2, half, size_z).transpose(1, 0, 2, 3)
-        solved = (
-            jnp.einsum("tk,ckrz->ctrz", inverse, rows_by_half, precision=lax.Precision.HIGHEST)
-            + fixed_by_half
-        )
+        solved = jnp.einsum("pq,qrz->prz", picks, got, precision=lax.Precision.HIGHEST).reshape(
+            2, total_epochs, half, size_z
+        ) + fixed_by_half
         updated = solved.transpose(1, 0, 2, 3).reshape(total_epochs, share_cells)
         halves = jnp.broadcast_to(solved[None], (src_count // 2,) + solved.shape).reshape(devices, half, size_z)
         mine = lax.all_to_all(halves, ("src", "ep"), split_axis=0, concat_axis=0, tiled=True)

time: 37.4 us -> 36.8 us (0.984)
  local copies, waits for them, and re-layouts: 1.36 us -> 0.73 us
    unnamed x8 -> x10, local copies, waits for them, and re-layouts: 0.68 us -> 0.02 us
    add x2 -> x1, other arithmetic: 1.59 us -> 1.58 us  [on_device(): summed = kept + lax.ppermute(sent, 'src', pairs) + first_chip * model_half]
where the time goes in v10:
time: 36.8 us; the launch traced here: 36.5 us
  waiting for transfers between devices  16.9 us (46%)
  starting transfers between devices  10.3 us (28%)
  Pallas kernels  4.32 us (12%)
  other arithmetic  3 us (8%)
  between operations  0.75 us (2%)
  local copies, waits for them, and re-layouts  0.73 us (2%)
  matrix products  0.39 us (1%)
    all_to_all x1, waiting for transfers between devices, on_device(): lax.all_to_all(halves, ('src', 'ep'), split_axis=0, concat_axis=0, tiled=...  7.68 us
    all_to_all x1, waiting for transfers between devices, on_device(): lax.all_to_all(summed, ('src', 'ep'), split_axis=0, concat_axis=0, tiled=...  7.5 us
    all_to_all x1, starting transfers between devices, on_device(): lax.all_to_all(summed, ('src', 'ep'), split_axis=0, concat_axis=0, tiled=...  7.2 us
    pallas_call x1, Pallas kernels, stencil_terms(): pl.pallas_call(functools.partial(stencil_kernel, size_y, half), out_shape...  4.32 us
    all_to_all x1, starting transfers between devices, on_device(): lax.all_to_all(halves, ('src', 'ep'), split_axis=0, concat_axis=0, tiled=...  2.58 us
    add x1, other arithmetic, on_device(): summed = kept + lax.ppermute(sent, 'src', pairs) + first_chip * model_half  1.58 us
    ppermute x1, waiting for transfers between devices, on_device(): summed = kept + lax.ppermute(sent, 'src', pairs) + first_chip * model_half  1.2 us
  transfers between devices with their start and end apart: 4, of which 4 were waited for; matrix products, arithmetic and copies ran while one was open for 2% of the time, Pallas kernels for 0%

profile of v10, /device:TPU:0, one launch (start us, length us, event | category | flops | bytes accessed | tf_op | source)
XLA Modules:
  0.0 36.5 jit_solution(8536094012922121757)
XLA Ops:
  0.6 0.0 copy-start
  0.7 4.3 %shard_map.121 = (f32[32,8,128]{2,1,0:T(8,128)}, f32[32,8,128]{2,1,0:T(8,128)}) custom-call(f32[512,128]{1,0:T(8,128)} %bitcast.47, f32[512,128]{1,0:T(8,128)} %bitcast.50, f32[512,128]{1,0:T(8,128)} %bitcast.51, s32[1,128]{1,0:T(1,128)} %bitcast.54, f32[1,128]{1,0:T(1,128)} %bitcast.55, f32[1]{0:T(128)} %constant.34.clone.1.keep_ref, s32[1]{0:T(128)} %bitcast.6.core_ref, ...), custom_call_target="tpu_custom_call" | custom-call | tf_op jit(solution)/shard_map/pallas_call | solution.py:261
  5.0 0.5 %collective-permute-start = (f32[32,8,128]{2,1,0:T(8,128)}, f32[32,8,128]{2,1,0:T(8,128)S(1)}, u32[]{:S(2)}, u32[]{:S(2)}) collective-permute-start(f32[32,8,128]{2,1,0:T(8,128)} %get-tuple-element.6), channel_id=1, source_target_pairs={{0,8},{8,0},{16,24},{24,16},{1,9},{9,1},{17,25},{25,17},{2,10},{10... | collective-permute-start | bytes 393224 | tf_op jit(solution)/shard_map/ppermute | solution.py:325
  5.4 1.2 %collective-permute-done = f32[32,8,128]{2,1,0:T(8,128)S(1)} collective-permute-done((f32[32,8,128]{2,1,0:T(8,128)}, f32[32,8,128]{2,1,0:T(8,128)S(1)}, u32[]{:S(2)}, u32[]{:S(2)}) %collective-permute-start) | collective-permute-done | bytes 131104 | tf_op jit(solution)/shard_map/ppermute | solution.py:325
  6.6 0.0 copy-done
  6.6 1.6 %fusion.2 = f32[32,8,128]{2,1,0:T(8,128)} fusion(f32[32,2,8,128]{3,2,1,0:T(8,128)S(1)} %bitcast.48, s32[]{:T(128)S(6)} %select_n.37, f32[32,8,128]{2,1,0:T(8,128)} %get-tuple-element.5, f32[32,8,128]{2,1,0:T(8,128)S(1)} %collective-permute-done, f32[]{:T(128)S(6)} %select_n.36), kind=kLoop, calls=%fused_computation.5 | loop fusion | flops 98304 | bytes 524296 | tf_op jit(solution)/shard_map/add | solution.py:325
  8.2 0.0 copy-start.1
  8.2 0.0 copy-start.2
  8.2 0.0 copy-start.4
  8.2 7.2 %all-to-all-start = ((f32[32,8,128]{2,1,0:T(8,128)}), f32[32,8,128]{2,1,0:T(8,128)S(1)}, u32[]{:S(2)}, u32[]{:S(2)}) async-start(f32[32,8,128]{2,1,0:T(8,128)} %fusion.2), calls=%async_computation | async-start | bytes 262144 | tf_op jit(solution)/shard_map/all_to_all | solution.py:326
  15.4 0.0 copy-done.1
  15.4 0.0 copy-done.2
  15.4 0.0 copy-done.4
  15.5 0.0 copy-start.3
  15.5 0.2 fusion.5
  15.7 7.5 %all-to-all-done = f32[32,8,128]{2,1,0:T(8,128)S(1)} async-done(((f32[32,8,128]{2,1,0:T(8,128)}), f32[32,8,128]{2,1,0:T(8,128)S(1)}, u32[]{:S(2)}, u32[]{:S(2)}) %all-to-all-start) | async-done | bytes 131104 | tf_op jit(solution)/shard_map/all_to_all | solution.py:326
  23.2 0.0 copy-done.3
  23.2 0.2 fusion
  23.4 0.7 %broadcast_in_dim.2 = f32[2,2,8,8,128]{4,3,2,1,0:T(8,128)} broadcast(f32[2,8,8,128]{3,2,1,0:T(8,128)S(1)} %copy.22), dimensions={1,2,3,4} | broadcast | bytes 196608 | tf_op jit(solution)/shard_map/broadcast_in_dim | solution.py:333
  24.1 2.6 %all-to-all-start.1 = ((f32[32,8,128]{2,1,0:T(8,128)}), f32[32,8,128]{2,1,0:T(8,128)S(1)}, u32[]{:S(2)}, u32[]{:S(2)}) async-start(f32[32,8,128]{2,1,0:T(8,128)} %bitcast.15), calls=%async_computation.1 | async-start | bytes 262144 | tf_op jit(solution)/shard_map/all_to_all | solution.py:334
  26.7 7.7 %all-to-all-done.1 = f32[32,8,128]{2,1,0:T(8,128)S(1)} async-done(((f32[32,8,128]{2,1,0:T(8,128)}), f32[32,8,128]{2,1,0:T(8,128)S(1)}, u32[]{:S(2)}, u32[]{:S(2)}) %all-to-all-start.1) | async-done | bytes 131104 | tf_op jit(solution)/shard_map/all_to_all | solution.py:334
  34.4 0.1 collective-permute-start.1
  34.5 0.7 %fusion.8 = (f32[6,2048]{1,0:T(8,128)}, f32[6,2048]{1,0:T(8,128)}) fusion(f32[6,2048]{1,0:T(8,128)S(1)} %copy-done.1, f32[1,6,16,128]{3,2,1,0:T(8,128)S(1)} %bitcast.53), kind=kLoop, calls=%fused_computation.16 | loop fusion | flops 49152 | bytes 196608 | tf_op jit(solution)/shard_map/sub | solution.py:349
  35.2 0.6 %collective-permute-done.1 = f32[32,8,128]{2,1,0:T(8,128)S(1)} collective-permute-done((f32[32,8,128]{2,1,0:T(8,128)S(1)}, f32[32,8,128]{2,1,0:T(8,128)S(1)}, u32[]{:S(2)}, u32[]{:S(2)}) %collective-permute-start.1) | collective-permute-done | bytes 131104 | tf_op jit(solution)/shard_map/ppermute | solution.py:335
  35.7 0.7 %maximum_select_fusion = f32[32,16,128]{2,1,0:T(8,128)} fusion(f32[32,8,128]{2,1,0:T(8,128)S(1)} %collective-permute-done.1, f32[32,8,128]{2,1,0:T(8,128)S(1)} %all-to-all-done.1, pred[]{:T(512)S(6)} %eq.5), kind=kLoop, calls=%fused_computation.2 | loop fusion | flops 196608 | bytes 524289 | tf_op jit(solution)/shard_map/jit(_where)/select_n | solution.py:336
  (3 shorter events, 0.1 us)
Async XLA Ops:
  0.6 6.0 %copy-start = (f32[1,16,32,128]{3,2,1,0:T(8,128)S(1)}, f32[1,16,32,128]{3,2,1,0:T(8,128)}, u32[]{:S(2)}) copy-start(f32[1,16,32,128]{3,2,1,0:T(8,128)} %param.10) | copy-start | bytes 786436
  5.0 1.7 %collective-permute-start = (f32[32,8,128]{2,1,0:T(8,128)}, f32[32,8,128]{2,1,0:T(8,128)S(1)}, u32[]{:S(2)}, u32[]{:S(2)}) collective-permute-start(f32[32,8,128]{2,1,0:T(8,128)} %get-tuple-element.6), channel_id=1, source_target_pairs={{0,8},{8,0},{16,24},{24,16},{1,9},{9,1},{17,25},{25,17},{2,10},{10... | collective-permute-start | bytes 393224 | tf_op jit(solution)/shard_map/ppermute | solution.py:325
  8.2 7.2 %copy-start.1 = (f32[6,2048]{1,0:T(8,128)S(1)}, f32[6,2048]{1,0:T(8,128)}, u32[]{:S(2)}) copy-start(f32[6,2048]{1,0:T(8,128)} %param.17) | copy-start | bytes 147460
  8.2 7.2 %copy-start.2 = (f32[6,2048]{1,0:T(8,128)S(1)}, f32[6,2048]{1,0:T(8,128)}, u32[]{:S(2)}) copy-start(f32[6,2048]{1,0:T(8,128)} %param.16) | copy-start | bytes 147460
  8.2 7.2 %copy-start.4 = (f32[8,6,1]{1,0,2:T(8,128)S(1)}, f32[8,6,1]{1,0,2:T(8,128)}, u32[]{:S(2)}) copy-start(f32[8,6,1]{1,0,2:T(8,128)} %constant.48) | copy-start | bytes 580
  8.2 15.0 %all-to-all-start = ((f32[32,8,128]{2,1,0:T(8,128)}), f32[32,8,128]{2,1,0:T(8,128)S(1)}, u32[]{:S(2)}, u32[]{:S(2)}) async-start(f32[32,8,128]{2,1,0:T(8,128)} %fusion.2), calls=%async_computation | async-start | bytes 262144 | tf_op jit(solution)/shard_map/all_to_all | solution.py:326
  15.5 7.7 %copy-start.3 = (f32[16,32,1]{1,0,2:T(8,128)S(1)}, f32[16,32,1]{1,0,2:T(8,128)}, u32[]{:S(2)}) copy-start(f32[16,32,1]{1,0,2:T(8,128)} %constant.47) | copy-start | bytes 6148
  24.1 10.3 %all-to-all-start.1 = ((f32[32,8,128]{2,1,0:T(8,128)}), f32[32,8,128]{2,1,0:T(8,128)S(1)}, u32[]{:S(2)}, u32[]{:S(2)}) async-start(f32[32,8,128]{2,1,0:T(8,128)} %bitcast.15), calls=%async_computation.1 | async-start | bytes 262144 | tf_op jit(solution)/shard_map/all_to_all | solution.py:334
  34.4 1.3 %collective-permute-start.1 = (f32[32,8,128]{2,1,0:T(8,128)S(1)}, f32[32,8,128]{2,1,0:T(8,128)S(1)}, u32[]{:S(2)}, u32[]{:S(2)}) collective-permute-start(f32[32,8,128]{2,1,0:T(8,128)S(1)} %all-to-all-done.1), channel_id=1, source_target_pairs={{0,8},{8,0},{16,24},{24,16},{1,9},{9,1},{17,25},{25,17},{2,10},{10... | collective-permute-start | bytes 393224 | tf_op jit(solution)/shard_map/ppermute | solution.py:335

commit v11 on v10

--- a/solution.py
+++ b/solution.py
@@ -222,7 +222,7 @@
     placed = (slot_row == cells // lanes).astype(jnp.float32)
     picked = lax.dot_general(
         forward.reshape(rows, lanes), placed, (((0,), (0,)), ((), ())),
-        precision=lax.Precision.HIGHEST, preferred_element_type=jnp.float32,
+        precision=lax.Precision.HIGH, preferred_element_type=jnp.float32,
     )
     hit = lax.broadcasted_iota(jnp.int32, (lanes, receivers), 0) == cells % lanes
     value = jnp.sum(jnp.where(hit, picked, 0.0), axis=0, keepdims=True)
@@ -230,7 +230,7 @@
     weighted = jnp.where(hit, DATA_WEIGHT * misfit, 0.0)
     drive = lax.dot_general(
         placed, weighted, (((1,), (1,)), ((), ())),
-        precision=lax.Precision.HIGHEST, preferred_element_type=jnp.float32,
+        precision=lax.Precision.HIGH, preferred_element_type=jnp.float32,
     )
     adjoint = relax(load(adjoint_ref), drive.reshape(shape))
     terms = keep_ref[0] * model - STEP_SIZE * (conductivity * (forward * adjoint))
@@ -326,7 +326,7 @@
         got = lax.all_to_all(summed, ("src", "ep"), split_axis=0, concat_axis=0, tiled=True)
         picks = np.kron(np.ones((1, src_count // 2)), np.kron(np.eye(2), inverse)).astype(np.float32)
         fixed_by_half = fixed_part.reshape(total_epochs, 2, half, size_z).transpose(1, 0, 2, 3)
-        solved = jnp.einsum("pq,qrz->prz", picks, got, precision=lax.Precision.HIGHEST).reshape(
+        solved = jnp.einsum("pq,qrz->prz", picks, got, precision=lax.Precision.HIGH).reshape(
             2, total_epochs, half, size_z
         ) + fixed_by_half
         updated = solved.transpose(1, 0, 2, 3).reshape(total_epochs, share_cells)

time: 36.8 us -> 36.6 us (level)
  no operation moved by 1% of the time
where the time goes in v11:
time: 36.6 us; the launch traced here: 36.3 us
  waiting for transfers between devices  16.9 us (46%)
  starting transfers between devices  10.3 us (28%)
  Pallas kernels  4.22 us (12%)
  other arithmetic  3 us (8%)
  between operations  0.74 us (2%)
  local copies, waits for them, and re-layouts  0.73 us (2%)
    all_to_all x1, waiting for transfers between devices, on_device(): lax.all_to_all(halves, ('src', 'ep'), split_axis=0, concat_axis=0, tiled=...  7.68 us
    all_to_all x1, waiting for transfers between devices, on_device(): lax.all_to_all(summed, ('src', 'ep'), split_axis=0, concat_axis=0, tiled=...  7.5 us
    all_to_all x1, starting transfers between devices, on_device(): lax.all_to_all(summed, ('src', 'ep'), split_axis=0, concat_axis=0, tiled=...  7.21 us
    pallas_call x1, Pallas kernels, stencil_terms(): pl.pallas_call(functools.partial(stencil_kernel, size_y, half), out_shape...  4.22 us
    all_to_all x1, starting transfers between devices, on_device(): lax.all_to_all(halves, ('src', 'ep'), split_axis=0, concat_axis=0, tiled=...  2.58 us
    add x1, other arithmetic, on_device(): summed = kept + lax.ppermute(sent, 'src', pairs) + first_chip * model_half  1.58 us
    ppermute x1, waiting for transfers between devices, on_device(): summed = kept + lax.ppermute(sent, 'src', pairs) + first_chip * model_half  1.2 us
  transfers between devices with their start and end apart: 4, of which 4 were waited for; matrix products, arithmetic and copies ran while one was open for 2% of the time, Pallas kernels for 0%

profile of v11, /device:TPU:0, one launch (start us, length us, event | category | flops | bytes accessed | tf_op | source)
XLA Modules:
  0.0 36.3 jit_solution(13925645239531159081)
XLA Ops:
  0.6 0.0 copy-start
  0.7 4.2 %shard_map.121 = (f32[32,8,128]{2,1,0:T(8,128)}, f32[32,8,128]{2,1,0:T(8,128)}) custom-call(f32[512,128]{1,0:T(8,128)} %bitcast.47, f32[512,128]{1,0:T(8,128)} %bitcast.50, f32[512,128]{1,0:T(8,128)} %bitcast.51, s32[1,128]{1,0:T(1,128)} %bitcast.54, f32[1,128]{1,0:T(1,128)} %bitcast.55, f32[1]{0:T(128)} %constant.34.clone.1.keep_ref, s32[1]{0:T(128)} %bitcast.6.core_ref, ...), custom_call_target="tpu_custom_call" | custom-call | tf_op jit(solution)/shard_map/pallas_call | solution.py:261
  4.9 0.4 %collective-permute-start = (f32[32,8,128]{2,1,0:T(8,128)}, f32[32,8,128]{2,1,0:T(8,128)S(1)}, u32[]{:S(2)}, u32[]{:S(2)}) collective-permute-start(f32[32,8,128]{2,1,0:T(8,128)} %get-tuple-element.6), channel_id=1, source_target_pairs={{0,8},{8,0},{16,24},{24,16},{1,9},{9,1},{17,25},{25,17},{2,10},{10... | collective-permute-start | bytes 393224 | tf_op jit(solution)/shard_map/ppermute | solution.py:325
  5.3 1.2 %collective-permute-done = f32[32,8,128]{2,1,0:T(8,128)S(1)} collective-permute-done((f32[32,8,128]{2,1,0:T(8,128)}, f32[32,8,128]{2,1,0:T(8,128)S(1)}, u32[]{:S(2)}, u32[]{:S(2)}) %collective-permute-start) | collective-permute-done | bytes 131104 | tf_op jit(solution)/shard_map/ppermute | solution.py:325
  6.5 0.0 copy-done
  6.5 1.6 %fusion.2 = f32[32,8,128]{2,1,0:T(8,128)} fusion(f32[32,2,8,128]{3,2,1,0:T(8,128)S(1)} %bitcast.48, s32[]{:T(128)S(6)} %select_n.37, f32[32,8,128]{2,1,0:T(8,128)} %get-tuple-element.5, f32[32,8,128]{2,1,0:T(8,128)S(1)} %collective-permute-done, f32[]{:T(128)S(6)} %select_n.36), kind=kLoop, calls=%fused_computation.5 | loop fusion | flops 98304 | bytes 524296 | tf_op jit(solution)/shard_map/add | solution.py:325
  8.1 0.0 copy-start.1
  8.1 0.0 copy-start.2
  8.1 0.0 copy-start.4
  8.1 7.2 %all-to-all-start = ((f32[32,8,128]{2,1,0:T(8,128)}), f32[32,8,128]{2,1,0:T(8,128)S(1)}, u32[]{:S(2)}, u32[]{:S(2)}) async-start(f32[32,8,128]{2,1,0:T(8,128)} %fusion.2), calls=%async_computation | async-start | bytes 262144 | tf_op jit(solution)/shard_map/all_to_all | solution.py:326
  15.3 0.0 copy-done.1
  15.3 0.0 copy-done.2
  15.3 0.0 copy-done.4
  15.4 0.0 copy-start.3
  15.4 0.2 fusion.5
  15.6 7.5 %all-to-all-done = f32[32,8,128]{2,1,0:T(8,128)S(1)} async-done(((f32[32,8,128]{2,1,0:T(8,128)}), f32[32,8,128]{2,1,0:T(8,128)S(1)}, u32[]{:S(2)}, u32[]{:S(2)}) %all-to-all-start) | async-done | bytes 131104 | tf_op jit(solution)/shard_map/all_to_all | solution.py:326
  23.1 0.0 copy-done.3
  23.1 0.2 fusion
  23.3 0.7 %broadcast_in_dim.2 = f32[2,2,8,8,128]{4,3,2,1,0:T(8,128)} broadcast(f32[2,8,8,128]{3,2,1,0:T(8,128)S(1)} %copy.22), dimensions={1,2,3,4} | broadcast | bytes 196608 | tf_op jit(solution)/shard_map/broadcast_in_dim | solution.py:333
  23.9 2.6 %all-to-all-start.1 = ((f32[32,8,128]{2,1,0:T(8,128)}), f32[32,8,128]{2,1,0:T(8,128)S(1)}, u32[]{:S(2)}, u32[]{:S(2)}) async-start(f32[32,8,128]{2,1,0:T(8,128)} %bitcast.15), calls=%async_computation.1 | async-start | bytes 262144 | tf_op jit(solution)/shard_map/all_to_all | solution.py:334
  26.6 7.7 %all-to-all-done.1 = f32[32,8,128]{2,1,0:T(8,128)S(1)} async-done(((f32[32,8,128]{2,1,0:T(8,128)}), f32[32,8,128]{2,1,0:T(8,128)S(1)}, u32[]{:S(2)}, u32[]{:S(2)}) %all-to-all-start.1) | async-done | bytes 131104 | tf_op jit(solution)/shard_map/all_to_all | solution.py:334
  34.3 0.1 collective-permute-start.1
  34.4 0.7 %fusion.8 = (f32[6,2048]{1,0:T(8,128)}, f32[6,2048]{1,0:T(8,128)}) fusion(f32[6,2048]{1,0:T(8,128)S(1)} %copy-done.1, f32[1,6,16,128]{3,2,1,0:T(8,128)S(1)} %bitcast.53), kind=kLoop, calls=%fused_computation.16 | loop fusion | flops 49152 | bytes 196608 | tf_op jit(solution)/shard_map/sub | solution.py:349
  35.0 0.6 %collective-permute-done.1 = f32[32,8,128]{2,1,0:T(8,128)S(1)} collective-permute-done((f32[32,8,128]{2,1,0:T(8,128)S(1)}, f32[32,8,128]{2,1,0:T(8,128)S(1)}, u32[]{:S(2)}, u32[]{:S(2)}) %collective-permute-start.1) | collective-permute-done | bytes 131104 | tf_op jit(solution)/shard_map/ppermute | solution.py:335
  35.6 0.7 %maximum_select_fusion = f32[32,16,128]{2,1,0:T(8,128)} fusion(f32[32,8,128]{2,1,0:T(8,128)S(1)} %collective-permute-done.1, f32[32,8,128]{2,1,0:T(8,128)S(1)} %all-to-all-done.1, pred[]{:T(512)S(6)} %eq.5), kind=kLoop, calls=%fused_computation.2 | loop fusion | flops 196608 | bytes 524289 | tf_op jit(solution)/shard_map/jit(_where)/select_n | solution.py:336
  (3 shorter events, 0.1 us)
Async XLA Ops:
  0.6 5.9 %copy-start = (f32[1,16,32,128]{3,2,1,0:T(8,128)S(1)}, f32[1,16,32,128]{3,2,1,0:T(8,128)}, u32[]{:S(2)}) copy-start(f32[1,16,32,128]{3,2,1,0:T(8,128)} %param.10) | copy-start | bytes 786436
  4.9 1.6 %collective-permute-start = (f32[32,8,128]{2,1,0:T(8,128)}, f32[32,8,128]{2,1,0:T(8,128)S(1)}, u32[]{:S(2)}, u32[]{:S(2)}) collective-permute-start(f32[32,8,128]{2,1,0:T(8,128)} %get-tuple-element.6), channel_id=1, source_target_pairs={{0,8},{8,0},{16,24},{24,16},{1,9},{9,1},{17,25},{25,17},{2,10},{10... | collective-permute-start | bytes 393224 | tf_op jit(solution)/shard_map/ppermute | solution.py:325
  8.1 7.2 %copy-start.1 = (f32[6,2048]{1,0:T(8,128)S(1)}, f32[6,2048]{1,0:T(8,128)}, u32[]{:S(2)}) copy-start(f32[6,2048]{1,0:T(8,128)} %param.17) | copy-start | bytes 147460
  8.1 7.2 %copy-start.2 = (f32[6,2048]{1,0:T(8,128)S(1)}, f32[6,2048]{1,0:T(8,128)}, u32[]{:S(2)}) copy-start(f32[6,2048]{1,0:T(8,128)} %param.16) | copy-start | bytes 147460
  8.1 7.2 %copy-start.4 = (f32[8,6,1]{1,0,2:T(8,128)S(1)}, f32[8,6,1]{1,0,2:T(8,128)}, u32[]{:S(2)}) copy-start(f32[8,6,1]{1,0,2:T(8,128)} %constant.48) | copy-start | bytes 580
  8.1 15.0 %all-to-all-start = ((f32[32,8,128]{2,1,0:T(8,128)}), f32[32,8,128]{2,1,0:T(8,128)S(1)}, u32[]{:S(2)}, u32[]{:S(2)}) async-start(f32[32,8,128]{2,1,0:T(8,128)} %fusion.2), calls=%async_computation | async-start | bytes 262144 | tf_op jit(solution)/shard_map/all_to_all | solution.py:326
  15.4 7.7 %copy-start.3 = (f32[16,32,1]{1,0,2:T(8,128)S(1)}, f32[16,32,1]{1,0,2:T(8,128)}, u32[]{:S(2)}) copy-start(f32[16,32,1]{1,0,2:T(8,128)} %constant.47) | copy-start | bytes 6148
  23.9 10.3 %all-to-all-start.1 = ((f32[32,8,128]{2,1,0:T(8,128)}), f32[32,8,128]{2,1,0:T(8,128)S(1)}, u32[]{:S(2)}, u32[]{:S(2)}) async-start(f32[32,8,128]{2,1,0:T(8,128)} %bitcast.15), calls=%async_computation.1 | async-start | bytes 262144 | tf_op jit(solution)/shard_map/all_to_all | solution.py:334
  34.3 1.3 %collective-permute-start.1 = (f32[32,8,128]{2,1,0:T(8,128)S(1)}, f32[32,8,128]{2,1,0:T(8,128)S(1)}, u32[]{:S(2)}, u32[]{:S(2)}) collective-permute-start(f32[32,8,128]{2,1,0:T(8,128)S(1)} %all-to-all-done.1), channel_id=1, source_target_pairs={{0,8},{8,0},{16,24},{24,16},{1,9},{9,1},{17,25},{25,17},{2,10},{10... | collective-permute-start | bytes 393224 | tf_op jit(solution)/shard_map/ppermute | solution.py:335

commit v12 on v10

--- a/solution.py
+++ b/solution.py
@@ -324,13 +324,20 @@
         )
         summed = kept + lax.ppermute(sent, "src", pairs) + first_chip * model_half
         got = lax.all_to_all(summed, ("src", "ep"), split_axis=0, concat_axis=0, tiled=True)
-        picks = np.kron(np.ones((1, src_count // 2)), np.kron(np.eye(2), inverse)).astype(np.float32)
         fixed_by_half = fixed_part.reshape(total_epochs, 2, half, size_z).transpose(1, 0, 2, 3)
-        solved = jnp.einsum("pq,qrz->prz", picks, got, precision=lax.Precision.HIGHEST).reshape(
-            2, total_epochs, half, size_z
-        ) + fixed_by_half
+        by_chip = got.reshape(src_count // 2, 2, total_epochs, half, size_z)
+        rows_by_half = by_chip[0]
+        for chip in range(1, src_count // 2):
+            rows_by_half = rows_by_half + by_chip[chip]
+        solved_rows = []
+        for t in range(total_epochs):
+            total = fixed_by_half[:, t]
+            for k in range(total_epochs):
+                total = total + float(inverse[t, k]) * rows_by_half[:, k]
+            solved_rows.append(total)
+        solved = jnp.stack(solved_rows, axis=1)
         updated = solved.transpose(1, 0, 2, 3).reshape(total_epochs, share_cells)
-        halves = jnp.broadcast_to(solved[None], (src_count // 2,) + solved.shape).reshape(devices, half, size_z)
+        halves = jnp.concatenate([solved] * (src_count // 2), axis=0).reshape(devices, half, size_z)
         mine = lax.all_to_all(halves, ("src", "ep"), split_axis=0, concat_axis=0, tiled=True)
         theirs = lax.ppermute(mine, "src", pairs)
         model_rows = jnp.where(

time: 36.8 us -> 36.7 us (level)
  other arithmetic: 3 us -> 3.78 us
  local copies, waits for them, and re-layouts: 0.73 us -> 0.03 us
    concatenate x0 -> x1, other arithmetic: none -> 0.66 us  [on_device(): jnp.concatenate([solved] * (src_count // 2), axis=0)]
    broadcast_in_dim x1 -> x0, local copies, waits for them, and re-layouts: 0.66 us -> none  [on_device(): jnp.broadcast_to(solved[None], (src_count // 2,) + solved.shape)]
where the time goes in v12:
time: 36.7 us; the launch traced here: 36.4 us
  waiting for transfers between devices  17 us (46%)
  starting transfers between devices  10.3 us (28%)
  Pallas kernels  4.31 us (12%)
  other arithmetic  3.78 us (10%)
  between operations  0.79 us (2%)
    all_to_all x1, waiting for transfers between devices, on_device(): lax.all_to_all(halves, ('src', 'ep'), split_axis=0, concat_axis=0, tiled=...  7.72 us
    all_to_all x1, waiting for transfers between devices, on_device(): lax.all_to_all(summed, ('src', 'ep'), split_axis=0, concat_axis=0, tiled=...  7.49 us
    all_to_all x1, starting transfers between devices, on_device(): lax.all_to_all(summed, ('src', 'ep'), split_axis=0, concat_axis=0, tiled=...  7.2 us
    pallas_call x1, Pallas kernels, stencil_terms(): pl.pallas_call(functools.partial(stencil_kernel, size_y, half), out_shape...  4.31 us
    all_to_all x1, starting transfers between devices, on_device(): lax.all_to_all(halves, ('src', 'ep'), split_axis=0, concat_axis=0, tiled=...  2.58 us
    add x1, other arithmetic, on_device(): summed = kept + lax.ppermute(sent, 'src', pairs) + first_chip * model_half  1.58 us
    ppermute x1, waiting for transfers between devices, on_device(): summed = kept + lax.ppermute(sent, 'src', pairs) + first_chip * model_half  1.2 us
  transfers between devices with their start and end apart: 4, of which 4 were waited for; matrix products, arithmetic and copies ran while one was open for 2% of the time, Pallas kernels for 0%

profile of v12, /device:TPU:0, one launch (start us, length us, event | category | flops | bytes accessed | tf_op | source)
XLA Modules:
  0.0 36.4 jit_solution(16914519861326677932)
XLA Ops:
  0.6 0.0 copy-start
  0.7 4.3 %shard_map.112 = (f32[32,8,128]{2,1,0:T(8,128)}, f32[32,8,128]{2,1,0:T(8,128)}) custom-call(f32[512,128]{1,0:T(8,128)} %bitcast.50, f32[512,128]{1,0:T(8,128)} %bitcast.62, f32[512,128]{1,0:T(8,128)} %bitcast.63, s32[1,128]{1,0:T(1,128)} %bitcast.64, f32[1,128]{1,0:T(1,128)} %bitcast.65, f32[1]{0:T(128)} %constant.35.clone.1.keep_ref, s32[1]{0:T(128)} %bitcast.9.core_ref, ...), custom_call_target="tpu_custom_call" | custom-call | tf_op jit(solution)/shard_map/pallas_call | solution.py:261
  5.0 0.5 %collective-permute-start = (f32[32,8,128]{2,1,0:T(8,128)}, f32[32,8,128]{2,1,0:T(8,128)S(1)}, u32[]{:S(2)}, u32[]{:S(2)}) collective-permute-start(f32[32,8,128]{2,1,0:T(8,128)} %get-tuple-element.6), channel_id=1, source_target_pairs={{0,8},{8,0},{16,24},{24,16},{1,9},{9,1},{17,25},{25,17},{2,10},{10... | collective-permute-start | bytes 393224 | tf_op jit(solution)/shard_map/ppermute | solution.py:325
  5.4 1.2 %collective-permute-done = f32[32,8,128]{2,1,0:T(8,128)S(1)} collective-permute-done((f32[32,8,128]{2,1,0:T(8,128)}, f32[32,8,128]{2,1,0:T(8,128)S(1)}, u32[]{:S(2)}, u32[]{:S(2)}) %collective-permute-start) | collective-permute-done | bytes 131104 | tf_op jit(solution)/shard_map/ppermute | solution.py:325
  6.6 0.0 copy-done
  6.6 1.6 %fusion.1 = f32[32,8,128]{2,1,0:T(8,128)} fusion(f32[32,2,8,128]{3,2,1,0:T(8,128)S(1)} %bitcast.51, s32[]{:T(128)S(6)} %select_n.37, f32[32,8,128]{2,1,0:T(8,128)} %get-tuple-element.5, f32[32,8,128]{2,1,0:T(8,128)S(1)} %collective-permute-done, f32[]{:T(128)S(6)} %select_n.36), kind=kLoop, calls=%fused_computation.4 | loop fusion | flops 98304 | bytes 524296 | tf_op jit(solution)/shard_map/add | solution.py:325
  8.2 0.0 copy-start.1
  8.2 0.0 copy-start.2
  8.2 0.0 copy-start.3
  8.2 7.2 %all-to-all-start = ((f32[32,8,128]{2,1,0:T(8,128)}), f32[32,8,128]{2,1,0:T(8,128)S(1)}, u32[]{:S(2)}, u32[]{:S(2)}) async-start(f32[32,8,128]{2,1,0:T(8,128)} %fusion.1), calls=%async_computation | async-start | bytes 262144 | tf_op jit(solution)/shard_map/all_to_all | solution.py:326
  15.4 0.0 copy-done.1
  15.4 0.0 copy-done.2
  15.4 0.0 copy-done.3
  15.4 0.2 fusion.2
  15.7 7.5 %all-to-all-done = f32[32,8,128]{2,1,0:T(8,128)S(1)} async-done(((f32[32,8,128]{2,1,0:T(8,128)}), f32[32,8,128]{2,1,0:T(8,128)S(1)}, u32[]{:S(2)}, u32[]{:S(2)}) %all-to-all-start) | async-done | bytes 131104 | tf_op jit(solution)/shard_map/all_to_all | solution.py:326
  23.3 0.7 %pad_maximum_fusion = f32[4,8,8,128]{3,2,1,0:T(8,128)} fusion(f32[2,8,8,128]{3,2,1,0:T(8,128)S(1)} %constant_dynamic-update-slice_fusion), kind=kLoop, calls=%fused_computation.1 | loop fusion | flops 32768 | bytes 196608 | tf_op jit(solution)/shard_map/concatenate | solution.py:340
  24.0 2.6 %all-to-all-start.1 = ((f32[32,8,128]{2,1,0:T(8,128)}), f32[32,8,128]{2,1,0:T(8,128)S(1)}, u32[]{:S(2)}, u32[]{:S(2)}) async-start(f32[32,8,128]{2,1,0:T(8,128)} %bitcast.14), calls=%async_computation.1 | async-start | bytes 262144 | tf_op jit(solution)/shard_map/all_to_all | solution.py:341
  26.6 7.7 %all-to-all-done.1 = f32[32,8,128]{2,1,0:T(8,128)S(1)} async-done(((f32[32,8,128]{2,1,0:T(8,128)}), f32[32,8,128]{2,1,0:T(8,128)S(1)}, u32[]{:S(2)}, u32[]{:S(2)}) %all-to-all-start.1) | async-done | bytes 131104 | tf_op jit(solution)/shard_map/all_to_all | solution.py:341
  34.3 0.1 collective-permute-start.1
  34.4 0.7 %fusion.6 = (f32[6,2048]{1,0:T(8,128)}, f32[6,2048]{1,0:T(8,128)}) fusion(f32[6,2048]{1,0:T(8,128)S(1)} %copy-done.1, f32[1,6,16,128]{3,2,1,0:T(8,128)S(1)} %copy_bitcast_fusion.1), kind=kLoop, calls=%fused_computation.16 | loop fusion | flops 49152 | bytes 196608 | tf_op jit(solution)/shard_map/sub | solution.py:356
  35.1 0.6 %collective-permute-done.1 = f32[32,8,128]{2,1,0:T(8,128)S(1)} collective-permute-done((f32[32,8,128]{2,1,0:T(8,128)S(1)}, f32[32,8,128]{2,1,0:T(8,128)S(1)}, u32[]{:S(2)}, u32[]{:S(2)}) %collective-permute-start.1) | collective-permute-done | bytes 131104 | tf_op jit(solution)/shard_map/ppermute | solution.py:342
  35.7 0.7 %maximum_select_fusion = f32[32,16,128]{2,1,0:T(8,128)} fusion(f32[32,8,128]{2,1,0:T(8,128)S(1)} %collective-permute-done.1, f32[32,8,128]{2,1,0:T(8,128)S(1)} %all-to-all-done.1, pred[]{:T(512)S(6)} %eq.5), kind=kLoop, calls=%fused_computation | loop fusion | flops 196608 | bytes 524289 | tf_op jit(solution)/shard_map/jit(_where)/select_n | solution.py:343
  (11 shorter events, 0.2 us)
Async XLA Ops:
  0.6 6.0 %copy-start = (f32[1,16,32,128]{3,2,1,0:T(8,128)S(1)}, f32[1,16,32,128]{3,2,1,0:T(8,128)}, u32[]{:S(2)}) copy-start(f32[1,16,32,128]{3,2,1,0:T(8,128)} %param.9) | copy-start | bytes 786436
  5.0 1.7 %collective-permute-start = (f32[32,8,128]{2,1,0:T(8,128)}, f32[32,8,128]{2,1,0:T(8,128)S(1)}, u32[]{:S(2)}, u32[]{:S(2)}) collective-permute-start(f32[32,8,128]{2,1,0:T(8,128)} %get-tuple-element.6), channel_id=1, source_target_pairs={{0,8},{8,0},{16,24},{24,16},{1,9},{9,1},{17,25},{25,17},{2,10},{10... | collective-permute-start | bytes 393224 | tf_op jit(solution)/shard_map/ppermute | solution.py:325
  8.2 7.2 %copy-start.1 = (f32[6,2048]{1,0:T(8,128)S(1)}, f32[6,2048]{1,0:T(8,128)}, u32[]{:S(2)}) copy-start(f32[6,2048]{1,0:T(8,128)} %param.16) | copy-start | bytes 147460
  8.2 7.2 %copy-start.2 = (f32[6,2048]{1,0:T(8,128)S(1)}, f32[6,2048]{1,0:T(8,128)}, u32[]{:S(2)}) copy-start(f32[6,2048]{1,0:T(8,128)} %param.15) | copy-start | bytes 147460
  8.2 7.2 %copy-start.3 = (f32[8,6,1]{1,0,2:T(8,128)S(1)}, f32[8,6,1]{1,0,2:T(8,128)}, u32[]{:S(2)}) copy-start(f32[8,6,1]{1,0,2:T(8,128)} %constant.84) | copy-start | bytes 580
  8.2 14.9 %all-to-all-start = ((f32[32,8,128]{2,1,0:T(8,128)}), f32[32,8,128]{2,1,0:T(8,128)S(1)}, u32[]{:S(2)}, u32[]{:S(2)}) async-start(f32[32,8,128]{2,1,0:T(8,128)} %fusion.1), calls=%async_computation | async-start | bytes 262144 | tf_op jit(solution)/shard_map/all_to_all | solution.py:326
  24.0 10.3 %all-to-all-start.1 = ((f32[32,8,128]{2,1,0:T(8,128)}), f32[32,8,128]{2,1,0:T(8,128)S(1)}, u32[]{:S(2)}, u32[]{:S(2)}) async-start(f32[32,8,128]{2,1,0:T(8,128)} %bitcast.14), calls=%async_computation.1 | async-start | bytes 262144 | tf_op jit(solution)/shard_map/all_to_all | solution.py:341
  34.3 1.3 %collective-permute-start.1 = (f32[32,8,128]{2,1,0:T(8,128)S(1)}, f32[32,8,128]{2,1,0:T(8,128)S(1)}, u32[]{:S(2)}, u32[]{:S(2)}) collective-permute-start(f32[32,8,128]{2,1,0:T(8,128)S(1)} %all-to-all-done.1), channel_id=1, source_target_pairs={{0,8},{8,0},{16,24},{24,16},{1,9},{9,1},{17,25},{25,17},{2,10},{10... | collective-permute-start | bytes 393224 | tf_op jit(solution)/shard_map/ppermute | solution.py:342

commit v13 on v8

--- a/solution.py
+++ b/solution.py
@@ -256,7 +256,7 @@
     inverse = np.linalg.inv(np.eye(epochs) + PENALTY * second.T @ second)
     solve = np.tile(inverse, (src_count, src_count))
     coupling = np.tile(PENALTY * inverse @ second.T, (src_count, 1))
-    return jnp.asarray(solve, jnp.float32), jnp.asarray(coupling, jnp.float32)
+    return solve.astype(np.float32), jnp.asarray(coupling, jnp.float32)
 
 
 def on_device(
@@ -294,23 +294,35 @@
     gaps = split_term.shape[0]
     gap = (split_term - dual_term).reshape(gaps, share_rows, size_z)
     fixed_part = jnp.einsum("pk,krz->prz", coupling, gap, precision=lax.Precision.HIGHEST)
-    back = jnp.einsum("pq,qrz->prz", solve, got, precision=lax.Precision.HIGHEST) + fixed_part
-    updated = back[:total_epochs].reshape(total_epochs, share_cells)
-    shifted = difference(updated) + dual_term
-    split_term = shifted - jnp.clip(shifted, -THRESHOLD, THRESHOLD)
-    dual_term = shifted - split_term
     half = share_rows // 2
     if share_rows % 2 == 0 and src_count % 2 == 0:
+        inverse = np.asarray(solve[:total_epochs, :total_epochs], np.float64)
+        summed = got[:total_epochs]
+        for s in range(1, src_count):
+            summed = summed + got[s * total_epochs : (s + 1) * total_epochs]
+        solved_rows = []
+        for t in range(total_epochs):
+            total = fixed_part[t]
+            for k in range(total_epochs):
+                total = total + float(inverse[t, k]) * summed[k]
+            solved_rows.append(total)
+        solved = jnp.stack(solved_rows)
+        updated = solved.reshape(total_epochs, share_cells)
         core = lax.axis_index("src") % 2
-        own_rows = back[:total_epochs].reshape(total_epochs, 2, half, size_z).transpose(1, 0, 2, 3)
-        halves = jnp.broadcast_to(own_rows[None], (src_count // 2,) + own_rows.shape).reshape(devices, half, size_z)
+        own_rows = solved.reshape(total_epochs, 2, half, size_z).transpose(1, 0, 2, 3)
+        halves = jnp.concatenate([own_rows] * (src_count // 2), axis=0).reshape(devices, half, size_z)
         mine = lax.all_to_all(halves, ("src", "ep"), split_axis=0, concat_axis=0, tiled=True)
         theirs = lax.ppermute(mine, "src", [(i, i ^ 1) for i in range(src_count)])
         model_rows = jnp.where(
             core == 0, jnp.concatenate([mine, theirs], axis=1), jnp.concatenate([theirs, mine], axis=1)
         )
     else:
+        back = jnp.einsum("pq,qrz->prz", solve, got, precision=lax.Precision.HIGHEST) + fixed_part
+        updated = back[:total_epochs].reshape(total_epochs, share_cells)
         model_rows = lax.all_to_all(back, ("src", "ep"), split_axis=0, concat_axis=0, tiled=True)
+    shifted = difference(updated) + dual_term
+    split_term = shifted - jnp.clip(shifted, -THRESHOLD, THRESHOLD)
+    dual_term = shifted - split_term
     model_log = model_rows.reshape(slab_epochs, size_x, size_y, size_z)
     return (model_log, split_term, dual_term)
 

time: 36.7 us -> 36.6 us (level)
  waiting for transfers between devices: 18.5 us -> 17.7 us
  other arithmetic: 1.4 us -> 2.2 us
  matrix products: 0.85 us -> 0.45 us
    all_to_all x1, waiting for transfers between devices: 10.2 us -> 9.44 us  [on_device(): lax.all_to_all(sent, ('src', 'ep'), split_axis=0, concat_axis=0, tiled=True)]
    unnamed x8 -> x21, local copies, waits for them, and re-layouts: 0.02 us -> 0.71 us
    concatenate x0 -> x1, other arithmetic: none -> 0.66 us  [on_device(): jnp.concatenate([own_rows] * (src_count // 2), axis=0)]
    broadcast_in_dim x1 -> x0, local copies, waits for them, and re-layouts: 0.66 us -> none  [on_device(): jnp.broadcast_to(own_rows[None], (src_count // 2,) + own_rows.shape)]
    dot_general x1 -> x0, matrix products: 0.45 us -> none  [on_device(): jnp.einsum('pq,qrz->prz', solve, got, precision=lax.Precision.HIGHEST)]
where the time goes in v13:
time: 36.6 us; the launch traced here: 36.3 us
  waiting for transfers between devices  17.7 us (48%)
  starting transfers between devices  9.98 us (27%)
  Pallas kernels  4.3 us (12%)
  other arithmetic  2.2 us (6%)
  between operations  0.91 us (2%)
  local copies, waits for them, and re-layouts  0.76 us (2%)
  matrix products  0.45 us (1%)
    all_to_all x1, waiting for transfers between devices, on_device(): lax.all_to_all(sent, ('src', 'ep'), split_axis=0, concat_axis=0, tiled=True)  9.44 us
    all_to_all x1, waiting for transfers between devices, on_device(): lax.all_to_all(halves, ('src', 'ep'), split_axis=0, concat_axis=0, tiled=...  7.71 us
    all_to_all x1, starting transfers between devices, on_device(): lax.all_to_all(sent, ('src', 'ep'), split_axis=0, concat_axis=0, tiled=True)  7.3 us
    pallas_call x1, Pallas kernels, stencil_terms(): pl.pallas_call(functools.partial(stencil_kernel, size_y), out_shape=jax.S...  4.3 us
    all_to_all x1, starting transfers between devices, on_device(): lax.all_to_all(halves, ('src', 'ep'), split_axis=0, concat_axis=0, tiled=...  2.58 us
  transfers between devices with their start and end apart: 3, of which 3 were waited for; matrix products, arithmetic and copies ran while one was open for 3% of the time, Pallas kernels for 0%

profile of v13, /device:TPU:0, one launch (start us, length us, event | category | flops | bytes accessed | tf_op | source)
XLA Modules:
  0.0 36.3 jit_solution(7441142892567305137)
XLA Ops:
  0.6 4.3 %shard_map.112 = f32[512,128]{1,0:T(8,128)} custom-call(f32[512,128]{1,0:T(8,128)} %bitcast.67, f32[512,128]{1,0:T(8,128)} %bitcast.68, f32[512,128]{1,0:T(8,128)} %bitcast.69, s32[1,128]{1,0:T(1,128)} %bitcast.79, f32[1,128]{1,0:T(1,128)} %bitcast.80, f32[1]{0:T(128)} %bitcast.7.keep_ref, s32[2]{0:T(128)} %bitcast.81, s32[128]{0:T(128)} %receiver_ref.1), custom_call_target="tpu_custom_call" | custom-call | tf_op jit(solution)/shard_map/pallas_call | solution.py:242
  4.9 0.0 copy-start
  4.9 0.0 copy-start.1
  4.9 7.3 %all-to-all-start = ((f32[32,16,128]{2,1,0:T(8,128)}), f32[32,16,128]{2,1,0:T(8,128)S(1)}, u32[]{:S(2)}, u32[]{:S(2)}) async-start(f32[32,16,128]{2,1,0:T(8,128)} %bitcast.65), calls=%async_computation | async-start | bytes 524288 | tf_op jit(solution)/shard_map/all_to_all | solution.py:292
  12.3 0.0 copy-start.2
  12.3 0.0 copy-done
  12.3 0.0 copy-done.1
  12.3 0.7 %copy-done.2 = f32[32,6,1]{0,1,2:T(8,128)S(1)} copy-done((f32[32,6,1]{0,1,2:T(8,128)S(1)}, f32[32,6,1]{0,1,2:T(8,128)}, u32[]{:S(2)}) %copy-start.2) | copy-done | bytes 792
  12.9 0.4 %fusion = f32[32,16,128]{2,0,1:T(8,128)S(1)} fusion(f32[32,6,1]{0,1,2:T(8,128)S(1)} %copy-done.2, f32[6,2048]{1,0:T(8,128)S(1)} %copy-done.1, f32[6,2048]{1,0:T(8,128)S(1)} %copy-done), kind=kOutput, calls=%fused_computation.7 | convolution fusion | flops 4730880 | bytes 361216 | tf_op jit(solution)/shard_map/pk,krz->prz/dot_general | solution.py:296
  13.5 9.4 %all-to-all-done = f32[32,16,128]{2,1,0:T(8,128)S(1)} async-done(((f32[32,16,128]{2,1,0:T(8,128)}), f32[32,16,128]{2,1,0:T(8,128)S(1)}, u32[]{:S(2)}, u32[]{:S(2)}) %all-to-all-start) | async-done | bytes 262176 | tf_op jit(solution)/shard_map/all_to_all | solution.py:292
  23.3 0.7 %pad_maximum_fusion = f32[4,8,8,128]{3,2,1,0:T(8,128)} fusion(f32[2,8,8,128]{3,2,1,0:T(8,128)S(1)} %bitcast.70), kind=kLoop, calls=%fused_computation.1 | loop fusion | flops 32768 | bytes 196608 | tf_op jit(solution)/shard_map/concatenate | solution.py:313
  23.9 2.6 %all-to-all-start.1 = ((f32[32,8,128]{2,1,0:T(8,128)}), f32[32,8,128]{2,1,0:T(8,128)S(1)}, u32[]{:S(2)}, u32[]{:S(2)}) async-start(f32[32,8,128]{2,1,0:T(8,128)} %bitcast.27), calls=%async_computation.1 | async-start | bytes 262144 | tf_op jit(solution)/shard_map/all_to_all | solution.py:314
  26.5 7.7 %all-to-all-done.1 = f32[32,8,128]{2,1,0:T(8,128)S(1)} async-done(((f32[32,8,128]{2,1,0:T(8,128)}), f32[32,8,128]{2,1,0:T(8,128)S(1)}, u32[]{:S(2)}, u32[]{:S(2)}) %all-to-all-start.1) | async-done | bytes 131104 | tf_op jit(solution)/shard_map/all_to_all | solution.py:314
  34.2 0.1 collective-permute-start
  34.3 0.7 %fusion.3 = (f32[6,2048]{1,0:T(8,128)}, f32[6,2048]{1,0:T(8,128)}) fusion(f32[6,2048]{1,0:T(8,128)S(1)} %copy-done, f32[1,6,16,128]{3,2,1,0:T(8,128)S(1)} %add_bitcast_fusion), kind=kLoop, calls=%fused_computation.37 | loop fusion | flops 49152 | bytes 196608 | tf_op jit(solution)/shard_map/sub | solution.py:325
  35.0 0.6 %collective-permute-done = f32[32,8,128]{2,1,0:T(8,128)S(1)} collective-permute-done((f32[32,8,128]{2,1,0:T(8,128)S(1)}, f32[32,8,128]{2,1,0:T(8,128)S(1)}, u32[]{:S(2)}, u32[]{:S(2)}) %collective-permute-start) | collective-permute-done | bytes 131104 | tf_op jit(solution)/shard_map/ppermute | solution.py:315
  35.6 0.7 %maximum_select_fusion = f32[32,16,128]{2,1,0:T(8,128)} fusion(f32[32,8,128]{2,1,0:T(8,128)S(1)} %collective-permute-done, f32[32,8,128]{2,1,0:T(8,128)S(1)} %all-to-all-done.1, pred[]{:T(512)S(6)} %eq.8), kind=kLoop, calls=%fused_computation | loop fusion | flops 196608 | bytes 524289 | tf_op jit(solution)/shard_map/jit(_where)/select_n | solution.py:316
  (27 shorter events, 0.2 us)
Async XLA Ops:
  4.9 7.3 %copy-start = (f32[6,2048]{1,0:T(8,128)S(1)}, f32[6,2048]{1,0:T(8,128)}, u32[]{:S(2)}) copy-start(f32[6,2048]{1,0:T(8,128)} %param.16) | copy-start | bytes 147460
  4.9 7.3 %copy-start.1 = (f32[6,2048]{1,0:T(8,128)S(1)}, f32[6,2048]{1,0:T(8,128)}, u32[]{:S(2)}) copy-start(f32[6,2048]{1,0:T(8,128)} %param.15) | copy-start | bytes 147460
  4.9 18.0 %all-to-all-start = ((f32[32,16,128]{2,1,0:T(8,128)}), f32[32,16,128]{2,1,0:T(8,128)S(1)}, u32[]{:S(2)}, u32[]{:S(2)}) async-start(f32[32,16,128]{2,1,0:T(8,128)} %bitcast.65), calls=%async_computation | async-start | bytes 524288 | tf_op jit(solution)/shard_map/all_to_all | solution.py:292
  12.3 0.7 %copy-start.2 = (f32[32,6,1]{0,1,2:T(8,128)S(1)}, f32[32,6,1]{0,1,2:T(8,128)}, u32[]{:S(2)}) copy-start(f32[32,6,1]{0,1,2:T(8,128)} %constant.77) | copy-start | bytes 2308
  23.9 10.3 %all-to-all-start.1 = ((f32[32,8,128]{2,1,0:T(8,128)}), f32[32,8,128]{2,1,0:T(8,128)S(1)}, u32[]{:S(2)}, u32[]{:S(2)}) async-start(f32[32,8,128]{2,1,0:T(8,128)} %bitcast.27), calls=%async_computation.1 | async-start | bytes 262144 | tf_op jit(solution)/shard_map/all_to_all | solution.py:314
  34.2 1.3 %collective-permute-start = (f32[32,8,128]{2,1,0:T(8,128)S(1)}, f32[32,8,128]{2,1,0:T(8,128)S(1)}, u32[]{:S(2)}, u32[]{:S(2)}) collective-permute-start(f32[32,8,128]{2,1,0:T(8,128)S(1)} %all-to-all-done.1), channel_id=1, source_target_pairs={{0,8},{8,0},{16,24},{24,16},{1,9},{9,1},{17,25},{25,17},{2,10},{10... | collective-permute-start | bytes 393224 | tf_op jit(solution)/shard_map/ppermute | solution.py:315
